TPU v7x, 256 devices: a whole 4x4x8 slice. The times are simulated.
256 devices in a mesh: grp: 32 (over z, y_hi, core), tp: 8 (over y_lo, x).
Axes of the slice: x: 4, y: 4 (y_hi: 2, y_lo: 2; y = y_hi * 2 + y_lo), z: 8, core: 2. Of those that a mesh axis runs over, the one named last changes fastest.
Arguments:
- states_in: bfloat16 [16384, 1536], P('grp', 'tp'), may hold values from -6 to 6
- segment_ids: int32 [16384], P('grp'), may hold values from 0 to 223, as said below
- positions: int32 [16384], P('grp'), may hold values from 0 to 1009, as said below
- attention_gain: bfloat16 [1536], P('tp'), may hold values from 0.5 to 1.5
- feedforward_gain: bfloat16 [1536], P('tp'), may hold values from 0.5 to 1.5
- query_weight: bfloat16 [1536, 1536], P('grp', 'tp'), may hold values from -1 to 1
- keyvalue_weight: bfloat16 [1536, 8, 128], P('grp', 'tp'), may hold values from -128 to 128
- output_weight: bfloat16 [1536, 1536], P('tp'), may hold values from -0.15625 to 0.15625
- route_experts: int32 [16384, 8], P('grp'), may hold values from 0 to 19, all different within a row; in each aligned block of 512 rows (0 to 511, 512 to 1023, ...) at most 256 rows name the same one
- route_weights: float32 [16384, 8], P('grp'), may hold values from 0.05 to 0.3
- expert_gateup: bfloat16 [40, 1536, 512], P('tp'), may hold values from -0.15625 to 0.15625
- expert_down: bfloat16 [40, 256, 1536], P('tp'), may hold values from -0.25 to 0.25
- cache_slots: int32 [16384], P('grp'), may hold values from 0 to 16383, as said below
Outputs:
- layer_output: bfloat16 [16384, 1536], P('grp', 'tp')
- paged_cache: bfloat16 [16384, 8, 128], P('grp', 'tp')
- log_sums: float32 [24, 16384], P('tp', 'grp')
Inputs may be any that keep to these rules, and one draw needn't show every extreme that they name: `segment_ids`: equal ids mark the tokens of one prompt; the tokens of a prompt lie within one pair of groups 2p and 2p+1. `positions`: positions count from 0 within each prompt; one prompt of groups 0 and 1 has 2 * (505) tokens. `route_experts`: each row names 8 different experts; at most 256 rows of one group name the same expert, and that number is reached. `cache_slots`: every cache row is named once; the tokens of each group fill exactly 16 rows of every group's block of 512 rows.
All inputs are finite; a program needn't handle non-finite values.
Results may differ from a plain program's by a relative error of at most 0.01.
The roundings to bfloat16 on the way count: a program that leaves them out, or rounds other values in their place, can miss the bound.
Values may be sent and summed in bfloat16 or wider, within the bound.
No kernel may reach another device: no remote copies, remote signals or barrier semaphores. Data moves between devices by JAX's collectives and lax.ppermute only.
A program may use at most 128 MiB of HBM per device.

v0:
```python
import jax
import jax.numpy as jnp
from jax import lax
from jax.sharding import PartitionSpec as P

HD = 64
CAP = 256


attn_scale = 0.015625
norm_eps = 1e-06
rope_base = 10000.0


def from_partner(value, axis, apart):
    mask = 2**apart
    pairs = [(source, source ^ mask) for source in range(lax.axis_size(axis))]
    return lax.ppermute(value, axis, pairs)


def rms_scale(values, gain_row):
    floats = values.astype(jnp.float32)
    mean_square = jnp.mean(floats * floats, axis=-1, keepdims=True)
    return (floats * lax.rsqrt(mean_square + norm_eps) * gain_row.astype(jnp.float32)).astype(
        jnp.bfloat16
    )


def rotate(values, places):
    half_width = values.shape[-1] // 2
    frequency = rope_base ** (-jnp.arange(half_width, dtype=jnp.float32) * 2.0 / values.shape[-1])
    angles = places.astype(jnp.float32)[:, None] * frequency[None, :]
    cosine = jnp.cos(angles)[:, None, :]
    sine_part = jnp.sin(angles)[:, None, :]
    leading = values[..., :half_width]
    trailing = values[..., half_width:]
    return jnp.concatenate(
        [leading * cosine - trailing * sine_part, trailing * cosine + leading * sine_part], axis=-1
    )


def attend_block(query_block, seg_block, pos_block, all_rows, all_seg, all_pos):
    key_part = all_rows[..., :HD]
    value_part = all_rows[..., HD:]
    scores = (
        jnp.einsum("qgrd,kgd->grqk", query_block, key_part, preferred_element_type=jnp.float32)
        * attn_scale
    )
    allowed = (seg_block[:, None] == all_seg[None, :]) & (all_pos[None, :] <= pos_block[:, None])
    masked = jnp.where(allowed, scores, -jnp.inf)
    row_peak = jnp.max(masked, axis=-1, keepdims=True)
    exponent = jnp.exp(masked - row_peak)
    row_total = jnp.sum(exponent, axis=-1, keepdims=True)
    log_total = (row_peak + jnp.log(row_total))[..., 0]
    weights_low = (exponent / row_total).astype(jnp.bfloat16)
    mixed_rows = jnp.einsum(
        "grqk,kgd->qgrd", weights_low, value_part, preferred_element_type=jnp.float32
    )
    return (mixed_rows.astype(jnp.bfloat16), log_total)


def expert_terms(normed, route_experts, route_weights, gateup, down, slot_first):
    tokens = normed.shape[0]
    width = normed.shape[1]
    local_experts = gateup.shape[0]
    half_units = down.shape[1]
    owned_experts = slot_first + jnp.arange(local_experts, dtype=jnp.int32)
    matches = route_experts[:, :, None] == owned_experts[None, None, :]
    chosen = jnp.any(matches, axis=1)
    route_scale = jnp.sum(jnp.where(matches, route_weights[:, :, None], 0.0), axis=1)
    offsets = jnp.arange(tokens, dtype=jnp.int32)[:, None]
    ranking = jnp.argsort(jnp.where(chosen, offsets, tokens + offsets), axis=0)[:CAP].T
    picked = normed[ranking]
    gate_up = jnp.einsum("ecd,edf->ecf", picked, gateup, preferred_element_type=jnp.float32)
    activated = (jax.nn.silu(gate_up[..., :half_units]) * gate_up[..., half_units:]).astype(
        jnp.bfloat16
    )
    produced = jnp.einsum("ecf,efd->ecd", activated, down, preferred_element_type=jnp.float32)
    scales = jnp.take_along_axis(route_scale.T, ranking, axis=1)
    contribution = (scales[..., None] * produced).reshape(-1, width)
    return jnp.zeros((tokens, width), jnp.float32).at[ranking.reshape(-1)].add(contribution)


def shards(
    states_in,
    segment_ids,
    positions,
    attention_gain,
    feedforward_gain,
    query_weight,
    keyvalue_weight,
    output_weight,
    route_experts,
    route_weights,
    expert_gateup,
    expert_down,
    cache_slots,
):
    tokens = states_in.shape[0]
    width_share = states_in.shape[1]
    head_rank = lax.axis_index("tp")
    group_rank = lax.axis_index("grp")
    states_full, gain_attend, gain_forward = (
        lax.all_gather(states_in, "tp", axis=1, tiled=True),
        lax.all_gather(attention_gain, "tp", axis=0, tiled=True),
        lax.all_gather(feedforward_gain, "tp", axis=0, tiled=True),
    )
    normed_in = rms_scale(states_full, gain_attend)
    query_cols = query_weight.shape[1]
    keyvalue_heads = keyvalue_weight.shape[1]
    heads_local = query_cols // HD
    pieces = (
        lax.all_gather(query_weight, "grp", axis=0, tiled=True),
        lax.all_gather(keyvalue_weight, "grp", axis=0, tiled=True),
    )
    piece_rows = pieces[0].shape[0]
    query_sum = jnp.dot(normed_in, pieces[0], preferred_element_type=jnp.float32)
    keyvalue_sum = jnp.dot(
        normed_in, pieces[1].reshape(piece_rows, -1), preferred_element_type=jnp.float32
    )
    query_sum, keyvalue_sum = (query_sum, keyvalue_sum)
    queries = rotate(query_sum.reshape(tokens, heads_local, HD), positions).astype(jnp.bfloat16)
    keyvalue_sum = keyvalue_sum.reshape(tokens, keyvalue_heads, 2 * HD)
    key_rows = rotate(keyvalue_sum[..., :HD], positions).astype(jnp.bfloat16)
    value_rows = keyvalue_sum[..., HD:].astype(jnp.bfloat16)
    own_rows = jnp.concatenate([key_rows, value_rows], axis=-1)
    other_rows, other_seg, other_pos = from_partner((own_rows, segment_ids, positions), "grp", 0)
    all_rows = jnp.concatenate([own_rows, other_rows], axis=0)
    all_seg = jnp.concatenate([segment_ids, other_seg], axis=0)
    all_pos = jnp.concatenate([positions, other_pos], axis=0)
    block_rows = min(tokens, 512)
    block_count = tokens // block_rows
    group_ratio = heads_local // keyvalue_heads
    query_blocks = queries.reshape(block_count, block_rows, keyvalue_heads, group_ratio, HD)

    def one_block(items):
        return attend_block(items[0], items[1], items[2], all_rows, all_seg, all_pos)

    mixed_all, log_all = lax.map(
        one_block,
        (
            query_blocks,
            segment_ids.reshape(block_count, block_rows),
            positions.reshape(block_count, block_rows),
        ),
    )
    attended = mixed_all.reshape(tokens, heads_local * HD)
    log_sums = jnp.transpose(
        log_all.reshape(block_count, heads_local, block_rows), (1, 0, 2)
    ).reshape(heads_local, tokens)
    partial_value = jnp.dot(attended, output_weight, preferred_element_type=jnp.float32)
    summed = lax.psum(partial_value, "tp")
    residual = (states_full.astype(jnp.float32) + summed).astype(jnp.bfloat16)
    normed = rms_scale(residual, gain_forward)
    residual_share = lax.dynamic_slice_in_dim(residual, head_rank * width_share, width_share, 1)
    slot_first = head_rank // 2 * expert_gateup.shape[0]
    terms = expert_terms(
        normed, route_experts, route_weights, expert_gateup, expert_down, slot_first
    )
    expert_share = lax.psum_scatter(
        terms.astype(jnp.bfloat16), "tp", scatter_dimension=1, tiled=True
    ).astype(jnp.float32)
    layer_output = (residual_share.astype(jnp.float32) + expert_share).astype(jnp.bfloat16)
    group_count = lax.axis_size("grp")
    per_owner = tokens // group_count
    owners = cache_slots // tokens
    sequence = jnp.arange(tokens, dtype=jnp.int32)
    ordering = jnp.argsort(owners * tokens + sequence)
    send_rows = own_rows[ordering].reshape(group_count, per_owner, keyvalue_heads, 2 * HD)
    send_slots = cache_slots[ordering].reshape(group_count, per_owner)
    got_rows, got_slots = (
        lax.all_to_all(send_rows, "grp", split_axis=0, concat_axis=0, tiled=True),
        lax.all_to_all(send_slots, "grp", split_axis=0, concat_axis=0, tiled=True),
    )
    targets = got_slots.reshape(tokens) - group_rank * tokens
    paged_rows = (
        jnp.zeros_like(own_rows).at[targets].set(got_rows.reshape(tokens, keyvalue_heads, 2 * HD))
    )
    return (layer_output, paged_rows, log_sums)


def solution(mesh):
    return jax.shard_map(
        shards,
        mesh=mesh,
        in_specs=(
            P("grp", "tp"),
            P("grp"),
            P("grp"),
            P("tp"),
            P("tp"),
            P("grp", "tp"),
            P("grp", "tp", None),
            P("tp", None),
            P("grp", None),
            P("grp", None),
            P("tp", None, None),
            P("tp", None, None),
            P("grp"),
        ),
        out_specs=(P("grp", "tp"), P("grp", "tp", None), P("tp", "grp")),
        check_vma=False,
    )
```

profile of v0, /device:TPU:32, one launch (start us, length us, event | category | flops | bytes accessed | tf_op | source)
XLA Modules:
  0.0 328.9 jit_solution(2951565056632396982)
XLA Ops:
  7.2 0.0 copy-start
  7.2 0.0 all-gather.2.cloned.1.call-start
  7.2 0.7 all-gather.2.cloned.1.call-update
  7.9 0.0 all-reduce.5.cloned.1.call-start
  8.0 0.1 collective-permute-start.1
  8.1 0.5 collective-permute-start.2
  8.6 0.7 convert_element_type.71
  9.2 1.3 dynamic-slice.2
  11.2 0.9 dynamic-update-slice
  12.0 0.8 dynamic-update-slice.1
  12.9 46.9 %all_gather.17 = bf16[1536,1,128]{2,0,1:T(8,128)(2,1)} all-gather(bf16[48,1,128]{2,0,1:T(8,128)(2,1)} %param.19), channel_id=1, replica_groups=mesh['grp'=32,'tp'=8] {'grp'}, dimensions={0}, use_global_device_ids=true | all-gather | bytes 405504 | tf_op jit(solution)/shard_map/all_gather | solution.py:114
  59.8 0.9 multiply_cosine_fusion
  60.7 39.2 %all_gather.18 = bf16[1536,192]{1,0:T(8,128)(2,1)S(1)} all-gather(bf16[48,192]{1,0:T(8,128)(2,1)} %param.18), channel_id=1, replica_groups=mesh['grp'=32,'tp'=8] {'grp'}, dimensions={0}, use_global_device_ids=true | all-gather | bytes 608256 | tf_op jit(solution)/shard_map/all_gather | solution.py:113
  99.9 19.2 %all-reduce.2 = (bf16[1536]{0:T(1024)(128)(2,1)S(1)}, bf16[1536]{0:T(1024)(128)(2,1)S(1)}) all-reduce(bf16[1536]{0:T(1024)(128)(2,1)S(1)} %dynamic-update-slice, bf16[1536]{0:T(1024)(128)(2,1)S(1)} %dynamic-update-slice.1), channel_id=1, replica_groups=mesh['grp'=32,'tp'=8] {'tp'}, use_global_device_ids=true, to_apply=%add | all-reduce | flops 3072 | bytes 12288
  119.2 0.7 pad_add_fusion
  119.9 0.7 pad_add_fusion.1
  120.5 1.5 compare_and_fusion
  122.1 0.0 all-gather.2.cloned.1.call-done
  122.1 1.7 copy.36
  123.8 0.4 fusion.5
  124.2 1.8 convolution_bitcast_fusion
  126.0 1.0 fusion.33
  127.0 0.7 fusion.47
  127.7 0.8 fusion.19
  128.5 0.1 subtract_convert_fusion
  128.5 0.5 collective-permute-done
  129.0 1.4 fusion.1
  130.4 1.4 fusion
  131.8 2.0 fusion.14
  133.9 0.0 copy-start.6
  133.9 2.3 fusion.49
  136.2 0.0 all-reduce.5.cloned.1.call-update
  136.2 0.2 reduce-scatter.4.cloned.1.call-start
  136.5 0.1 compare_reduce_fusion
  136.6 3.9 %sort.34 = (s32[512,5]{0,1:T(8,128)}, s32[512,5]{0,1:T(8,128)S(1)}) sort(s32[512,5]{0,1:T(8,128)S(1)} %iota_select_fusion, s32[512,5]{0,1:T(8,128)S(1)} %iota.37), dimensions={0}, to_apply=%region_5.6 | sort | flops 30720 | bytes 40960 | tf_op jit(solution)/shard_map/jit(argsort)/sort | solution.py:72
  140.6 0.1 fusion.31
  140.7 0.1 copy.38
  140.9 8.5 %gather_fusion.3 = f32[1280]{0:T(1024)S(1)} fusion(f32[5,512]{0,1:T(8,128)S(1)} %bitcast.78, s32[1280]{0:T(1024)S(1)} %reshape.346), kind=kCustom, calls=%fused_computation.3 | custom fusion | bytes 20480 | tf_op jit(solution)/shard_map/jit(take_along_axis)/gather | solution.py:79
  149.5 80.8 %all-reduce.5.cloned.1.call-done = f32[512,1536]{1,0:T(8,128)} async-done(((f32[512,1536]{1,0:T(8,128)}), f32[512,1536]{1,0:T(8,128)}) %all-reduce.5.cloned.1.call-update) | async-done | bytes 3145744 | tf_op jit(solution)/shard_map/psum | solution.py:152
  230.3 2.4 fusion.2
  232.7 1.1 copy-done.3
  233.8 0.4 fusion.4
  234.2 5.4 %gather_fusion = bf16[1280,1536]{1,0:T(8,128)(2,1)} fusion(bf16[512,1536]{1,0:T(8,128)(2,1)S(1)} %fusion.4, s32[2048]{0:T(1024)S(1)} %pad_clamp_fusion), kind=kCustom, calls=%fused_computation | custom fusion | bytes 7869440 | tf_op jit(solution)/shard_map/gather | solution.py:73
  239.7 6.7 %fusion.50 = f32[5,256,512]{2,1,0:T(8,128)S(1)} fusion(bf16[5,256,1536]{2,1,0:T(8,128)(2,1)} %bitcast.80, bf16[5,1536,512]{2,1,0:T(8,128)(2,1)} %param.23), kind=kOutput, calls=%fused_computation.100 | convolution fusion | flops 2013265920 | bytes 14417920 | tf_op jit(solution)/shard_map/ecd,edf->ecf/dot_general | solution.py:74
  246.4 4.4 %convolution_multiply_fusion = f32[5,256,1536]{2,1,0:T(8,128)} fusion(bf16[5,256,1536]{2,1,0:T(8,128)(2,1)S(1)} %copy-done.2, f32[5,256]{1,0:T(8,128)S(1)} %and_select_fusion, f32[5,256,512]{2,1,0:T(8,128)S(1)} %fusion.50), kind=kOutput, calls=%fused_computation.10 | convolution fusion | flops 1010565120 | bytes 14423040 | tf_op jit(solution)/shard_map/ecf,efd->ecd/dot_general | solution.py:78
  250.8 18.5 %scatter_custom_fusion = f32[512,1536]{1,0:T(8,128)} fusion(s32[1280]{0:T(1024)S(1)} %fusion.38, f32[1280,1536]{1,0:T(8,128)} %bitcast.79, f32[]{:T(128)} %constant.52.clone.1), kind=kCustom, calls=%fused_computation.27 | custom fusion | flops 1966080 | bytes 3146240 | tf_op jit(solution)/shard_map/scatter-add | solution.py:81
  269.3 2.1 convert_element_type.82
  271.4 1.6 copy.44
  273.0 0.0 reduce-scatter.4.cloned.1.call-update
  273.0 3.8 %sort.35 = (s32[512]{0:T(512)}, s32[512]{0:T(512)S(1)}) sort(s32[512]{0:T(512)S(1)} %fusion.41, s32[512]{0:T(512)S(1)} %iota.39), dimensions={0}, to_apply=%region_10.11 | sort | flops 4608 | bytes 8192 | tf_op jit(solution)/shard_map/jit(argsort)/sort | solution.py:168
  276.8 3.5 %gather_fusion.1 = s32[512]{0:T(512)S(1)} fusion(s32[512]{0:T(512)S(1)} %copy-done.1, s32[1024]{0:T(1024)S(1)} %pad_clamp_fusion.1), kind=kCustom, calls=%fused_computation.1 | custom fusion | bytes 6144 | tf_op jit(solution)/shard_map/gather | solution.py:170
  280.3 0.7 all_to_all.9
  281.0 9.8 %all-to-all-start = ((s32[32,1,16]{2,1,0:T(1,128)}), s32[32,1,16]{2,1,0:T(1,128)S(1)}, u32[]{:S(2)}, u32[]{:S(2)}) async-start(s32[32,1,16]{2,1,0:T(1,128)} %bitcast.19), calls=%async_computation | async-start | bytes 32768 | tf_op jit(solution)/shard_map/all_to_all | solution.py:173
  290.8 8.5 %all-to-all-done = s32[32,1,16]{2,1,0:T(1,128)S(1)} async-done(((s32[32,1,16]{2,1,0:T(1,128)}), s32[32,1,16]{2,1,0:T(1,128)S(1)}, u32[]{:S(2)}, u32[]{:S(2)}) %all-to-all-start) | async-done | bytes 2080 | tf_op jit(solution)/shard_map/all_to_all | solution.py:173
  299.4 0.1 sub.52
  299.5 0.1 copy.40
  299.6 1.9 gather_fusion.2
  301.5 4.9 %all-to-all-start.1 = ((bf16[32,16,1,128]{3,1,2,0:T(8,128)(2,1)}), bf16[32,16,1,128]{3,1,2,0:T(8,128)(2,1)S(1)}, u32[]{:S(2)}, u32[]{:S(2)}) async-start(bf16[32,16,1,128]{3,1,2,0:T(8,128)(2,1)} %bitcast.23), calls=%async_computation.1 | async-start | bytes 262144 | tf_op jit(solution)/shard_map/all_to_all | solution.py:172
  306.5 0.6 log_add_fusion
  307.1 9.9 %all-to-all-done.1 = bf16[32,16,1,128]{3,1,2,0:T(8,128)(2,1)S(1)} async-done(((bf16[32,16,1,128]{3,1,2,0:T(8,128)(2,1)}), bf16[32,16,1,128]{3,1,2,0:T(8,128)(2,1)S(1)}, u32[]{:S(2)}, u32[]{:S(2)}) %all-to-all-start.1) | async-done | bytes 131104 | tf_op jit(solution)/shard_map/all_to_all | solution.py:172
  317.0 2.4 scatter_custom_fusion.1
  319.4 1.1 copy.45
  320.4 1.2 add_convert_fusion
  321.6 0.8 copy.42
  (48 shorter events, 0.3 us)
Async XLA Ops:
  7.2 126.7 %copy-start = (bf16[192,1536]{1,0:T(8,128)(2,1)S(1)}, bf16[192,1536]{1,0:T(8,128)(2,1)}, u32[]{:S(2)}) copy-start(bf16[192,1536]{1,0:T(8,128)(2,1)} %param.20) | copy-start | bytes 1769476
  7.2 114.9 %all-gather.2.cloned.1.call-start = ((), (), s32[]{:S(2)}) async-start(), calls=%async_computation.3 | async-start | bytes 1769472 | tf_op jit(solution)/shard_map/all_gather | solution.py:104
  7.9 222.3 %all-reduce.5.cloned.1.call-start = ((), (), s32[]{:S(2)}) async-start(), calls=%async_computation.4 | async-start | bytes 6291456 | tf_op jit(solution)/shard_map/psum | solution.py:152
  8.0 111.2 %collective-permute-start.1 = (s32[512]{0:T(512)}, s32[512]{0:T(512)S(1)}, u32[]{:S(2)}, u32[]{:S(2)}) collective-permute-start(s32[512]{0:T(512)} %param.14), channel_id=1, source_target_pairs={{0,8},{8,0},{16,24},{24,16},{32,40},{40,32},{48,56},{56,48},{64,72... | collective-permute-start | bytes 6152 | tf_op jit(solution)/shard_map/ppermute | solution.py:18
  8.1 111.8 %collective-permute-start.2 = (s32[512]{0:T(512)}, s32[512]{0:T(512)S(1)}, u32[]{:S(2)}, u32[]{:S(2)}) collective-permute-start(s32[512]{0:T(512)} %param.15), channel_id=1, source_target_pairs={{0,8},{8,0},{16,24},{24,16},{32,40},{40,32},{48,56},{56,48},{64,72... | collective-permute-start | bytes 6152 | tf_op jit(solution)/shard_map/ppermute | solution.py:18
  12.9 47.8 %copy-start.8 = (f32[32]{0:T(128)}, f32[32]{0:T(128)S(1)}, u32[]{:S(2)}) copy-start(f32[32]{0:T(128)S(1)} %multiply_power_fusion) | copy-start | bytes 388
  124.2 4.2 %copy-start.5 = (f32[512,32]{0,1:T(8,128)S(1)}, f32[512,32]{0,1:T(8,128)}, u32[]{:S(2)}) copy-start(f32[512,32]{0,1:T(8,128)} %get-tuple-element.57) | copy-start | bytes 196612
  127.7 1.3 collective-permute-start
  133.9 2.6 copy-start.6
  133.9 6.8 %copy-start.7 = (f32[512,8]{0,1:T(8,128)S(1)}, f32[512,8]{0,1:T(8,128)}, u32[]{:S(2)}) copy-start(f32[512,8]{0,1:T(8,128)} %param.22) | copy-start | bytes 49156
  136.2 183.1 %reduce-scatter.4.cloned.1.call-start = ((), (), s32[]{:S(2)}) async-start(), calls=%async_computation.5 | async-start | bytes 1769472
  232.7 1.1 copy-start.3
  239.7 6.8 %copy-start.2 = (bf16[5,256,1536]{2,1,0:T(8,128)(2,1)S(1)}, bf16[5,256,1536]{2,1,0:T(8,128)(2,1)}, u32[]{:S(2)}) copy-start(bf16[5,256,1536]{2,1,0:T(8,128)(2,1)} %param.24) | copy-start | bytes 11796484
  271.4 1.7 copy-start.1
  271.4 28.1 %copy-start.4 = (bf16[512,128]{0,1:T(8,128)(2,1)S(1)}, bf16[512,128]{0,1:T(8,128)(2,1)}, u32[]{:S(2)}) copy-start(bf16[512,128]{0,1:T(8,128)(2,1)} %get-tuple-element.54) | copy-start | bytes 393220
  281.0 18.3 %all-to-all-start = ((s32[32,1,16]{2,1,0:T(1,128)}), s32[32,1,16]{2,1,0:T(1,128)S(1)}, u32[]{:S(2)}, u32[]{:S(2)}) async-start(s32[32,1,16]{2,1,0:T(1,128)} %bitcast.19), calls=%async_computation | async-start | bytes 32768 | tf_op jit(solution)/shard_map/all_to_all | solution.py:173
  301.5 15.5 %all-to-all-start.1 = ((bf16[32,16,1,128]{3,1,2,0:T(8,128)(2,1)}), bf16[32,16,1,128]{3,1,2,0:T(8,128)(2,1)S(1)}, u32[]{:S(2)}, u32[]{:S(2)}) async-start(bf16[32,16,1,128]{3,1,2,0:T(8,128)(2,1)} %bitcast.23), calls=%async_computation.1 | async-start | bytes 262144 | tf_op jit(solution)/shard_map/all_to_all | solution.py:172
Sparse Core Ops, SparseCore 0:
  9.8 45.6 all-gather.1
  136.3 93.8 all-reduce.4
  273.1 43.5 reduce-scatter.3
where the time goes:
time: 331 us; the launch traced here: 329 us
  blocking collectives  105 us (32%)
  waiting for transfers between devices  100 us (30%)
  other arithmetic  41.2 us (12%)
  local copies, waits for them, and re-layouts  32.1 us (10%)
  matrix products  19.4 us (6%)
  starting transfers between devices  15.6 us (5%)
  between operations  14.9 us (5%)
    psum x1, waiting for transfers between devices, shards(): summed = lax.psum(partial_value, 'tp')  80.8 us
    all_gather x1, blocking collectives, shards(): lax.all_gather(keyvalue_weight, 'grp', axis=0, tiled=True)  46.9 us
    all_gather x1, blocking collectives, shards(): lax.all_gather(query_weight, 'grp', axis=0, tiled=True)  39.2 us
    unnamed x1, blocking collectives  19.2 us
    scatter-add x1, other arithmetic, expert_terms(): jnp.zeros((tokens, width), jnp.float32).at[ranking.reshape(-1)]  18.5 us
    all_to_all x1, waiting for transfers between devices, shards(): lax.all_to_all(send_rows, 'grp', split_axis=0, concat_axis=0, tiled=True)  9.94 us
    all_to_all x1, starting transfers between devices, shards(): lax.all_to_all(send_slots, 'grp', split_axis=0, concat_axis=0, tiled=True)  9.78 us
    gather x3, local copies, waits for them, and re-layouts, expert_terms(): scales = jnp.take_along_axis(route_scale.T, ranking, axis=1)  8.52 us
  transfers between devices with their start and end apart: 8, of which 4 were waited for; matrix products, arithmetic and copies ran while one was open for 10% of the time, Pallas kernels for 0%

commit v1 on v0

v1 whole, which is shorter than its diff:
```python
import jax
import jax.numpy as jnp
from jax import lax
from jax.sharding import Mesh
from jax.sharding import PartitionSpec as P

HD = 64

attn_scale = 0.015625
norm_eps = 1e-06
rope_base = 10000.0

G = ("z", "yh", "c")
T = ("yl", "x")


def rms_scale(values, gain_row):
    floats = values.astype(jnp.float32)
    mean_square = jnp.mean(floats * floats, axis=-1, keepdims=True)
    return (floats * lax.rsqrt(mean_square + norm_eps) * gain_row.astype(jnp.float32)).astype(
        jnp.bfloat16
    )


def rotate(values, places):
    half_width = values.shape[-1] // 2
    frequency = rope_base ** (-jnp.arange(half_width, dtype=jnp.float32) * 2.0 / values.shape[-1])
    angles = places.astype(jnp.float32)[:, None] * frequency[None, :]
    cosine = jnp.cos(angles)[:, None, :]
    sine_part = jnp.sin(angles)[:, None, :]
    leading = values[..., :half_width]
    trailing = values[..., half_width:]
    return jnp.concatenate(
        [leading * cosine - trailing * sine_part, trailing * cosine + leading * sine_part], axis=-1
    )


def attend_block(query_block, seg_block, pos_block, all_rows, all_seg, all_pos):
    key_part = all_rows[..., :HD]
    value_part = all_rows[..., HD:]
    scores = (
        jnp.einsum("qgrd,kgd->grqk", query_block, key_part, preferred_element_type=jnp.float32)
        * attn_scale
    )
    allowed = (seg_block[:, None] == all_seg[None, :]) & (all_pos[None, :] <= pos_block[:, None])
    masked = jnp.where(allowed, scores, -jnp.inf)
    row_peak = jnp.max(masked, axis=-1, keepdims=True)
    exponent = jnp.exp(masked - row_peak)
    row_total = jnp.sum(exponent, axis=-1, keepdims=True)
    log_total = (row_peak + jnp.log(row_total))[..., 0]
    weights_low = (exponent / row_total).astype(jnp.bfloat16)
    mixed_rows = jnp.einsum(
        "grqk,kgd->qgrd", weights_low, value_part, preferred_element_type=jnp.float32
    )
    return (mixed_rows.astype(jnp.bfloat16), log_total)


def expert_terms(normed, route_experts, route_weights, gateup, down, slot_first):
    local_experts = gateup.shape[0]
    half_units = down.shape[1]
    owned_experts = slot_first + jnp.arange(local_experts, dtype=jnp.int32)
    matches = route_experts[:, :, None] == owned_experts[None, None, :]
    route_scale = jnp.sum(jnp.where(matches, route_weights[:, :, None], 0.0), axis=1)
    gate_up = jnp.einsum("td,edf->etf", normed, gateup, preferred_element_type=jnp.float32)
    activated = (jax.nn.silu(gate_up[..., :half_units]) * gate_up[..., half_units:]).astype(
        jnp.bfloat16
    )
    produced = jnp.einsum("etf,efd->etd", activated, down, preferred_element_type=jnp.float32)
    return jnp.sum(route_scale.T[:, :, None] * produced, axis=0)


def gather_rows_over_groups(block):
    width = block.shape[1]
    nz = lax.axis_size("z")
    zi = lax.axis_index("z")
    got = [block]
    for k in range(1, nz):
        got.append(lax.ppermute(block, "z", [(i, (i + k) % nz) for i in range(nz)]))
    stacked = jnp.stack(got)
    zfull = jnp.take(stacked, (zi - jnp.arange(nz)) % nz, axis=0)
    yi = lax.axis_index("yh")
    other_y = lax.ppermute(zfull, "yh", [(0, 1), (1, 0)])
    yfull = jnp.where(yi == 0, jnp.stack([zfull, other_y]), jnp.stack([other_y, zfull]))
    ci = lax.axis_index("c")
    other_c = lax.ppermute(yfull, "c", [(0, 1), (1, 0)])
    cfull = jnp.where(ci == 0, jnp.stack([yfull, other_c]), jnp.stack([other_c, yfull]))
    return cfull.transpose(2, 1, 0, 3, 4).reshape(-1, width)


def shards(
    states_in,
    segment_ids,
    positions,
    attention_gain,
    feedforward_gain,
    query_weight,
    keyvalue_weight,
    output_weight,
    route_experts,
    route_weights,
    expert_gateup,
    expert_down,
    cache_slots,
):
    tokens = states_in.shape[0]
    width_share = states_in.shape[1]
    head_rank = lax.axis_index(T)
    group_rank = lax.axis_index(G)
    gain_rows = jnp.zeros((8, width_share), states_in.dtype)
    gain_rows = gain_rows.at[0].set(attention_gain).at[1].set(feedforward_gain)
    packed = jnp.concatenate([states_in, gain_rows], axis=0)
    packed_full = lax.all_gather(packed, T, axis=1, tiled=True)
    states_full = packed_full[:tokens]
    gain_attend = packed_full[tokens]
    gain_forward = packed_full[tokens + 1]
    normed_in = rms_scale(states_full, gain_attend)
    query_cols = query_weight.shape[1]
    keyvalue_heads = keyvalue_weight.shape[1]
    heads_local = query_cols // HD
    piece_rows = query_weight.shape[0]
    weights_packed = jnp.concatenate(
        [query_weight, keyvalue_weight.reshape(piece_rows, -1)], axis=1
    )
    weights_full = gather_rows_over_groups(weights_packed)
    query_full_w = weights_full[:, :query_cols]
    keyvalue_full_w = weights_full[:, query_cols:]
    query_sum = jnp.dot(normed_in, query_full_w, preferred_element_type=jnp.float32)
    keyvalue_sum = jnp.dot(normed_in, keyvalue_full_w, preferred_element_type=jnp.float32)
    queries = rotate(query_sum.reshape(tokens, heads_local, HD), positions).astype(jnp.bfloat16)
    keyvalue_sum = keyvalue_sum.reshape(tokens, keyvalue_heads, 2 * HD)
    key_rows = rotate(keyvalue_sum[..., :HD], positions).astype(jnp.bfloat16)
    value_rows = keyvalue_sum[..., HD:].astype(jnp.bfloat16)
    own_rows = jnp.concatenate([key_rows, value_rows], axis=-1)
    other_rows, other_seg, other_pos = lax.ppermute(
        (own_rows, segment_ids, positions), "c", [(0, 1), (1, 0)]
    )
    all_rows = jnp.concatenate([own_rows, other_rows], axis=0)
    all_seg = jnp.concatenate([segment_ids, other_seg], axis=0)
    all_pos = jnp.concatenate([positions, other_pos], axis=0)
    group_ratio = heads_local // keyvalue_heads
    query_block = queries.reshape(tokens, keyvalue_heads, group_ratio, HD)
    mixed, log_part = attend_block(query_block, segment_ids, positions, all_rows, all_seg, all_pos)
    attended = mixed.reshape(tokens, heads_local * HD)
    log_sums = log_part.reshape(heads_local, tokens)
    partial_value = jnp.dot(attended, output_weight, preferred_element_type=jnp.float32)
    summed = lax.psum(partial_value, T)
    residual = (states_full.astype(jnp.float32) + summed).astype(jnp.bfloat16)
    normed = rms_scale(residual, gain_forward)
    residual_share = lax.dynamic_slice_in_dim(residual, head_rank * width_share, width_share, 1)
    slot_first = head_rank // 2 * expert_gateup.shape[0]
    terms = expert_terms(
        normed, route_experts, route_weights, expert_gateup, expert_down, slot_first
    )
    expert_share = lax.psum_scatter(
        terms.astype(jnp.bfloat16), T, scatter_dimension=1, tiled=True
    ).astype(jnp.float32)
    layer_output = (residual_share.astype(jnp.float32) + expert_share).astype(jnp.bfloat16)
    group_count = lax.axis_size(G)
    per_owner = tokens // group_count
    owners = cache_slots // tokens
    sequence = jnp.arange(tokens, dtype=jnp.int32)
    ordering = jnp.argsort(owners * tokens + sequence)
    send_rows = own_rows[ordering].reshape(group_count, per_owner, keyvalue_heads, 2 * HD)
    send_slots = cache_slots[ordering].reshape(group_count, per_owner)
    got_rows, got_slots = (
        lax.all_to_all(send_rows, G, split_axis=0, concat_axis=0, tiled=True),
        lax.all_to_all(send_slots, G, split_axis=0, concat_axis=0, tiled=True),
    )
    targets = got_slots.reshape(tokens) - group_rank * tokens
    paged_rows = (
        jnp.zeros_like(own_rows).at[targets].set(got_rows.reshape(tokens, keyvalue_heads, 2 * HD))
    )
    return (layer_output, paged_rows, log_sums)


def solution(mesh):
    fine = Mesh(mesh.devices.reshape(8, 2, 2, 2, 4), ("z", "yh", "c", "yl", "x"))
    return jax.shard_map(
        shards,
        mesh=fine,
        in_specs=(
            P(G, T),
            P(G),
            P(G),
            P(T),
            P(T),
            P(G, T),
            P(G, T, None),
            P(T, None),
            P(G, None),
            P(G, None),
            P(T, None, None),
            P(T, None, None),
            P(G),
        ),
        out_specs=(P(G, T), P(G, T, None), P(T, G)),
        check_vma=False,
    )
```

time: 331 us -> 253 us (0.76)
  blocking collectives: 105 us -> 0 us
  waiting for transfers between devices: 100 us -> 141 us
  other arithmetic: 41.2 us -> 19.6 us
  starting transfers between devices: 15.6 us -> 36.6 us
  local copies, waits for them, and re-layouts: 32.1 us -> 19.8 us
    all_gather x2 -> x0, blocking collectives: 86.1 us -> none  [the longest x1 46.9 us: shards(): lax.all_gather(keyvalue_weight, 'grp', axis=0, tiled=True)]
    ppermute x3 -> x12, waiting for transfers between devices: 0.49 us -> 24.4 us  [the longest x1 20.7 us: gather_rows_over_groups(): other_y = lax.ppermute(zfull, 'yh', [(0, 1), (1, 0)])]
    ppermute x3 -> x12, starting transfers between devices: 0.59 us -> 21.6 us  [the longest x7 17.7 us: gather_rows_over_groups(): got.append(lax.ppermute(block, 'z', [(i, (i + k) % nz) for i in range(nz)]))]
    unnamed x1 -> x0, blocking collectives: 19.2 us -> none
    scatter-add x1 -> x0, other arithmetic: 18.5 us -> none  [expert_terms(): jnp.zeros((tokens, width), jnp.float32).at[ranking.reshape(-1)]]
    psum x1, waiting for transfers between devices: 80.8 us -> 95.4 us  [shards(): summed = lax.psum(partial_value, T)]
    gather x4 -> x1, local copies, waits for them, and re-layouts: 14 us -> 0.61 us  [gather_rows_over_groups(): zfull = jnp.take(stacked, (zi - jnp.arange(nz)) % nz, axis=0)]
    sort x1 -> x0, other arithmetic: 3.91 us -> none  [expert_terms(): jnp.argsort(jnp.where(chosen, offsets, tokens + offsets), axis=0)[:CAP]]
  transfers between devices with their start and end apart: 8 -> 17, of which waited for: 4 -> 9; matrix products, arithmetic and copies ran while one was open for 10% -> 9% of each run, Pallas kernels for 0% -> 0%
where the time goes in v1:
time: 253 us; the launch traced here: 250 us
  waiting for transfers between devices  141 us (56%)
  starting transfers between devices  36.6 us (14%)
  local copies, waits for them, and re-layouts  19.8 us (8%)
  other arithmetic  19.6 us (8%)
  matrix products  19.4 us (8%)
  between operations  14.3 us (6%)
    psum x1, waiting for transfers between devices, shards(): summed = lax.psum(partial_value, T)  95.4 us
    ppermute x1, waiting for transfers between devices, gather_rows_over_groups(): other_y = lax.ppermute(zfull, 'yh', [(0, 1), (1, 0)])  20.7 us
    ppermute x7, starting transfers between devices, gather_rows_over_groups(): got.append(lax.ppermute(block, 'z', [(i, (i + k) % nz) for i in range(nz)]))  17.7 us
    all_to_all x1, waiting for transfers between devices, shards(): lax.all_to_all(send_rows, G, split_axis=0, concat_axis=0, tiled=True)  9.98 us
    all_to_all x1, starting transfers between devices, shards(): lax.all_to_all(send_slots, G, split_axis=0, concat_axis=0, tiled=True)  9.79 us
    all_to_all x1, waiting for transfers between devices, shards(): lax.all_to_all(send_slots, G, split_axis=0, concat_axis=0, tiled=True)  8.5 us
    dot_general x1, matrix products, expert_terms(): jnp.einsum('td,edf->etf', normed, gateup, preferred_element_type=jnp.floa...  7.52 us
    unnamed x28, local copies, waits for them, and re-layouts  5.29 us
  transfers between devices with their start and end apart: 17, of which 9 were waited for; matrix products, arithmetic and copies ran while one was open for 9% of the time, Pallas kernels for 0%

profile of v1, /device:TPU:32, one launch (start us, length us, event | category | flops | bytes accessed | tf_op | source)
XLA Modules:
  0.0 250.3 jit_solution(752531297667724004)
XLA Ops:
  7.2 0.9 pad_maximum_fusion.3
  8.1 1.9 collective-permute-start
  10.1 4.5 %collective-permute-start.1 = (bf16[48,320]{1,0:T(8,128)(2,1)S(1)}, bf16[48,320]{1,0:T(8,128)(2,1)S(1)}, u32[]{:S(2)}, u32[]{:S(2)}) collective-permute-start(bf16[48,320]{1,0:T(8,128)(2,1)S(1)} %pad_maximum_fusion.3), channel_id=1, source_target_pairs={{0,64},{32,96},{64,128},{96,160},{128,192},{160,224},{192,0},{224,... | collective-permute-start | bytes 92168 | tf_op jit(solution)/shard_map/ppermute | solution.py:78
  14.6 1.9 collective-permute-start.2
  16.5 1.4 collective-permute-start.3
  17.9 0.7 reshape.415
  18.6 0.7 reshape.416
  19.3 0.1 copy.48
  19.4 1.7 pad_maximum_fusion.1
  21.3 0.8 bitcast_dynamic-update-slice_fusion.7
  22.1 0.7 convert_element_type.66
  22.8 0.3 multiply_cosine_fusion
  23.2 3.2 %collective-permute-start.4 = (bf16[48,320]{1,0:T(8,128)(2,1)S(1)}, bf16[48,320]{1,0:T(8,128)(2,1)S(1)}, u32[]{:S(2)}, u32[]{:S(2)}) collective-permute-start(bf16[48,320]{1,0:T(8,128)(2,1)S(1)} %pad_maximum_fusion.3), channel_id=1, source_target_pairs={{0,160},{32,192},{64,224},{96,0},{128,32},{160,64},{192,96},{224,1... | collective-permute-start | bytes 92168 | tf_op jit(solution)/shard_map/ppermute | solution.py:78
  26.4 0.7 pad_add_fusion
  27.1 2.5 collective-permute-start.5
  29.5 2.3 collective-permute-start.6
  32.1 1.5 collective-permute-done.6
  33.6 0.6 gather_fusion
  34.2 0.1 broadcast_select_fusion
  34.3 3.3 %collective-permute-start.7 = (bf16[8,48,320]{2,1,0:T(8,128)(2,1)S(1)}, bf16[8,48,320]{2,1,0:T(8,128)(2,1)S(1)}, u32[]{:S(2)}, u32[]{:S(2)}) collective-permute-start(bf16[8,48,320]{2,1,0:T(8,128)(2,1)S(1)} %broadcast_select_fusion), channel_id=1, source_target_pairs={{0,16},{16,0},{1,17},{17,1},{2,18},{18,2},{3,19},{19,3},{4,20},{20... | collective-permute-start | bytes 737288 | tf_op jit(solution)/shard_map/ppermute | solution.py:82
  37.6 0.7 pad_add_fusion.1
  38.3 0.1 bitcast_select_fusion.1
  38.4 20.7 %collective-permute-done.7 = bf16[8,48,320]{2,1,0:T(8,128)(2,1)S(1)} collective-permute-done((bf16[8,48,320]{2,1,0:T(8,128)(2,1)S(1)}, bf16[8,48,320]{2,1,0:T(8,128)(2,1)S(1)}, u32[]{:S(2)}, u32[]{:S(2)}) %collective-permute-start.7) | collective-permute-done | bytes 245792 | tf_op jit(solution)/shard_map/ppermute | solution.py:82
  59.1 0.2 maximum_select_fusion.2
  59.3 0.3 collective-permute-start.8
  59.6 0.8 compare_and_fusion
  60.4 0.1 fusion.59
  60.5 0.2 maximum_select_fusion.1
  60.7 0.8 collective-permute-done.8
  61.5 0.4 fusion.18
  61.9 1.1 copy.50
  63.0 2.3 all-gather.2.cloned.1.call-done
  65.3 2.6 %slice.95 = bf16[512,1536]{0,1:T(8,128)(2,1)} slice(bf16[520,1536]{0,1:T(8,128)(2,1)} %all-gather.2.cloned.1.call-done), slice={[0:512], [0:1536]} | slice | bytes 3145728 | tf_op jit(solution)/shard_map/slice | solution.py:113
  68.0 1.7 copy.59
  69.7 0.4 fusion.5
  70.1 1.5 convert_reduce_fusion
  71.6 2.0 convolution_bitcast_fusion.1
  73.6 0.3 fusion.36
  74.0 0.8 fusion.22
  75.0 1.3 collective-permute-done.9
  76.3 1.3 fusion.1
  77.6 1.4 fusion
  79.0 2.0 fusion.19
  81.0 2.3 fusion.54
  83.4 0.3 reduce-scatter.4.cloned.1.call-start
  83.8 95.4 %all-reduce.3.cloned.1.call-done = f32[512,1536]{1,0:T(8,128)} async-done(((f32[512,1536]{1,0:T(8,128)}), f32[512,1536]{1,0:T(8,128)}) %all-reduce.3.cloned.1.call-update) | async-done | bytes 3145744 | tf_op jit(solution)/shard_map/psum | solution.py:146
  179.2 2.4 fusion.2
  181.7 7.5 %convolution_bitcast_fusion = f32[5,512,512]{2,1,0:T(8,128)S(1)} fusion(bf16[5,1536,512]{2,1,0:T(8,128)(2,1)} %param.27, bf16[512,1536]{1,0:T(8,128)(2,1)S(1)} %get-tuple-element.47, f32[1536]{0:T(1024)S(1)} %get-tuple-element.44, f32[512]{0:T(512)S(1)} %add_rsqrt_fusion), kind=kOutput, calls=%fused_computation.26 | convolution fusion | flops 4029677568 | bytes 14688256 | tf_op jit(solution)/shard_map/td,edf->etf/dot_general | solution.py:64
  189.2 3.5 %multiply_reduce_fusion = bf16[512,1536]{1,0:T(8,128)(2,1)S(1)} fusion(bf16[5,256,1536]{2,1,0:T(8,128)(2,1)S(1)} %copy-done.8, f32[5,512]{1,0:T(8,128)S(1)} %bitcast.103, f32[5,512,512]{2,1,0:T(8,128)S(1)} %convolution_bitcast_fusion), kind=kOutput, calls=%fused_computation.4 | convolution fusion | flops 2024275968 | bytes 10758144 | tf_op jit(solution)/shard_map/etf,efd->etd/dot_general | solution.py:68
  192.7 1.6 copy.57
  194.4 3.8 %sort.17 = (s32[512]{0:T(512)}, s32[512]{0:T(512)S(1)}) sort(s32[512]{0:T(512)S(1)} %fusion.43, s32[512]{0:T(512)S(1)} %iota.31), dimensions={0}, to_apply=%region_8.9 | sort | flops 4608 | bytes 8192 | tf_op jit(solution)/shard_map/jit(argsort)/sort | solution.py:162
  198.2 3.5 %gather_fusion.1 = s32[512]{0:T(512)S(1)} fusion(s32[512]{0:T(512)S(1)} %copy-done.1, s32[1024]{0:T(1024)S(1)} %pad_clamp_fusion), kind=kCustom, calls=%fused_computation.1 | custom fusion | bytes 6144 | tf_op jit(solution)/shard_map/gather | solution.py:164
  201.7 0.7 all_to_all.9
  202.3 9.8 %all-to-all-start = ((s32[32,1,16]{2,1,0:T(1,128)}), s32[32,1,16]{2,1,0:T(1,128)S(1)}, u32[]{:S(2)}, u32[]{:S(2)}) async-start(s32[32,1,16]{2,1,0:T(1,128)} %bitcast.32), calls=%async_computation | async-start | bytes 32768 | tf_op jit(solution)/shard_map/all_to_all | solution.py:167
  212.2 8.5 %all-to-all-done = s32[32,1,16]{2,1,0:T(1,128)S(1)} async-done(((s32[32,1,16]{2,1,0:T(1,128)}), s32[32,1,16]{2,1,0:T(1,128)S(1)}, u32[]{:S(2)}, u32[]{:S(2)}) %all-to-all-start) | async-done | bytes 2080 | tf_op jit(solution)/shard_map/all_to_all | solution.py:167
  220.8 0.1 copy.53
  220.9 1.9 gather_fusion.2
  222.8 4.9 %all-to-all-start.1 = ((bf16[32,16,1,128]{3,1,2,0:T(8,128)(2,1)}), bf16[32,16,1,128]{3,1,2,0:T(8,128)(2,1)S(1)}, u32[]{:S(2)}, u32[]{:S(2)}) async-start(bf16[32,16,1,128]{3,1,2,0:T(8,128)(2,1)} %bitcast.36), calls=%async_computation.1 | async-start | bytes 262144 | tf_op jit(solution)/shard_map/all_to_all | solution.py:166
  227.8 0.6 log_add_fusion
  228.4 10.0 %all-to-all-done.1 = bf16[32,16,1,128]{3,1,2,0:T(8,128)(2,1)S(1)} async-done(((bf16[32,16,1,128]{3,1,2,0:T(8,128)(2,1)}), bf16[32,16,1,128]{3,1,2,0:T(8,128)(2,1)S(1)}, u32[]{:S(2)}, u32[]{:S(2)}) %all-to-all-start.1) | async-done | bytes 131104 | tf_op jit(solution)/shard_map/all_to_all | solution.py:166
  238.4 2.4 scatter_custom_fusion
  240.7 1.1 copy.58
  241.8 1.2 add_convert_fusion
  243.0 0.8 copy.55
  (63 shorter events, 1.1 us)
Async XLA Ops:
  7.2 73.8 %copy-start = (bf16[192,1536]{1,0:T(8,128)(2,1)S(1)}, bf16[192,1536]{1,0:T(8,128)(2,1)}, u32[]{:S(2)}) copy-start(bf16[192,1536]{1,0:T(8,128)(2,1)} %param.24) | copy-start | bytes 1769476
  7.2 52.4 %copy-start.7 = (s32[512]{0:T(512)S(1)}, s32[512]{0:T(512)}, u32[]{:S(2)}) copy-start(s32[512]{0:T(512)} %param.18) | copy-start | bytes 6148
  7.2 52.4 %copy-start.4 = (s32[512]{0:T(512)S(1)}, s32[512]{0:T(512)}, u32[]{:S(2)}) copy-start(s32[512]{0:T(512)} %param.19) | copy-start | bytes 6148
  7.2 58.1 %all-gather.2.cloned.1.call-start = ((), (), s32[]{:S(2)}) async-start(), calls=%async_computation.3 | async-start | bytes 2211840 | tf_op jit(solution)/shard_map/all_gather | solution.py:112
  8.1 18.9 %collective-permute-start = (bf16[48,320]{1,0:T(8,128)(2,1)S(1)}, bf16[48,320]{1,0:T(8,128)(2,1)S(1)}, u32[]{:S(2)}, u32[]{:S(2)}) collective-permute-start(bf16[48,320]{1,0:T(8,128)(2,1)S(1)} %pad_maximum_fusion.3), channel_id=1, source_target_pairs={{0,32},{32,64},{64,96},{96,128},{128,160},{160,192},{192,224},{224... | collective-permute-start | bytes 92168 | tf_op jit(solution)/shard_map/ppermute | solution.py:78
  10.1 19.5 %collective-permute-start.1 = (bf16[48,320]{1,0:T(8,128)(2,1)S(1)}, bf16[48,320]{1,0:T(8,128)(2,1)S(1)}, u32[]{:S(2)}, u32[]{:S(2)}) collective-permute-start(bf16[48,320]{1,0:T(8,128)(2,1)S(1)} %pad_maximum_fusion.3), channel_id=1, source_target_pairs={{0,64},{32,96},{64,128},{96,160},{128,192},{160,224},{192,0},{224,... | collective-permute-start | bytes 92168 | tf_op jit(solution)/shard_map/ppermute | solution.py:78
  14.6 17.3 %collective-permute-start.2 = (bf16[48,320]{1,0:T(8,128)(2,1)S(1)}, bf16[48,320]{1,0:T(8,128)(2,1)S(1)}, u32[]{:S(2)}, u32[]{:S(2)}) collective-permute-start(bf16[48,320]{1,0:T(8,128)(2,1)S(1)} %pad_maximum_fusion.3), channel_id=1, source_target_pairs={{0,96},{32,128},{64,160},{96,192},{128,224},{160,0},{192,32},{224,... | collective-permute-start | bytes 92168 | tf_op jit(solution)/shard_map/ppermute | solution.py:78
  16.5 15.5 %collective-permute-start.3 = (bf16[48,320]{1,0:T(8,128)(2,1)S(1)}, bf16[48,320]{1,0:T(8,128)(2,1)S(1)}, u32[]{:S(2)}, u32[]{:S(2)}) collective-permute-start(bf16[48,320]{1,0:T(8,128)(2,1)S(1)} %pad_maximum_fusion.3), channel_id=1, source_target_pairs={{0,128},{32,160},{64,192},{96,224},{128,0},{160,32},{192,64},{224,... | collective-permute-start | bytes 92168 | tf_op jit(solution)/shard_map/ppermute | solution.py:78
  21.1 158.1 %all-reduce.3.cloned.1.call-start = ((), (), s32[]{:S(2)}) async-start(), calls=%async_computation.4 | async-start | bytes 6291456 | tf_op jit(solution)/shard_map/psum | solution.py:146
  21.2 2.0 collective-permute-start.10
  23.2 8.8 %collective-permute-start.4 = (bf16[48,320]{1,0:T(8,128)(2,1)S(1)}, bf16[48,320]{1,0:T(8,128)(2,1)S(1)}, u32[]{:S(2)}, u32[]{:S(2)}) collective-permute-start(bf16[48,320]{1,0:T(8,128)(2,1)S(1)} %pad_maximum_fusion.3), channel_id=1, source_target_pairs={{0,160},{32,192},{64,224},{96,0},{128,32},{160,64},{192,96},{224,1... | collective-permute-start | bytes 92168 | tf_op jit(solution)/shard_map/ppermute | solution.py:78
  27.1 5.0 %collective-permute-start.5 = (bf16[48,320]{1,0:T(8,128)(2,1)S(1)}, bf16[48,320]{1,0:T(8,128)(2,1)S(1)}, u32[]{:S(2)}, u32[]{:S(2)}) collective-permute-start(bf16[48,320]{1,0:T(8,128)(2,1)S(1)} %pad_maximum_fusion.3), channel_id=1, source_target_pairs={{0,192},{32,224},{64,0},{96,32},{128,64},{160,96},{192,128},{224,1... | collective-permute-start | bytes 92168 | tf_op jit(solution)/shard_map/ppermute | solution.py:78
  29.5 4.0 %collective-permute-start.6 = (bf16[48,320]{1,0:T(8,128)(2,1)S(1)}, bf16[48,320]{1,0:T(8,128)(2,1)S(1)}, u32[]{:S(2)}, u32[]{:S(2)}) collective-permute-start(bf16[48,320]{1,0:T(8,128)(2,1)S(1)} %pad_maximum_fusion.3), channel_id=1, source_target_pairs={{0,224},{32,0},{64,32},{96,64},{128,96},{160,128},{192,160},{224,1... | collective-permute-start | bytes 92168 | tf_op jit(solution)/shard_map/ppermute | solution.py:78
  31.8 5.7 %collective-permute-start.11 = (s32[512]{0:T(512)}, s32[512]{0:T(512)S(1)}, u32[]{:S(2)}, u32[]{:S(2)}) collective-permute-start(s32[512]{0:T(512)} %param.19), channel_id=1, source_target_pairs={{0,8},{8,0},{1,9},{9,1},{2,10},{10,2},{3,11},{11,3},{4,12},{12,4},... | collective-permute-start | bytes 6152 | tf_op jit(solution)/shard_map/ppermute | solution.py:134
  34.3 24.8 %collective-permute-start.7 = (bf16[8,48,320]{2,1,0:T(8,128)(2,1)S(1)}, bf16[8,48,320]{2,1,0:T(8,128)(2,1)S(1)}, u32[]{:S(2)}, u32[]{:S(2)}) collective-permute-start(bf16[8,48,320]{2,1,0:T(8,128)(2,1)S(1)} %broadcast_select_fusion), channel_id=1, source_target_pairs={{0,16},{16,0},{1,17},{17,1},{2,18},{18,2},{3,19},{19,3},{4,20},{20... | collective-permute-start | bytes 737288 | tf_op jit(solution)/shard_map/ppermute | solution.py:82
  59.3 2.3 collective-permute-start.8
  69.7 4.3 %copy-start.3 = (bf16[8,2,2,48,320]{4,3,2,1,0:T(8,128)(2,1)S(1)}, bf16[8,2,2,48,320]{4,3,2,1,0:T(8,128)(2,1)}, u32[]{:S(2)}) copy-start(bf16[8,2,2,48,320]{4,3,2,1,0:T(8,128)(2,1)} %copy.50) | copy-start | bytes 2949124
  74.8 1.4 collective-permute-start.9
  81.0 2.7 %copy-start.5 = (f32[512,8]{0,1:T(8,128)S(1)}, f32[512,8]{0,1:T(8,128)}, u32[]{:S(2)}) copy-start(f32[512,8]{0,1:T(8,128)} %param.26) | copy-start | bytes 49156
  81.0 2.7 %copy-start.6 = (s32[512,8]{0,1:T(8,128)S(1)}, s32[512,8]{0,1:T(8,128)}, u32[]{:S(2)}) copy-start(s32[512,8]{0,1:T(8,128)} %param.25) | copy-start | bytes 49156
  83.4 157.4 %reduce-scatter.4.cloned.1.call-start = ((), (), s32[]{:S(2)}) async-start(), calls=%async_computation.5 | async-start | bytes 1769472
  181.7 7.6 %copy-start.2 = (bf16[512,1536]{1,0:T(8,128)(2,1)}, bf16[512,1536]{1,0:T(8,128)(2,1)S(1)}, u32[]{:S(2)}) copy-start(bf16[512,1536]{1,0:T(8,128)(2,1)S(1)} %get-tuple-element.47) | copy-start | bytes 4718596
  181.7 7.6 %copy-start.8 = (bf16[5,256,1536]{2,1,0:T(8,128)(2,1)S(1)}, bf16[5,256,1536]{2,1,0:T(8,128)(2,1)}, u32[]{:S(2)}) copy-start(bf16[5,256,1536]{2,1,0:T(8,128)(2,1)} %param.28) | copy-start | bytes 11796484
  192.7 1.6 copy-start.1
  202.3 18.3 %all-to-all-start = ((s32[32,1,16]{2,1,0:T(1,128)}), s32[32,1,16]{2,1,0:T(1,128)S(1)}, u32[]{:S(2)}, u32[]{:S(2)}) async-start(s32[32,1,16]{2,1,0:T(1,128)} %bitcast.32), calls=%async_computation | async-start | bytes 32768 | tf_op jit(solution)/shard_map/all_to_all | solution.py:167
  222.8 15.5 %all-to-all-start.1 = ((bf16[32,16,1,128]{3,1,2,0:T(8,128)(2,1)}), bf16[32,16,1,128]{3,1,2,0:T(8,128)(2,1)S(1)}, u32[]{:S(2)}, u32[]{:S(2)}) async-start(bf16[32,16,1,128]{3,1,2,0:T(8,128)(2,1)} %bitcast.36), calls=%async_computation.1 | async-start | bytes 262144 | tf_op jit(solution)/shard_map/all_to_all | solution.py:166
Sparse Core Ops, SparseCore 0:
  21.2 44.0 all-gather.1
  83.5 95.7 all-reduce.2
  194.5 43.5 reduce-scatter.3

commit v2 on v1

--- a/solution.py
+++ b/solution.py
@@ -85,6 +85,25 @@
     other_c = lax.ppermute(yfull, "c", [(0, 1), (1, 0)])
     cfull = jnp.where(ci == 0, jnp.stack([yfull, other_c]), jnp.stack([other_c, yfull]))
     return cfull.transpose(2, 1, 0, 3, 4).reshape(-1, width)
+
+
+def place_cache_rows(own_rows, cache_slots, group_rank):
+    tokens, keyvalue_heads, row_width = own_rows.shape
+    group_count = lax.axis_size(G)
+    per_owner = tokens // group_count
+    owners = cache_slots // tokens
+    sequence = jnp.arange(tokens, dtype=jnp.int32)
+    ordering = jnp.argsort(owners * tokens + sequence)
+    send_rows = own_rows[ordering].reshape(group_count, per_owner, keyvalue_heads, row_width)
+    send_slots = cache_slots[ordering].reshape(group_count, per_owner)
+    got_rows, got_slots = (
+        lax.all_to_all(send_rows, G, split_axis=0, concat_axis=0, tiled=True),
+        lax.all_to_all(send_slots, G, split_axis=0, concat_axis=0, tiled=True),
+    )
+    targets = got_slots.reshape(tokens) - group_rank * tokens
+    return jnp.zeros_like(own_rows).at[targets].set(
+        got_rows.reshape(tokens, keyvalue_heads, row_width)
+    )
 
 
 def shards(
@@ -143,8 +162,13 @@
     attended = mixed.reshape(tokens, heads_local * HD)
     log_sums = log_part.reshape(heads_local, tokens)
     partial_value = jnp.dot(attended, output_weight, preferred_element_type=jnp.float32)
-    summed = lax.psum(partial_value, T)
-    residual = (states_full.astype(jnp.float32) + summed).astype(jnp.bfloat16)
+    partial_low, own_rows, cache_slots = lax.optimization_barrier(
+        (partial_value.astype(jnp.bfloat16), own_rows, cache_slots)
+    )
+    summed = lax.psum(partial_low, T)
+    paged_rows = place_cache_rows(own_rows, cache_slots, group_rank)
+    summed, paged_rows = lax.optimization_barrier((summed, paged_rows))
+    residual = (states_full.astype(jnp.float32) + summed.astype(jnp.float32)).astype(jnp.bfloat16)
     normed = rms_scale(residual, gain_forward)
     residual_share = lax.dynamic_slice_in_dim(residual, head_rank * width_share, width_share, 1)
     slot_first = head_rank // 2 * expert_gateup.shape[0]
@@ -155,21 +179,6 @@
         terms.astype(jnp.bfloat16), T, scatter_dimension=1, tiled=True
     ).astype(jnp.float32)
     layer_output = (residual_share.astype(jnp.float32) + expert_share).astype(jnp.bfloat16)
-    group_count = lax.axis_size(G)
-    per_owner = tokens // group_count
-    owners = cache_slots // tokens
-    sequence = jnp.arange(tokens, dtype=jnp.int32)
-    ordering = jnp.argsort(owners * tokens + sequence)
-    send_rows = own_rows[ordering].reshape(group_count, per_owner, keyvalue_heads, 2 * HD)
-    send_slots = cache_slots[ordering].reshape(group_count, per_owner)
-    got_rows, got_slots = (
-        lax.all_to_all(send_rows, G, split_axis=0, concat_axis=0, tiled=True),
-        lax.all_to_all(send_slots, G, split_axis=0, concat_axis=0, tiled=True),
-    )
-    targets = got_slots.reshape(tokens) - group_rank * tokens
-    paged_rows = (
-        jnp.zeros_like(own_rows).at[targets].set(got_rows.reshape(tokens, keyvalue_heads, 2 * HD))
-    )
     return (layer_output, paged_rows, log_sums)
 
 

time: 253 us -> 236 us (0.933)
  waiting for transfers between devices: 141 us -> 126 us
    psum x1, waiting for transfers between devices: 95.4 us -> 40.3 us  [shards(): summed = lax.psum(partial_low, T)]
    unnamed x4, waiting for transfers between devices: 0.05 us -> 42.7 us
  transfers between devices with their start and end apart: 17 -> 17, of which waited for: 9 -> 10; matrix products, arithmetic and copies ran while one was open for 9% -> 10% of each run, Pallas kernels for 0% -> 0%
where the time goes in v2:
time: 236 us; the launch traced here: 235 us
  waiting for transfers between devices  126 us (53%)
  starting transfers between devices  37.2 us (16%)
  local copies, waits for them, and re-layouts  19.8 us (8%)
  other arithmetic  19.2 us (8%)
  matrix products  18.9 us (8%)
  between operations  14.3 us (6%)
    unnamed x4, waiting for transfers between devices  42.7 us
    psum x1, waiting for transfers between devices, shards(): summed = lax.psum(partial_low, T)  40.3 us
    ppermute x1, waiting for transfers between devices, gather_rows_over_groups(): other_y = lax.ppermute(zfull, 'yh', [(0, 1), (1, 0)])  20.7 us
    ppermute x7, starting transfers between devices, gather_rows_over_groups(): got.append(lax.ppermute(block, 'z', [(i, (i + k) % nz) for i in range(nz)]))  17.7 us
    all_to_all x1, starting transfers between devices, place_cache_rows(): lax.all_to_all(send_slots, G, split_axis=0, concat_axis=0, tiled=True)  10.4 us
    all_to_all x1, waiting for transfers between devices, place_cache_rows(): lax.all_to_all(send_rows, G, split_axis=0, concat_axis=0, tiled=True)  10.1 us
    dot_general x1, matrix products, expert_terms(): jnp.einsum('td,edf->etf', normed, gateup, preferred_element_type=jnp.floa...  7.51 us
    all_to_all x1, waiting for transfers between devices, place_cache_rows(): lax.all_to_all(send_slots, G, split_axis=0, concat_axis=0, tiled=True)  6.36 us
  transfers between devices with their start and end apart: 17, of which 10 were waited for; matrix products, arithmetic and copies ran while one was open for 10% of the time, Pallas kernels for 0%

profile of v2, /device:TPU:32, one launch (start us, length us, event | category | flops | bytes accessed | tf_op | source)
XLA Modules:
  0.0 235.5 jit_solution(6388496924861221764)
XLA Ops:
  7.2 0.9 pad_maximum_fusion.3
  8.1 1.9 collective-permute-start
  10.1 4.5 %collective-permute-start.1 = (bf16[48,320]{1,0:T(8,128)(2,1)S(1)}, bf16[48,320]{1,0:T(8,128)(2,1)S(1)}, u32[]{:S(2)}, u32[]{:S(2)}) collective-permute-start(bf16[48,320]{1,0:T(8,128)(2,1)S(1)} %pad_maximum_fusion.3), channel_id=1, source_target_pairs={{0,64},{32,96},{64,128},{96,160},{128,192},{160,224},{192,0},{224,... | collective-permute-start | bytes 92168 | tf_op jit(solution)/shard_map/ppermute | solution.py:78
  14.6 1.9 collective-permute-start.2
  16.5 1.4 collective-permute-start.3
  17.9 0.7 reshape.415
  18.6 0.7 reshape.416
  19.3 0.1 copy.48
  19.4 1.7 pad_maximum_fusion.1
  21.3 0.8 bitcast_dynamic-update-slice_fusion.7
  22.1 0.7 convert_element_type.72
  22.8 0.3 multiply_cosine_fusion
  23.2 3.2 %collective-permute-start.4 = (bf16[48,320]{1,0:T(8,128)(2,1)S(1)}, bf16[48,320]{1,0:T(8,128)(2,1)S(1)}, u32[]{:S(2)}, u32[]{:S(2)}) collective-permute-start(bf16[48,320]{1,0:T(8,128)(2,1)S(1)} %pad_maximum_fusion.3), channel_id=1, source_target_pairs={{0,160},{32,192},{64,224},{96,0},{128,32},{160,64},{192,96},{224,1... | collective-permute-start | bytes 92168 | tf_op jit(solution)/shard_map/ppermute | solution.py:78
  26.4 0.7 pad_add_fusion
  27.1 2.5 %collective-permute-start.5 = (bf16[48,320]{1,0:T(8,128)(2,1)S(1)}, bf16[48,320]{1,0:T(8,128)(2,1)S(1)}, u32[]{:S(2)}, u32[]{:S(2)}) collective-permute-start(bf16[48,320]{1,0:T(8,128)(2,1)S(1)} %pad_maximum_fusion.3), channel_id=1, source_target_pairs={{0,192},{32,224},{64,0},{96,32},{128,64},{160,96},{192,128},{224,1... | collective-permute-start | bytes 92168 | tf_op jit(solution)/shard_map/ppermute | solution.py:78
  29.5 2.3 collective-permute-start.6
  32.1 1.5 collective-permute-done.6
  33.6 0.6 gather_fusion
  34.2 0.1 broadcast_select_fusion
  34.3 3.3 %collective-permute-start.7 = (bf16[8,48,320]{2,1,0:T(8,128)(2,1)S(1)}, bf16[8,48,320]{2,1,0:T(8,128)(2,1)S(1)}, u32[]{:S(2)}, u32[]{:S(2)}) collective-permute-start(bf16[8,48,320]{2,1,0:T(8,128)(2,1)S(1)} %broadcast_select_fusion), channel_id=1, source_target_pairs={{0,16},{16,0},{1,17},{17,1},{2,18},{18,2},{3,19},{19,3},{4,20},{20... | collective-permute-start | bytes 737288 | tf_op jit(solution)/shard_map/ppermute | solution.py:82
  37.6 0.7 pad_add_fusion.1
  38.4 20.7 %collective-permute-done.7 = bf16[8,48,320]{2,1,0:T(8,128)(2,1)S(1)} collective-permute-done((bf16[8,48,320]{2,1,0:T(8,128)(2,1)S(1)}, bf16[8,48,320]{2,1,0:T(8,128)(2,1)S(1)}, u32[]{:S(2)}, u32[]{:S(2)}) %collective-permute-start.7) | collective-permute-done | bytes 245792 | tf_op jit(solution)/shard_map/ppermute | solution.py:82
  59.1 0.2 maximum_select_fusion.2
  59.3 0.3 collective-permute-start.8
  59.6 0.8 compare_and_fusion
  60.4 0.1 fusion.57
  60.5 0.2 maximum_select_fusion.1
  60.7 0.8 collective-permute-done.8
  61.5 0.4 fusion.18
  61.9 1.1 copy.50
  63.0 2.3 all-gather.2.cloned.1.call-done
  65.3 2.6 %slice.95 = bf16[512,1536]{0,1:T(8,128)(2,1)} slice(bf16[520,1536]{0,1:T(8,128)(2,1)} %all-gather.2.cloned.1.call-done), slice={[0:512], [0:1536]} | slice | bytes 3145728 | tf_op jit(solution)/shard_map/slice | solution.py:132
  68.0 1.7 copy.59
  69.7 0.4 fusion.5
  70.1 1.5 convert_reduce_fusion
  71.6 2.0 convolution_bitcast_fusion.1
  73.6 0.3 fusion.36
  74.0 0.8 fusion.22
  75.0 1.3 collective-permute-done.9
  76.3 1.4 fusion.1
  77.6 1.4 fusion
  79.0 2.0 fusion.19
  81.1 1.8 convolution_convert_fusion
  83.0 3.8 %sort.17 = (s32[512]{0:T(512)}, s32[512]{0:T(512)S(1)}) sort(s32[512]{0:T(512)S(1)} %fusion.43, s32[512]{0:T(512)S(1)} %iota.30), dimensions={0}, to_apply=%region_4.5 | sort | flops 4608 | bytes 8192 | tf_op jit(solution)/shard_map/jit(argsort)/sort | solution.py:96
  86.7 3.5 %gather_fusion.1 = s32[512]{0:T(512)S(1)} fusion(s32[512]{0:T(512)S(1)} %copy-done.1, s32[1024]{0:T(1024)S(1)} %pad_clamp_fusion), kind=kCustom, calls=%fused_computation.1 | custom fusion | bytes 6144 | tf_op jit(solution)/shard_map/gather | solution.py:98
  90.2 0.7 all_to_all.9
  90.9 10.4 %all-to-all-start = ((s32[32,1,16]{2,1,0:T(1,128)}), s32[32,1,16]{2,1,0:T(1,128)S(1)}, u32[]{:S(2)}, u32[]{:S(2)}) async-start(s32[32,1,16]{2,1,0:T(1,128)} %bitcast.29), calls=%async_computation | async-start | bytes 32768 | tf_op jit(solution)/shard_map/all_to_all | solution.py:101
  101.5 0.1 copy.53
  101.6 1.9 gather_fusion.2
  103.5 6.4 %all-to-all-done = s32[32,1,16]{2,1,0:T(1,128)S(1)} async-done(((s32[32,1,16]{2,1,0:T(1,128)}), s32[32,1,16]{2,1,0:T(1,128)S(1)}, u32[]{:S(2)}, u32[]{:S(2)}) %all-to-all-start) | async-done | bytes 2080 | tf_op jit(solution)/shard_map/all_to_all | solution.py:101
  109.9 4.9 %all-to-all-start.1 = ((bf16[32,16,1,128]{3,1,2,0:T(8,128)(2,1)}), bf16[32,16,1,128]{3,1,2,0:T(8,128)(2,1)S(1)}, u32[]{:S(2)}, u32[]{:S(2)}) async-start(bf16[32,16,1,128]{3,1,2,0:T(8,128)(2,1)} %bitcast.33), calls=%async_computation.1 | async-start | bytes 262144 | tf_op jit(solution)/shard_map/all_to_all | solution.py:100
  114.8 0.3 reduce-scatter.4.cloned.1.call-start
  115.2 10.1 %all-to-all-done.1 = bf16[32,16,1,128]{3,1,2,0:T(8,128)(2,1)S(1)} async-done(((bf16[32,16,1,128]{3,1,2,0:T(8,128)(2,1)}), bf16[32,16,1,128]{3,1,2,0:T(8,128)(2,1)S(1)}, u32[]{:S(2)}, u32[]{:S(2)}) %all-to-all-start.1) | async-done | bytes 131104 | tf_op jit(solution)/shard_map/all_to_all | solution.py:100
  125.3 2.4 %scatter_custom_fusion = bf16[512,128]{1,0:T(8,128)(2,1)} fusion(s32[512]{0:T(512)S(1)} %bitcast.104, bf16[512,128]{1,0:T(8,128)(2,1)S(1)} %bitcast.100, bf16[]{:T(256)} %constant.139.clone.1), kind=kCustom, calls=%fused_computation.72 | custom fusion | bytes 131074 | tf_op jit(solution)/shard_map/scatter | solution.py:104
  127.7 40.3 %all-reduce.3.cloned.1.call-done = bf16[512,1536]{1,0:T(8,128)(2,1)} async-done(((bf16[512,1536]{1,0:T(8,128)(2,1)}), bf16[512,1536]{1,0:T(8,128)(2,1)}) %all-reduce.3.cloned.1.call-update) | async-done | bytes 1572880 | tf_op jit(solution)/shard_map/psum | solution.py:168
  168.0 2.0 fusion.2
  170.0 7.5 %convolution_bitcast_fusion = f32[5,512,512]{2,1,0:T(8,128)S(1)} fusion(bf16[5,1536,512]{2,1,0:T(8,128)(2,1)} %param.27, bf16[512,1536]{1,0:T(8,128)(2,1)S(1)} %get-tuple-element.57, f32[1536]{0:T(1024)S(1)} %get-tuple-element.54, f32[512]{0:T(512)S(1)} %add_rsqrt_fusion), kind=kOutput, calls=%fused_computation.27 | convolution fusion | flops 4029677568 | bytes 14688256 | tf_op jit(solution)/shard_map/td,edf->etf/dot_general | solution.py:64
  177.6 3.5 %multiply_reduce_fusion = bf16[512,1536]{1,0:T(8,128)(2,1)S(1)} fusion(bf16[5,256,1536]{2,1,0:T(8,128)(2,1)S(1)} %copy-done.8, f32[5,512]{1,0:T(8,128)S(1)} %bitcast.103, f32[5,512,512]{2,1,0:T(8,128)S(1)} %convolution_bitcast_fusion), kind=kOutput, calls=%fused_computation.4 | convolution fusion | flops 2024275968 | bytes 10758144 | tf_op jit(solution)/shard_map/etf,efd->etd/dot_general | solution.py:68
  181.1 1.6 copy.57
  182.7 0.6 log_add_fusion
  183.3 42.6 %reduce-scatter.4.cloned.1.call-done = bf16[192,512]{1,0:T(8,128)(2,1)} async-done(((bf16[1536,512]{1,0:T(8,128)(2,1)}), bf16[192,512]{1,0:T(8,128)(2,1)}) %reduce-scatter.4.cloned.1.call-update) | async-done | bytes 196624
  225.9 1.1 copy.58
  227.0 1.2 add_convert_fusion
  228.1 0.8 copy.55
  (63 shorter events, 1.2 us)
Async XLA Ops:
  7.2 74.0 %copy-start = (bf16[192,1536]{1,0:T(8,128)(2,1)S(1)}, bf16[192,1536]{1,0:T(8,128)(2,1)}, u32[]{:S(2)}) copy-start(bf16[192,1536]{1,0:T(8,128)(2,1)} %param.24) | copy-start | bytes 1769476
  7.2 52.4 %copy-start.7 = (s32[512]{0:T(512)S(1)}, s32[512]{0:T(512)}, u32[]{:S(2)}) copy-start(s32[512]{0:T(512)} %param.18) | copy-start | bytes 6148
  7.2 52.4 %copy-start.4 = (s32[512]{0:T(512)S(1)}, s32[512]{0:T(512)}, u32[]{:S(2)}) copy-start(s32[512]{0:T(512)} %param.19) | copy-start | bytes 6148
  7.2 58.1 %all-gather.2.cloned.1.call-start = ((), (), s32[]{:S(2)}) async-start(), calls=%async_computation.3 | async-start | bytes 2211840 | tf_op jit(solution)/shard_map/all_gather | solution.py:131
  8.1 18.9 %collective-permute-start = (bf16[48,320]{1,0:T(8,128)(2,1)S(1)}, bf16[48,320]{1,0:T(8,128)(2,1)S(1)}, u32[]{:S(2)}, u32[]{:S(2)}) collective-permute-start(bf16[48,320]{1,0:T(8,128)(2,1)S(1)} %pad_maximum_fusion.3), channel_id=1, source_target_pairs={{0,32},{32,64},{64,96},{96,128},{128,160},{160,192},{192,224},{224... | collective-permute-start | bytes 92168 | tf_op jit(solution)/shard_map/ppermute | solution.py:78
  10.1 19.5 %collective-permute-start.1 = (bf16[48,320]{1,0:T(8,128)(2,1)S(1)}, bf16[48,320]{1,0:T(8,128)(2,1)S(1)}, u32[]{:S(2)}, u32[]{:S(2)}) collective-permute-start(bf16[48,320]{1,0:T(8,128)(2,1)S(1)} %pad_maximum_fusion.3), channel_id=1, source_target_pairs={{0,64},{32,96},{64,128},{96,160},{128,192},{160,224},{192,0},{224,... | collective-permute-start | bytes 92168 | tf_op jit(solution)/shard_map/ppermute | solution.py:78
  14.6 17.3 %collective-permute-start.2 = (bf16[48,320]{1,0:T(8,128)(2,1)S(1)}, bf16[48,320]{1,0:T(8,128)(2,1)S(1)}, u32[]{:S(2)}, u32[]{:S(2)}) collective-permute-start(bf16[48,320]{1,0:T(8,128)(2,1)S(1)} %pad_maximum_fusion.3), channel_id=1, source_target_pairs={{0,96},{32,128},{64,160},{96,192},{128,224},{160,0},{192,32},{224,... | collective-permute-start | bytes 92168 | tf_op jit(solution)/shard_map/ppermute | solution.py:78
  16.5 15.5 %collective-permute-start.3 = (bf16[48,320]{1,0:T(8,128)(2,1)S(1)}, bf16[48,320]{1,0:T(8,128)(2,1)S(1)}, u32[]{:S(2)}, u32[]{:S(2)}) collective-permute-start(bf16[48,320]{1,0:T(8,128)(2,1)S(1)} %pad_maximum_fusion.3), channel_id=1, source_target_pairs={{0,128},{32,160},{64,192},{96,224},{128,0},{160,32},{192,64},{224,... | collective-permute-start | bytes 92168 | tf_op jit(solution)/shard_map/ppermute | solution.py:78
  21.1 146.9 %all-reduce.3.cloned.1.call-start = ((), (), s32[]{:S(2)}) async-start(), calls=%async_computation.4 | async-start | bytes 3145728 | tf_op jit(solution)/shard_map/psum | solution.py:168
  21.2 2.0 collective-permute-start.10
  23.2 8.8 %collective-permute-start.4 = (bf16[48,320]{1,0:T(8,128)(2,1)S(1)}, bf16[48,320]{1,0:T(8,128)(2,1)S(1)}, u32[]{:S(2)}, u32[]{:S(2)}) collective-permute-start(bf16[48,320]{1,0:T(8,128)(2,1)S(1)} %pad_maximum_fusion.3), channel_id=1, source_target_pairs={{0,160},{32,192},{64,224},{96,0},{128,32},{160,64},{192,96},{224,1... | collective-permute-start | bytes 92168 | tf_op jit(solution)/shard_map/ppermute | solution.py:78
  27.1 5.0 %collective-permute-start.5 = (bf16[48,320]{1,0:T(8,128)(2,1)S(1)}, bf16[48,320]{1,0:T(8,128)(2,1)S(1)}, u32[]{:S(2)}, u32[]{:S(2)}) collective-permute-start(bf16[48,320]{1,0:T(8,128)(2,1)S(1)} %pad_maximum_fusion.3), channel_id=1, source_target_pairs={{0,192},{32,224},{64,0},{96,32},{128,64},{160,96},{192,128},{224,1... | collective-permute-start | bytes 92168 | tf_op jit(solution)/shard_map/ppermute | solution.py:78
  29.5 4.0 %collective-permute-start.6 = (bf16[48,320]{1,0:T(8,128)(2,1)S(1)}, bf16[48,320]{1,0:T(8,128)(2,1)S(1)}, u32[]{:S(2)}, u32[]{:S(2)}) collective-permute-start(bf16[48,320]{1,0:T(8,128)(2,1)S(1)} %pad_maximum_fusion.3), channel_id=1, source_target_pairs={{0,224},{32,0},{64,32},{96,64},{128,96},{160,128},{192,160},{224,1... | collective-permute-start | bytes 92168 | tf_op jit(solution)/shard_map/ppermute | solution.py:78
  31.8 5.7 %collective-permute-start.11 = (s32[512]{0:T(512)}, s32[512]{0:T(512)S(1)}, u32[]{:S(2)}, u32[]{:S(2)}) collective-permute-start(s32[512]{0:T(512)} %param.19), channel_id=1, source_target_pairs={{0,8},{8,0},{1,9},{9,1},{2,10},{10,2},{3,11},{11,3},{4,12},{12,4},... | collective-permute-start | bytes 6152 | tf_op jit(solution)/shard_map/ppermute | solution.py:153
  34.3 24.8 %collective-permute-start.7 = (bf16[8,48,320]{2,1,0:T(8,128)(2,1)S(1)}, bf16[8,48,320]{2,1,0:T(8,128)(2,1)S(1)}, u32[]{:S(2)}, u32[]{:S(2)}) collective-permute-start(bf16[8,48,320]{2,1,0:T(8,128)(2,1)S(1)} %broadcast_select_fusion), channel_id=1, source_target_pairs={{0,16},{16,0},{1,17},{17,1},{2,18},{18,2},{3,19},{19,3},{4,20},{20... | collective-permute-start | bytes 737288 | tf_op jit(solution)/shard_map/ppermute | solution.py:82
  59.3 2.3 collective-permute-start.8
  69.7 4.3 %copy-start.3 = (bf16[8,2,2,48,320]{4,3,2,1,0:T(8,128)(2,1)S(1)}, bf16[8,2,2,48,320]{4,3,2,1,0:T(8,128)(2,1)}, u32[]{:S(2)}) copy-start(bf16[8,2,2,48,320]{4,3,2,1,0:T(8,128)(2,1)} %copy.50) | copy-start | bytes 2949124
  74.8 1.4 collective-permute-start.9
  81.1 1.9 copy-start.1
  81.1 20.2 %copy-start.5 = (f32[512,8]{0,1:T(8,128)S(1)}, f32[512,8]{0,1:T(8,128)}, u32[]{:S(2)}) copy-start(f32[512,8]{0,1:T(8,128)} %param.26) | copy-start | bytes 49156
  81.1 20.2 %copy-start.6 = (s32[512,8]{0,1:T(8,128)S(1)}, s32[512,8]{0,1:T(8,128)}, u32[]{:S(2)}) copy-start(s32[512,8]{0,1:T(8,128)} %param.25) | copy-start | bytes 49156
  90.9 18.9 %all-to-all-start = ((s32[32,1,16]{2,1,0:T(1,128)}), s32[32,1,16]{2,1,0:T(1,128)S(1)}, u32[]{:S(2)}, u32[]{:S(2)}) async-start(s32[32,1,16]{2,1,0:T(1,128)} %bitcast.29), calls=%async_computation | async-start | bytes 32768 | tf_op jit(solution)/shard_map/all_to_all | solution.py:101
  109.9 15.5 %all-to-all-start.1 = ((bf16[32,16,1,128]{3,1,2,0:T(8,128)(2,1)}), bf16[32,16,1,128]{3,1,2,0:T(8,128)(2,1)S(1)}, u32[]{:S(2)}, u32[]{:S(2)}) async-start(bf16[32,16,1,128]{3,1,2,0:T(8,128)(2,1)} %bitcast.33), calls=%async_computation.1 | async-start | bytes 262144 | tf_op jit(solution)/shard_map/all_to_all | solution.py:100
  114.8 111.1 %reduce-scatter.4.cloned.1.call-start = ((), (), s32[]{:S(2)}) async-start(), calls=%async_computation.5 | async-start | bytes 1769472
  170.0 7.6 %copy-start.2 = (bf16[512,1536]{1,0:T(8,128)(2,1)}, bf16[512,1536]{1,0:T(8,128)(2,1)S(1)}, u32[]{:S(2)}) copy-start(bf16[512,1536]{1,0:T(8,128)(2,1)S(1)} %get-tuple-element.57) | copy-start | bytes 4718596
  170.0 7.5 %copy-start.8 = (bf16[5,256,1536]{2,1,0:T(8,128)(2,1)S(1)}, bf16[5,256,1536]{2,1,0:T(8,128)(2,1)}, u32[]{:S(2)}) copy-start(bf16[5,256,1536]{2,1,0:T(8,128)(2,1)} %param.28) | copy-start | bytes 11796484
Sparse Core Ops, SparseCore 0:
  21.2 44.0 all-gather.1
  83.0 84.8 all-reduce.2
  182.8 43.0 reduce-scatter.3

commit v3 on v2

--- a/solution.py
+++ b/solution.py
@@ -104,6 +104,23 @@
     return jnp.zeros_like(own_rows).at[targets].set(
         got_rows.reshape(tokens, keyvalue_heads, row_width)
     )
+
+
+def gather_rows_over_heads(block):
+    width = block.shape[1]
+    nt = lax.axis_size(T)
+    ti = lax.axis_index(T)
+    ci = lax.axis_index("c")
+    half = block.shape[0] // 2
+    mine = lax.dynamic_slice_in_dim(block, ci * half, half, 0)
+    got = [mine]
+    for k in range(1, nt):
+        got.append(lax.ppermute(mine, T, [(i, (i + k) % nt) for i in range(nt)]))
+    stacked = jnp.stack(got)
+    halves = jnp.take(stacked, (ti - jnp.arange(nt)) % nt, axis=0)
+    other_c = lax.ppermute(halves, "c", [(0, 1), (1, 0)])
+    full = jnp.where(ci == 0, jnp.stack([halves, other_c], axis=1), jnp.stack([other_c, halves], axis=1))
+    return full.reshape(-1, width)
 
 
 def shards(
@@ -141,6 +158,7 @@
         [query_weight, keyvalue_weight.reshape(piece_rows, -1)], axis=1
     )
     weights_full = gather_rows_over_groups(weights_packed)
+    output_full = gather_rows_over_heads(output_weight)
     query_full_w = weights_full[:, :query_cols]
     keyvalue_full_w = weights_full[:, query_cols:]
     query_sum = jnp.dot(normed_in, query_full_w, preferred_element_type=jnp.float32)
@@ -161,14 +179,12 @@
     mixed, log_part = attend_block(query_block, segment_ids, positions, all_rows, all_seg, all_pos)
     attended = mixed.reshape(tokens, heads_local * HD)
     log_sums = log_part.reshape(heads_local, tokens)
-    partial_value = jnp.dot(attended, output_weight, preferred_element_type=jnp.float32)
-    partial_low, own_rows, cache_slots = lax.optimization_barrier(
-        (partial_value.astype(jnp.bfloat16), own_rows, cache_slots)
-    )
-    summed = lax.psum(partial_low, T)
+    attended, own_rows, cache_slots = lax.optimization_barrier((attended, own_rows, cache_slots))
+    attended_full = lax.all_gather(attended, T, axis=1, tiled=True)
     paged_rows = place_cache_rows(own_rows, cache_slots, group_rank)
-    summed, paged_rows = lax.optimization_barrier((summed, paged_rows))
-    residual = (states_full.astype(jnp.float32) + summed.astype(jnp.float32)).astype(jnp.bfloat16)
+    attended_full, paged_rows = lax.optimization_barrier((attended_full, paged_rows))
+    mixed_out = jnp.dot(attended_full, output_full, preferred_element_type=jnp.float32)
+    residual = (states_full.astype(jnp.float32) + mixed_out).astype(jnp.bfloat16)
     normed = rms_scale(residual, gain_forward)
     residual_share = lax.dynamic_slice_in_dim(residual, head_rank * width_share, width_share, 1)
     slot_first = head_rank // 2 * expert_gateup.shape[0]

time: 236 us -> 252 us (1.068)
  waiting for transfers between devices: 126 us -> 98.2 us
  starting transfers between devices: 37.2 us -> 51.8 us
  other arithmetic: 19.2 us -> 31.5 us
  local copies, waits for them, and re-layouts: 19.8 us -> 31 us
  matrix products: 18.9 us -> 24.2 us
    psum x1 -> x0, waiting for transfers between devices: 40.3 us -> none  [shards(): summed = lax.psum(partial_low, T)]
    ppermute x1, waiting for transfers between devices: 20.7 us -> 40.4 us  [gather_rows_over_groups(): other_y = lax.ppermute(zfull, 'yh', [(0, 1), (1, 0)])]
    ppermute x0 -> x8, starting transfers between devices: none -> 10.7 us  [the longest x7 10.7 us: gather_rows_over_heads(): got.append(lax.ppermute(mine, T, [(i, (i + k) % nt) for i in range(nt)]))]
    select_n x0 -> x4, other arithmetic: none -> 10.3 us  [the longest x1 6.87 us: gather_rows_over_heads(): jnp.where(ci == 0, jnp.stack([halves, other_c], axis=1), jnp.stack([other...]
    ppermute x0 -> x8, waiting for transfers between devices: none -> 8.43 us  [the longest x7 8.42 us: gather_rows_over_heads(): got.append(lax.ppermute(mine, T, [(i, (i + k) % nt) for i in range(nt)]))]
    unnamed x28 -> x35, local copies, waits for them, and re-layouts: 5.29 us -> 13.3 us
    all_to_all x1, waiting for transfers between devices: 6.36 us -> 0.01 us  [place_cache_rows(): lax.all_to_all(send_slots, G, split_axis=0, concat_axis=0, tiled=True)]
    all_to_all x1, starting transfers between devices: 4.92 us -> 9.77 us  [place_cache_rows(): lax.all_to_all(send_rows, G, split_axis=0, concat_axis=0, tiled=True)]
  transfers between devices with their start and end apart: 17 -> 25, of which waited for: 10 -> 7; matrix products, arithmetic and copies ran while one was open for 10% -> 26% of each run, Pallas kernels for 0% -> 0%
where the time goes in v3:
time: 252 us; the launch traced here: 251 us
  waiting for transfers between devices  98.2 us (39%)
  starting transfers between devices  51.8 us (21%)
  other arithmetic  31.5 us (12%)
  local copies, waits for them, and re-layouts  31 us (12%)
  matrix products  24.2 us (10%)
  between operations  14.2 us (6%)
    ppermute x1, waiting for transfers between devices, gather_rows_over_groups(): other_y = lax.ppermute(zfull, 'yh', [(0, 1), (1, 0)])  40.4 us
    unnamed x4, waiting for transfers between devices  37.9 us
    ppermute x7, starting transfers between devices, gather_rows_over_groups(): got.append(lax.ppermute(block, 'z', [(i, (i + k) % nz) for i in range(nz)]))  17.7 us
    unnamed x35, local copies, waits for them, and re-layouts  13.3 us
    ppermute x7, starting transfers between devices, gather_rows_over_heads(): got.append(lax.ppermute(mine, T, [(i, (i + k) % nt) for i in range(nt)]))  10.7 us
    all_to_all x1, waiting for transfers between devices, place_cache_rows(): lax.all_to_all(send_rows, G, split_axis=0, concat_axis=0, tiled=True)  10.3 us
    all_to_all x1, starting transfers between devices, place_cache_rows(): lax.all_to_all(send_rows, G, split_axis=0, concat_axis=0, tiled=True)  9.77 us
    all_to_all x1, starting transfers between devices, place_cache_rows(): lax.all_to_all(send_slots, G, split_axis=0, concat_axis=0, tiled=True)  8.78 us
  transfers between devices with their start and end apart: 25, of which 7 were waited for; matrix products, arithmetic and copies ran while one was open for 26% of the time, Pallas kernels for 0%

profile of v3, /device:TPU:32, one launch (start us, length us, event | category | flops | bytes accessed | tf_op | source)
XLA Modules:
  0.0 251.0 jit_solution(4576907844648661248)
XLA Ops:
  7.2 0.8 pad_maximum_fusion.3
  8.0 1.9 collective-permute-start
  10.0 4.5 %collective-permute-start.1 = (bf16[48,320]{1,0:T(8,128)(2,1)S(1)}, bf16[48,320]{1,0:T(8,128)(2,1)S(1)}, u32[]{:S(2)}, u32[]{:S(2)}) collective-permute-start(bf16[48,320]{1,0:T(8,128)(2,1)S(1)} %pad_maximum_fusion.3), channel_id=1, source_target_pairs={{0,64},{32,96},{64,128},{96,160},{128,192},{160,224},{192,0},{224,... | collective-permute-start | bytes 92168 | tf_op jit(solution)/shard_map/ppermute | solution.py:78
  14.5 1.9 collective-permute-start.2
  16.4 1.4 collective-permute-start.3
  17.8 0.7 reshape.481
  19.3 1.7 pad_maximum_fusion.1
  21.1 0.8 bitcast_dynamic-update-slice_fusion.15
  22.0 0.7 convert_element_type.66
  22.7 0.9 multiply_cosine_fusion
  23.7 1.7 bitcast_dynamic-update-slice_fusion.7
  26.0 0.7 pad_add_fusion.1
  27.0 3.1 %collective-permute-start.4 = (bf16[48,320]{1,0:T(8,128)(2,1)S(1)}, bf16[48,320]{1,0:T(8,128)(2,1)S(1)}, u32[]{:S(2)}, u32[]{:S(2)}) collective-permute-start(bf16[48,320]{1,0:T(8,128)(2,1)S(1)} %pad_maximum_fusion.3), channel_id=1, source_target_pairs={{0,160},{32,192},{64,224},{96,0},{128,32},{160,64},{192,96},{224,1... | collective-permute-start | bytes 92168 | tf_op jit(solution)/shard_map/ppermute | solution.py:78
  30.1 0.7 pad_add_fusion
  30.8 1.5 compare_and_fusion
  32.4 2.5 collective-permute-start.5
  34.9 2.3 collective-permute-start.6
  37.2 1.6 collective-permute-start.12
  38.7 2.8 %collective-permute-start.13 = (bf16[96,1536]{1,0:T(8,128)(2,1)S(1)}, bf16[96,1536]{1,0:T(8,128)(2,1)S(1)}, u32[]{:S(2)}, u32[]{:S(2)}) collective-permute-start(bf16[96,1536]{1,0:T(8,128)(2,1)S(1)} %get-tuple-element.57), channel_id=1, source_target_pairs={{0,2},{1,3},{2,4},{3,5},{4,6},{5,7},{6,0},{7,1},{8,10},{9,11},{10,... | collective-permute-start | bytes 884744 | tf_op jit(solution)/shard_map/ppermute | solution.py:118
  41.6 2.5 %collective-permute-start.14 = (bf16[96,1536]{1,0:T(8,128)(2,1)S(1)}, bf16[96,1536]{1,0:T(8,128)(2,1)S(1)}, u32[]{:S(2)}, u32[]{:S(2)}) collective-permute-start(bf16[96,1536]{1,0:T(8,128)(2,1)S(1)} %get-tuple-element.57), channel_id=1, source_target_pairs={{0,3},{1,4},{2,5},{3,6},{4,7},{5,0},{6,1},{7,2},{8,11},{9,12},{10,... | collective-permute-start | bytes 884744 | tf_op jit(solution)/shard_map/ppermute | solution.py:118
  45.4 3.3 %collective-permute-start.7 = (bf16[8,48,320]{2,1,0:T(8,128)(2,1)S(1)}, bf16[8,48,320]{2,1,0:T(8,128)(2,1)S(1)}, u32[]{:S(2)}, u32[]{:S(2)}) collective-permute-start(bf16[8,48,320]{2,1,0:T(8,128)(2,1)S(1)} %broadcast_select_fusion.1), channel_id=1, source_target_pairs={{0,16},{16,0},{1,17},{17,1},{2,18},{18,2},{3,19},{19,3},{4,20},{20... | collective-permute-start | bytes 737288 | tf_op jit(solution)/shard_map/ppermute | solution.py:82
  48.9 40.4 %collective-permute-done.7 = bf16[8,48,320]{2,1,0:T(8,128)(2,1)S(1)} collective-permute-done((bf16[8,48,320]{2,1,0:T(8,128)(2,1)S(1)}, bf16[8,48,320]{2,1,0:T(8,128)(2,1)S(1)}, u32[]{:S(2)}, u32[]{:S(2)}) %collective-permute-start.7) | collective-permute-done | bytes 245792 | tf_op jit(solution)/shard_map/ppermute | solution.py:82
  89.3 1.0 maximum_select_fusion.3
  90.5 0.7 bitcast_dynamic-update-slice_fusion.6
  91.3 3.2 %collective-permute-start.18 = (bf16[96,1536]{1,0:T(8,128)(2,1)S(1)}, bf16[96,1536]{1,0:T(8,128)(2,1)S(1)}, u32[]{:S(2)}, u32[]{:S(2)}) collective-permute-start(bf16[96,1536]{1,0:T(8,128)(2,1)S(1)} %get-tuple-element.57), channel_id=1, source_target_pairs={{0,7},{1,0},{2,1},{3,2},{4,3},{5,4},{6,5},{7,6},{8,15},{9,8},{10,9... | collective-permute-start | bytes 884744 | tf_op jit(solution)/shard_map/ppermute | solution.py:118
  94.5 0.7 bitcast_dynamic-update-slice_fusion.5
  95.2 0.8 bitcast_dynamic-update-slice_fusion.4
  96.0 1.7 bitcast_dynamic-update-slice_fusion.3
  97.7 8.0 %collective-permute-done.16 = bf16[96,1536]{1,0:T(8,128)(2,1)S(1)} collective-permute-done((bf16[96,1536]{1,0:T(8,128)(2,1)S(1)}, bf16[96,1536]{1,0:T(8,128)(2,1)S(1)}, u32[]{:S(2)}, u32[]{:S(2)}) %collective-permute-start.16) | collective-permute-done | bytes 294944 | tf_op jit(solution)/shard_map/ppermute | solution.py:118
  105.7 0.7 bitcast_dynamic-update-slice_fusion.2
  106.5 0.7 bitcast_dynamic-update-slice_fusion.1
  107.6 0.7 bitcast_dynamic-update-slice_fusion
  108.3 2.4 gather_fusion.3
  110.7 1.7 broadcast_select_fusion
  112.4 1.7 fusion.18
  114.1 1.1 copy.53
  115.2 2.7 %slice.97 = bf16[512,1536]{0,1:T(8,128)(2,1)} slice(bf16[520,1536]{0,1:T(8,128)(2,1)} %all-gather.3.cloned.1.call-done), slice={[0:512], [0:1536]} | slice | bytes 3145728 | tf_op jit(solution)/shard_map/slice | solution.py:149
  117.9 2.6 %copy.63 = bf16[512,1536]{1,0:T(8,128)(2,1)} copy(bf16[512,1536]{0,1:T(8,128)(2,1)} %slice.97) | data formatting | bytes 3145728
  120.5 1.9 fusion.5
  122.5 1.6 convert_reduce_fusion
  124.1 1.9 fusion.22
  126.0 2.1 convolution_bitcast_fusion.1
  128.5 0.8 collective-permute-start.9
  129.4 0.9 collective-permute-done.9
  130.3 1.3 fusion.1
  131.6 1.4 fusion
  133.0 2.7 %fusion.19 = bf16[64,3,512]{2,0,1:T(8,128)(2,1)} fusion(f32[3,512]{1,0:T(4,128)S(1)} %fusion, f32[3,512]{1,0:T(4,128)S(1)} %get-tuple-element.64, f32[1024,512,3]{1,0,2:T(8,128)S(1)} %get-tuple-element.65, pred[512,1024]{0,1:T(8,128)(4,1)S(1)} %compare_and_fusion, bf16[1024,1,128]{0,2,1:T(8,128)(2,1)S(1)} %pad_maximum_fusion), kind=kOutput, calls=%fused_computation.38 | convolution fusion | flops 209289216 | bytes 7159808 | tf_op jit(solution)/shard_map/grqk,kgd->qgrd/dot_general | solution.py:52
  135.9 1.8 bitcast_select_fusion.1
  137.7 3.8 %sort.17 = (s32[512]{0:T(512)}, s32[512]{0:T(512)S(1)}) sort(s32[512]{0:T(512)S(1)} %fusion.43, s32[512]{0:T(512)S(1)} %iota.36), dimensions={0}, to_apply=%region_3.4 | sort | flops 4608 | bytes 8192 | tf_op jit(solution)/shard_map/jit(argsort)/sort | solution.py:96
  141.5 3.5 %gather_fusion.1 = s32[512]{0:T(512)S(1)} fusion(s32[512]{0:T(512)S(1)} %copy-done, s32[1024]{0:T(1024)S(1)} %pad_clamp_fusion.1), kind=kCustom, calls=%fused_computation.1 | custom fusion | bytes 6144 | tf_op jit(solution)/shard_map/gather | solution.py:98
  145.0 0.7 all_to_all.9
  145.7 8.8 %all-to-all-start = ((s32[32,1,16]{2,1,0:T(1,128)}), s32[32,1,16]{2,1,0:T(1,128)S(1)}, u32[]{:S(2)}, u32[]{:S(2)}) async-start(s32[32,1,16]{2,1,0:T(1,128)} %bitcast.29), calls=%async_computation | async-start | bytes 32768 | tf_op jit(solution)/shard_map/all_to_all | solution.py:101
  154.5 6.9 %maximum_select_fusion = bf16[8,2,96,1536]{3,2,1,0:T(8,128)(2,1)} fusion(bf16[8,1,96,1536]{3,2,1,0:T(8,128)(2,1)} %bitcast.47, bf16[8,1,96,1536]{3,2,1,0:T(8,128)(2,1)} %bitcast_select_fusion.1, pred[]{:T(512)S(6)} %eq.36), kind=kLoop, calls=%fused_computation.14 | loop fusion | flops 7077888 | bytes 9437185 | tf_op jit(solution)/shard_map/jit(_where)/select_n | solution.py:122
  161.5 1.9 gather_fusion.2
  163.4 9.8 %all-to-all-start.1 = ((bf16[32,16,1,128]{3,1,2,0:T(8,128)(2,1)}), bf16[32,16,1,128]{3,1,2,0:T(8,128)(2,1)S(1)}, u32[]{:S(2)}, u32[]{:S(2)}) async-start(bf16[32,16,1,128]{3,1,2,0:T(8,128)(2,1)} %bitcast.33), calls=%async_computation.1 | async-start | bytes 262144 | tf_op jit(solution)/shard_map/all_to_all | solution.py:100
  173.4 10.3 %all-to-all-done.1 = bf16[32,16,1,128]{3,1,2,0:T(8,128)(2,1)S(1)} async-done(((bf16[32,16,1,128]{3,1,2,0:T(8,128)(2,1)}), bf16[32,16,1,128]{3,1,2,0:T(8,128)(2,1)S(1)}, u32[]{:S(2)}, u32[]{:S(2)}) %all-to-all-start.1) | async-done | bytes 131104 | tf_op jit(solution)/shard_map/all_to_all | solution.py:100
  183.7 2.4 scatter_custom_fusion
  186.0 5.7 %fusion.2 = (f32[512]{0:T(512)S(1)}, bf16[512,1536]{1,0:T(8,128)(2,1)S(1)}) fusion(bf16[512,1536]{0,1:T(8,128)(2,1)} %all-gather.5.cloned.1.call-done, bf16[1536,1536]{1,0:T(8,128)(2,1)} %bitcast.114, bf16[512,1536]{1,0:T(8,128)(2,1)S(1)} %copy-done.2), kind=kOutput, calls=%fused_computation.17 | convolution fusion | flops 2420637184 | bytes 9439232 | tf_op jit(solution)/shard_map/dot_general | solution.py:186
  191.8 7.1 %convolution_bitcast_fusion = f32[5,512,512]{2,1,0:T(8,128)S(1)} fusion(bf16[5,1536,512]{2,1,0:T(8,128)(2,1)} %param.27, bf16[512,1536]{1,0:T(8,128)(2,1)S(1)} %get-tuple-element.67, f32[1536]{0:T(1024)S(1)} %get-tuple-element.54, f32[512]{0:T(512)S(1)} %add_rsqrt_fusion), kind=kOutput, calls=%fused_computation.28 | convolution fusion | flops 4029677568 | bytes 14688256 | tf_op jit(solution)/shard_map/td,edf->etf/dot_general | solution.py:64
  198.9 3.5 %multiply_reduce_fusion = bf16[512,1536]{1,0:T(8,128)(2,1)S(1)} fusion(bf16[5,256,1536]{2,1,0:T(8,128)(2,1)S(1)} %copy-done.8, f32[5,512]{1,0:T(8,128)S(1)} %bitcast.127, f32[5,512,512]{2,1,0:T(8,128)S(1)} %convolution_bitcast_fusion), kind=kOutput, calls=%fused_computation.5 | convolution fusion | flops 2024275968 | bytes 10758144 | tf_op jit(solution)/shard_map/etf,efd->etd/dot_general | solution.py:68
  202.3 1.6 copy.61
  204.6 37.8 %reduce-scatter.4.cloned.1.call-done = bf16[192,512]{1,0:T(8,128)(2,1)} async-done(((bf16[1536,512]{1,0:T(8,128)(2,1)}), bf16[192,512]{1,0:T(8,128)(2,1)}) %reduce-scatter.4.cloned.1.call-update) | async-done | bytes 196624
  242.4 1.1 copy.62
  243.6 0.8 copy.59
  (93 shorter events, 5.9 us)
Async XLA Ops:
  7.2 108.0 %all-gather.3.cloned.1.call-start = ((), (), s32[]{:S(2)}) async-start(), calls=%async_computation.3 | async-start | bytes 2211840 | tf_op jit(solution)/shard_map/all_gather | solution.py:148
  8.0 24.3 %collective-permute-start = (bf16[48,320]{1,0:T(8,128)(2,1)S(1)}, bf16[48,320]{1,0:T(8,128)(2,1)S(1)}, u32[]{:S(2)}, u32[]{:S(2)}) collective-permute-start(bf16[48,320]{1,0:T(8,128)(2,1)S(1)} %pad_maximum_fusion.3), channel_id=1, source_target_pairs={{0,32},{32,64},{64,96},{96,128},{128,160},{160,192},{192,224},{224... | collective-permute-start | bytes 92168 | tf_op jit(solution)/shard_map/ppermute | solution.py:78
  10.0 24.9 %collective-permute-start.1 = (bf16[48,320]{1,0:T(8,128)(2,1)S(1)}, bf16[48,320]{1,0:T(8,128)(2,1)S(1)}, u32[]{:S(2)}, u32[]{:S(2)}) collective-permute-start(bf16[48,320]{1,0:T(8,128)(2,1)S(1)} %pad_maximum_fusion.3), channel_id=1, source_target_pairs={{0,64},{32,96},{64,128},{96,160},{128,192},{160,224},{192,0},{224,... | collective-permute-start | bytes 92168 | tf_op jit(solution)/shard_map/ppermute | solution.py:78
  14.5 22.7 %collective-permute-start.2 = (bf16[48,320]{1,0:T(8,128)(2,1)S(1)}, bf16[48,320]{1,0:T(8,128)(2,1)S(1)}, u32[]{:S(2)}, u32[]{:S(2)}) collective-permute-start(bf16[48,320]{1,0:T(8,128)(2,1)S(1)} %pad_maximum_fusion.3), channel_id=1, source_target_pairs={{0,96},{32,128},{64,160},{96,192},{128,224},{160,0},{192,32},{224,... | collective-permute-start | bytes 92168 | tf_op jit(solution)/shard_map/ppermute | solution.py:78
  16.4 22.3 %collective-permute-start.3 = (bf16[48,320]{1,0:T(8,128)(2,1)S(1)}, bf16[48,320]{1,0:T(8,128)(2,1)S(1)}, u32[]{:S(2)}, u32[]{:S(2)}) collective-permute-start(bf16[48,320]{1,0:T(8,128)(2,1)S(1)} %pad_maximum_fusion.3), channel_id=1, source_target_pairs={{0,128},{32,160},{64,192},{96,224},{128,0},{160,32},{192,64},{224,... | collective-permute-start | bytes 92168 | tf_op jit(solution)/shard_map/ppermute | solution.py:78
  17.8 7.6 %collective-permute-start.11 = (s32[512]{0:T(512)}, s32[512]{0:T(512)S(1)}, u32[]{:S(2)}, u32[]{:S(2)}) collective-permute-start(s32[512]{0:T(512)} %param.19), channel_id=1, source_target_pairs={{0,8},{8,0},{1,9},{9,1},{2,10},{10,2},{3,11},{11,3},{4,12},{12,4},... | collective-permute-start | bytes 6152 | tf_op jit(solution)/shard_map/ppermute | solution.py:171
  21.0 165.0 %all-gather.5.cloned.1.call-start = ((), (), s32[]{:S(2)}) async-start(), calls=%async_computation.4 | async-start | bytes 1769472 | tf_op jit(solution)/shard_map/all_gather | solution.py:183
  22.0 10.4 %copy-start.6 = (f32[32]{0:T(128)}, f32[32]{0:T(128)S(1)}, u32[]{:S(2)}) copy-start(f32[32]{0:T(128)S(1)} %multiply_power_fusion) | copy-start | bytes 388
  25.4 1.6 collective-permute-start.10
  27.0 14.5 %collective-permute-start.4 = (bf16[48,320]{1,0:T(8,128)(2,1)S(1)}, bf16[48,320]{1,0:T(8,128)(2,1)S(1)}, u32[]{:S(2)}, u32[]{:S(2)}) collective-permute-start(bf16[48,320]{1,0:T(8,128)(2,1)S(1)} %pad_maximum_fusion.3), channel_id=1, source_target_pairs={{0,160},{32,192},{64,224},{96,0},{128,32},{160,64},{192,96},{224,1... | collective-permute-start | bytes 92168 | tf_op jit(solution)/shard_map/ppermute | solution.py:78
  32.4 11.7 %collective-permute-start.5 = (bf16[48,320]{1,0:T(8,128)(2,1)S(1)}, bf16[48,320]{1,0:T(8,128)(2,1)S(1)}, u32[]{:S(2)}, u32[]{:S(2)}) collective-permute-start(bf16[48,320]{1,0:T(8,128)(2,1)S(1)} %pad_maximum_fusion.3), channel_id=1, source_target_pairs={{0,192},{32,224},{64,0},{96,32},{128,64},{160,96},{192,128},{224,1... | collective-permute-start | bytes 92168 | tf_op jit(solution)/shard_map/ppermute | solution.py:78
  34.9 9.8 %collective-permute-start.6 = (bf16[48,320]{1,0:T(8,128)(2,1)S(1)}, bf16[48,320]{1,0:T(8,128)(2,1)S(1)}, u32[]{:S(2)}, u32[]{:S(2)}) collective-permute-start(bf16[48,320]{1,0:T(8,128)(2,1)S(1)} %pad_maximum_fusion.3), channel_id=1, source_target_pairs={{0,224},{32,0},{64,32},{96,64},{128,96},{160,128},{192,160},{224,1... | collective-permute-start | bytes 92168 | tf_op jit(solution)/shard_map/ppermute | solution.py:78
  37.2 53.3 %collective-permute-start.12 = (bf16[96,1536]{1,0:T(8,128)(2,1)S(1)}, bf16[96,1536]{1,0:T(8,128)(2,1)S(1)}, u32[]{:S(2)}, u32[]{:S(2)}) collective-permute-start(bf16[96,1536]{1,0:T(8,128)(2,1)S(1)} %get-tuple-element.57), channel_id=1, source_target_pairs={{0,1},{1,2},{2,3},{3,4},{4,5},{5,6},{6,7},{7,0},{8,9},{9,10},{10,1... | collective-permute-start | bytes 884744 | tf_op jit(solution)/shard_map/ppermute | solution.py:118
  38.7 52.5 %collective-permute-start.13 = (bf16[96,1536]{1,0:T(8,128)(2,1)S(1)}, bf16[96,1536]{1,0:T(8,128)(2,1)S(1)}, u32[]{:S(2)}, u32[]{:S(2)}) collective-permute-start(bf16[96,1536]{1,0:T(8,128)(2,1)S(1)} %get-tuple-element.57), channel_id=1, source_target_pairs={{0,2},{1,3},{2,4},{3,5},{4,6},{5,7},{6,0},{7,1},{8,10},{9,11},{10,... | collective-permute-start | bytes 884744 | tf_op jit(solution)/shard_map/ppermute | solution.py:118
  41.6 53.7 %collective-permute-start.14 = (bf16[96,1536]{1,0:T(8,128)(2,1)S(1)}, bf16[96,1536]{1,0:T(8,128)(2,1)S(1)}, u32[]{:S(2)}, u32[]{:S(2)}) collective-permute-start(bf16[96,1536]{1,0:T(8,128)(2,1)S(1)} %get-tuple-element.57), channel_id=1, source_target_pairs={{0,3},{1,4},{2,5},{3,6},{4,7},{5,0},{6,1},{7,2},{8,11},{9,12},{10,... | collective-permute-start | bytes 884744 | tf_op jit(solution)/shard_map/ppermute | solution.py:118
  44.1 51.9 %collective-permute-start.15 = (bf16[96,1536]{1,0:T(8,128)(2,1)S(1)}, bf16[96,1536]{1,0:T(8,128)(2,1)}, u32[]{:S(2)}, u32[]{:S(2)}) collective-permute-start(bf16[96,1536]{1,0:T(8,128)(2,1)S(1)} %get-tuple-element.57), channel_id=1, source_target_pairs={{0,4},{1,5},{2,6},{3,7},{4,0},{5,1},{6,2},{7,3},{8,12},{9,13},{10,... | collective-permute-start | bytes 884744 | tf_op jit(solution)/shard_map/ppermute | solution.py:118
  45.4 43.9 %collective-permute-start.7 = (bf16[8,48,320]{2,1,0:T(8,128)(2,1)S(1)}, bf16[8,48,320]{2,1,0:T(8,128)(2,1)S(1)}, u32[]{:S(2)}, u32[]{:S(2)}) collective-permute-start(bf16[8,48,320]{2,1,0:T(8,128)(2,1)S(1)} %broadcast_select_fusion.1), channel_id=1, source_target_pairs={{0,16},{16,0},{1,17},{17,1},{2,18},{18,2},{3,19},{19,3},{4,20},{20... | collective-permute-start | bytes 737288 | tf_op jit(solution)/shard_map/ppermute | solution.py:82
  89.3 16.5 %collective-permute-start.16 = (bf16[96,1536]{1,0:T(8,128)(2,1)S(1)}, bf16[96,1536]{1,0:T(8,128)(2,1)S(1)}, u32[]{:S(2)}, u32[]{:S(2)}) collective-permute-start(bf16[96,1536]{1,0:T(8,128)(2,1)S(1)} %get-tuple-element.57), channel_id=1, source_target_pairs={{0,5},{1,6},{2,7},{3,0},{4,1},{5,2},{6,3},{7,4},{8,13},{9,14},{10,... | collective-permute-start | bytes 884744 | tf_op jit(solution)/shard_map/ppermute | solution.py:118
  90.5 16.0 %collective-permute-start.17 = (bf16[96,1536]{1,0:T(8,128)(2,1)S(1)}, bf16[96,1536]{1,0:T(8,128)(2,1)S(1)}, u32[]{:S(2)}, u32[]{:S(2)}) collective-permute-start(bf16[96,1536]{1,0:T(8,128)(2,1)S(1)} %get-tuple-element.57), channel_id=1, source_target_pairs={{0,6},{1,7},{2,0},{3,1},{4,2},{5,3},{6,4},{7,5},{8,14},{9,15},{10,... | collective-permute-start | bytes 884744 | tf_op jit(solution)/shard_map/ppermute | solution.py:118
  91.3 16.3 %collective-permute-start.18 = (bf16[96,1536]{1,0:T(8,128)(2,1)S(1)}, bf16[96,1536]{1,0:T(8,128)(2,1)S(1)}, u32[]{:S(2)}, u32[]{:S(2)}) collective-permute-start(bf16[96,1536]{1,0:T(8,128)(2,1)S(1)} %get-tuple-element.57), channel_id=1, source_target_pairs={{0,7},{1,0},{2,1},{3,2},{4,3},{5,4},{6,5},{7,6},{8,15},{9,8},{10,9... | collective-permute-start | bytes 884744 | tf_op jit(solution)/shard_map/ppermute | solution.py:118
  95.2 17.2 %collective-permute-start.8 = (bf16[2,8,48,320]{3,2,1,0:T(8,128)(2,1)}, bf16[2,8,48,320]{3,2,1,0:T(8,128)(2,1)}, u32[]{:S(2)}, u32[]{:S(2)}) collective-permute-start(bf16[2,8,48,320]{3,2,1,0:T(8,128)(2,1)} %maximum_select_fusion.3), channel_id=1, source_target_pairs={{0,8},{8,0},{1,9},{9,1},{2,10},{10,2},{3,11},{11,3},{4,12},{12,4},... | collective-permute-start | bytes 1474568 | tf_op jit(solution)/shard_map/ppermute | solution.py:85
  112.4 42.1 %collective-permute-start.19 = (bf16[8,96,1536]{2,1,0:T(8,128)(2,1)}, bf16[8,96,1536]{2,1,0:T(8,128)(2,1)}, u32[]{:S(2)}, u32[]{:S(2)}) collective-permute-start(bf16[8,96,1536]{2,1,0:T(8,128)(2,1)} %broadcast_select_fusion), channel_id=1, source_target_pairs={{0,8},{8,0},{1,9},{9,1},{2,10},{10,2},{3,11},{11,3},{4,12},{12,4},... | collective-permute-start | bytes 7077896 | tf_op jit(solution)/shard_map/ppermute | solution.py:121
  120.5 3.5 %copy-start.1 = (bf16[512,1536]{1,0:T(8,128)(2,1)S(1)}, bf16[512,1536]{1,0:T(8,128)(2,1)}, u32[]{:S(2)}) copy-start(bf16[512,1536]{1,0:T(8,128)(2,1)} %copy.63) | copy-start | bytes 4718596
  126.0 2.1 copy-start.7
  126.0 3.3 %copy-start.3 = (f32[512,32]{0,1:T(8,128)S(1)}, f32[512,32]{0,1:T(8,128)}, u32[]{:S(2)}) copy-start(f32[512,32]{0,1:T(8,128)} %get-tuple-element.63) | copy-start | bytes 196612
  128.5 1.8 collective-permute-start.9
  133.0 2.8 %copy-start.4 = (f32[512,8]{0,1:T(8,128)S(1)}, f32[512,8]{0,1:T(8,128)}, u32[]{:S(2)}) copy-start(f32[512,8]{0,1:T(8,128)} %param.26) | copy-start | bytes 49156
  133.0 2.8 %copy-start.5 = (s32[512,8]{0,1:T(8,128)S(1)}, s32[512,8]{0,1:T(8,128)}, u32[]{:S(2)}) copy-start(s32[512,8]{0,1:T(8,128)} %param.25) | copy-start | bytes 49156
  135.9 1.8 copy-start
  145.7 17.7 %all-to-all-start = ((s32[32,1,16]{2,1,0:T(1,128)}), s32[32,1,16]{2,1,0:T(1,128)S(1)}, u32[]{:S(2)}, u32[]{:S(2)}) async-start(s32[32,1,16]{2,1,0:T(1,128)} %bitcast.29), calls=%async_computation | async-start | bytes 32768 | tf_op jit(solution)/shard_map/all_to_all | solution.py:101
  154.5 31.6 %copy-start.2 = (bf16[512,1536]{1,0:T(8,128)(2,1)S(1)}, bf16[512,1536]{1,0:T(8,128)(2,1)}, u32[]{:S(2)}) copy-start(bf16[512,1536]{1,0:T(8,128)(2,1)} %copy.63) | copy-start | bytes 4718596
  163.4 20.3 %all-to-all-start.1 = ((bf16[32,16,1,128]{3,1,2,0:T(8,128)(2,1)}), bf16[32,16,1,128]{3,1,2,0:T(8,128)(2,1)S(1)}, u32[]{:S(2)}, u32[]{:S(2)}) async-start(bf16[32,16,1,128]{3,1,2,0:T(8,128)(2,1)} %bitcast.33), calls=%async_computation.1 | async-start | bytes 262144 | tf_op jit(solution)/shard_map/all_to_all | solution.py:100
  173.2 69.2 %reduce-scatter.4.cloned.1.call-start = ((), (), s32[]{:S(2)}) async-start(), calls=%async_computation.5 | async-start | bytes 1769472
  191.8 7.1 %copy-start.8 = (bf16[5,256,1536]{2,1,0:T(8,128)(2,1)S(1)}, bf16[5,256,1536]{2,1,0:T(8,128)(2,1)}, u32[]{:S(2)}) copy-start(bf16[5,256,1536]{2,1,0:T(8,128)(2,1)} %param.28) | copy-start | bytes 11796484
Sparse Core Ops, SparseCore 0:
  21.2 60.6 all-gather.2
  135.9 42.7 all-gather.4
  204.1 38.2 reduce-scatter.3

commit v4 on v2

--- a/solution.py
+++ b/solution.py
@@ -162,22 +162,23 @@
     attended = mixed.reshape(tokens, heads_local * HD)
     log_sums = log_part.reshape(heads_local, tokens)
     partial_value = jnp.dot(attended, output_weight, preferred_element_type=jnp.float32)
-    partial_low, own_rows, cache_slots = lax.optimization_barrier(
-        (partial_value.astype(jnp.bfloat16), own_rows, cache_slots)
-    )
-    summed = lax.psum(partial_low, T)
+    tp_count = lax.axis_size(T)
+    value_parts = partial_value.astype(jnp.bfloat16).reshape(tokens, tp_count, width_share).transpose(1, 0, 2)
+    value_got = lax.all_to_all(value_parts, T, 0, 0, tiled=True)
+    summed_share = jnp.sum(value_got.astype(jnp.float32), axis=0)
+    residual_share = (states_in.astype(jnp.float32) + summed_share).astype(jnp.bfloat16)
+    residual_share, own_rows, cache_slots = lax.optimization_barrier((residual_share, own_rows, cache_slots))
+    residual = lax.all_gather(residual_share, T, axis=1, tiled=True)
     paged_rows = place_cache_rows(own_rows, cache_slots, group_rank)
-    summed, paged_rows = lax.optimization_barrier((summed, paged_rows))
-    residual = (states_full.astype(jnp.float32) + summed.astype(jnp.float32)).astype(jnp.bfloat16)
+    residual, paged_rows = lax.optimization_barrier((residual, paged_rows))
     normed = rms_scale(residual, gain_forward)
-    residual_share = lax.dynamic_slice_in_dim(residual, head_rank * width_share, width_share, 1)
     slot_first = head_rank // 2 * expert_gateup.shape[0]
     terms = expert_terms(
         normed, route_experts, route_weights, expert_gateup, expert_down, slot_first
     )
-    expert_share = lax.psum_scatter(
-        terms.astype(jnp.bfloat16), T, scatter_dimension=1, tiled=True
-    ).astype(jnp.float32)
+    term_parts = terms.astype(jnp.bfloat16).reshape(tokens, tp_count, width_share).transpose(1, 0, 2)
+    term_got = lax.all_to_all(term_parts, T, 0, 0, tiled=True)
+    expert_share = jnp.sum(term_got.astype(jnp.float32), axis=0)
     layer_output = (residual_share.astype(jnp.float32) + expert_share).astype(jnp.bfloat16)
     return (layer_output, paged_rows, log_sums)
 

time: 236 us -> 203 us (0.86); the launches traced: 235 us -> 200 us
  waiting for transfers between devices: 126 us -> 64.4 us
  blocking collectives: 0 us -> 25.8 us
  local copies, waits for them, and re-layouts: 19.8 us -> 14.2 us
  starting transfers between devices: 37.2 us -> 40.5 us
    unnamed x4 -> x2, waiting for transfers between devices: 42.7 us -> 0.03 us
    psum x1 -> x0, waiting for transfers between devices: 40.3 us -> none  [shards(): summed = lax.psum(partial_low, T)]
    all_to_all x0 -> x1, blocking collectives: none -> 25.8 us  [shards(): value_got = lax.all_to_all(value_parts, T, 0, 0, tiled=True)]
    all_to_all x0 -> x1, waiting for transfers between devices: none -> 20.6 us  [shards(): term_got = lax.all_to_all(term_parts, T, 0, 0, tiled=True)]
    unnamed x28 -> x26, local copies, waits for them, and re-layouts: 5.29 us -> 0.12 us
    all_to_all x0 -> x1, starting transfers between devices: none -> 3.71 us  [shards(): term_got = lax.all_to_all(term_parts, T, 0, 0, tiled=True)]
    convert_element_type x0 -> x2, local copies, waits for them, and re-layouts: none -> 3.21 us  [the longest x1 1.6 us: shards(): partial_value.astype(jnp.bfloat16).reshape(tokens, tp_count, width_share)]
    slice x1 -> x0, local copies, waits for them, and re-layouts: 2.64 us -> none  [shards(): states_full = packed_full[:tokens]]
  transfers between devices with their start and end apart: 17 -> 17, of which waited for: 10 -> 9; matrix products, arithmetic and copies ran while one was open for 10% -> 11% of each run, Pallas kernels for 0% -> 0%
where the time goes in v4:
time: 203 us; the launch traced here: 200 us
  waiting for transfers between devices  64.4 us (32%)
  starting transfers between devices  40.5 us (20%)
  blocking collectives  25.8 us (13%)
  other arithmetic  21.2 us (10%)
  matrix products  19.2 us (9%)
  between operations  14.5 us (7%)
  local copies, waits for them, and re-layouts  14.2 us (7%)
    all_to_all x1, blocking collectives, shards(): value_got = lax.all_to_all(value_parts, T, 0, 0, tiled=True)  25.8 us
    ppermute x1, waiting for transfers between devices, gather_rows_over_groups(): other_y = lax.ppermute(zfull, 'yh', [(0, 1), (1, 0)])  20.7 us
    all_to_all x1, waiting for transfers between devices, shards(): term_got = lax.all_to_all(term_parts, T, 0, 0, tiled=True)  20.6 us
    ppermute x7, starting transfers between devices, gather_rows_over_groups(): got.append(lax.ppermute(block, 'z', [(i, (i + k) % nz) for i in range(nz)]))  17.7 us
    all_to_all x1, waiting for transfers between devices, place_cache_rows(): lax.all_to_all(send_rows, G, split_axis=0, concat_axis=0, tiled=True)  10.4 us
    all_to_all x1, starting transfers between devices, place_cache_rows(): lax.all_to_all(send_slots, G, split_axis=0, concat_axis=0, tiled=True)  10.2 us
    dot_general x1, matrix products, expert_terms(): jnp.einsum('td,edf->etf', normed, gateup, preferred_element_type=jnp.floa...  8.72 us
    all_to_all x1, waiting for transfers between devices, place_cache_rows(): lax.all_to_all(send_slots, G, split_axis=0, concat_axis=0, tiled=True)  6.43 us
  transfers between devices with their start and end apart: 17, of which 9 were waited for; matrix products, arithmetic and copies ran while one was open for 11% of the time, Pallas kernels for 0%

profile of v4, /device:TPU:32, one launch (start us, length us, event | category | flops | bytes accessed | tf_op | source)
XLA Modules:
  0.0 199.9 jit_solution(4606948455053897623)
XLA Ops:
  7.2 0.9 pad_maximum_fusion.3
  8.1 1.9 collective-permute-start
  10.1 4.5 %collective-permute-start.1 = (bf16[48,320]{1,0:T(8,128)(2,1)S(1)}, bf16[48,320]{1,0:T(8,128)(2,1)S(1)}, u32[]{:S(2)}, u32[]{:S(2)}) collective-permute-start(bf16[48,320]{1,0:T(8,128)(2,1)S(1)} %pad_maximum_fusion.3), channel_id=1, source_target_pairs={{0,64},{32,96},{64,128},{96,160},{128,192},{160,224},{192,0},{224,... | collective-permute-start | bytes 92168 | tf_op jit(solution)/shard_map/ppermute | solution.py:78
  14.6 1.9 collective-permute-start.2
  16.5 1.4 collective-permute-start.3
  17.9 0.7 reshape.421
  18.6 0.7 reshape.422
  19.3 0.1 copy.40
  19.4 1.7 pad_maximum_fusion.1
  21.3 0.8 bitcast_dynamic-update-slice_fusion.7
  22.1 0.7 convert_element_type.79
  22.8 0.3 multiply_cosine_fusion
  23.2 3.2 %collective-permute-start.4 = (bf16[48,320]{1,0:T(8,128)(2,1)S(1)}, bf16[48,320]{1,0:T(8,128)(2,1)S(1)}, u32[]{:S(2)}, u32[]{:S(2)}) collective-permute-start(bf16[48,320]{1,0:T(8,128)(2,1)S(1)} %pad_maximum_fusion.3), channel_id=1, source_target_pairs={{0,160},{32,192},{64,224},{96,0},{128,32},{160,64},{192,96},{224,1... | collective-permute-start | bytes 92168 | tf_op jit(solution)/shard_map/ppermute | solution.py:78
  26.4 0.7 pad_add_fusion
  27.1 2.5 %collective-permute-start.5 = (bf16[48,320]{1,0:T(8,128)(2,1)S(1)}, bf16[48,320]{1,0:T(8,128)(2,1)S(1)}, u32[]{:S(2)}, u32[]{:S(2)}) collective-permute-start(bf16[48,320]{1,0:T(8,128)(2,1)S(1)} %pad_maximum_fusion.3), channel_id=1, source_target_pairs={{0,192},{32,224},{64,0},{96,32},{128,64},{160,96},{192,128},{224,1... | collective-permute-start | bytes 92168 | tf_op jit(solution)/shard_map/ppermute | solution.py:78
  29.5 2.3 %collective-permute-start.6 = (bf16[48,320]{1,0:T(8,128)(2,1)S(1)}, bf16[48,320]{1,0:T(8,128)(2,1)S(1)}, u32[]{:S(2)}, u32[]{:S(2)}) collective-permute-start(bf16[48,320]{1,0:T(8,128)(2,1)S(1)} %pad_maximum_fusion.3), channel_id=1, source_target_pairs={{0,224},{32,0},{64,32},{96,64},{128,96},{160,128},{192,160},{224,1... | collective-permute-start | bytes 92168 | tf_op jit(solution)/shard_map/ppermute | solution.py:78
  32.1 1.5 collective-permute-done.6
  33.6 0.6 gather_fusion
  34.2 0.1 broadcast_select_fusion
  34.3 3.3 %collective-permute-start.7 = (bf16[8,48,320]{2,1,0:T(8,128)(2,1)S(1)}, bf16[8,48,320]{2,1,0:T(8,128)(2,1)S(1)}, u32[]{:S(2)}, u32[]{:S(2)}) collective-permute-start(bf16[8,48,320]{2,1,0:T(8,128)(2,1)S(1)} %broadcast_select_fusion), channel_id=1, source_target_pairs={{0,16},{16,0},{1,17},{17,1},{2,18},{18,2},{3,19},{19,3},{4,20},{20... | collective-permute-start | bytes 737288 | tf_op jit(solution)/shard_map/ppermute | solution.py:82
  37.6 0.7 pad_add_fusion.1
  38.4 20.7 %collective-permute-done.7 = bf16[8,48,320]{2,1,0:T(8,128)(2,1)S(1)} collective-permute-done((bf16[8,48,320]{2,1,0:T(8,128)(2,1)S(1)}, bf16[8,48,320]{2,1,0:T(8,128)(2,1)S(1)}, u32[]{:S(2)}, u32[]{:S(2)}) %collective-permute-start.7) | collective-permute-done | bytes 245792 | tf_op jit(solution)/shard_map/ppermute | solution.py:82
  59.1 0.2 maximum_select_fusion.2
  59.4 0.8 compare_and_fusion
  60.2 0.1 fusion.55
  60.4 0.2 maximum_select_fusion.1
  60.5 0.8 collective-permute-done.8
  61.4 0.4 fusion.17
  61.7 0.1 copy.41
  61.9 3.4 %all-gather.3.cloned.1.call-done = bf16[520,1536]{0,1:T(8,128)(2,1)} async-done(((bf16[520,192]{0,1:T(8,128)(2,1)}), bf16[520,1536]{0,1:T(8,128)(2,1)}) %all-gather.3.cloned.1.call-update) | async-done | bytes 1597456 | tf_op jit(solution)/shard_map/all_gather | solution.py:131
  65.3 1.8 fusion.2
  67.1 1.7 convert_reduce_fusion.2
  68.8 2.3 %convolution_bitcast_fusion.1 = f32[512,1,128]{0,2,1:T(8,128)S(1)} fusion(bf16[1536,320]{1,0:T(8,128)(2,1)S(1)} %bitcast.94, f32[1536]{0:T(1024)S(1)} %get-tuple-element.40, f32[512]{0:T(512)S(1)} %add_rsqrt_fusion.1, bf16[520,1536]{0,1:T(8,128)(2,1)} %all-gather.3.cloned.1.call-done), kind=kOutput, calls=%fused_computation.36 | convolution fusion | flops 204472320 | bytes 2238464 | tf_op jit(solution)/shard_map/dot_general | solution.py:147
  71.1 0.3 fusion.35
  71.5 0.3 collective-permute-start.9
  71.8 0.8 fusion.21
  72.7 0.4 collective-permute-done.9
  73.1 1.3 fusion.1
  74.4 1.4 fusion
  75.8 2.0 %fusion.18 = bf16[64,3,512]{2,0,1:T(8,128)(2,1)S(1)} fusion(f32[3,512]{1,0:T(4,128)S(1)} %fusion, f32[3,512]{1,0:T(4,128)S(1)} %get-tuple-element.47, f32[1024,512,3]{1,0,2:T(8,128)S(1)} %get-tuple-element.48, pred[512,1024]{0,1:T(8,128)(4,1)S(1)} %compare_and_fusion, bf16[1024,1,128]{0,2,1:T(8,128)(2,1)S(1)} %pad_maximum_fusion), kind=kOutput, calls=%fused_computation.35 | convolution fusion | flops 209289216 | bytes 7159808 | tf_op jit(solution)/shard_map/grqk,kgd->qgrd/dot_general | solution.py:52
  77.8 0.6 convolution_convert_fusion
  78.4 1.6 copy.43
  80.0 25.8 %all_to_all.24 = bf16[8,512,192]{1,2,0:T(8,128)(2,1)S(1)} all-to-all(bf16[8,512,192]{1,2,0:T(8,128)(2,1)} %bitcast.93), channel_id=1, replica_groups=mesh['z'=8,'yh'=2,'c'=2,'yl'=2,'x'=4] {'yl','x'}, dimensions={0} | all-to-all | bytes 3145728 | tf_op jit(solution)/shard_map/all_to_all | solution.py:167
  105.8 0.2 convert_reduce_fusion.1
  106.1 0.7 add_convert_fusion.1
  106.9 3.8 %sort.17 = (s32[512]{0:T(512)}, s32[512]{0:T(512)S(1)}) sort(s32[512]{0:T(512)S(1)} %fusion.42, s32[512]{0:T(512)S(1)} %iota.31), dimensions={0}, to_apply=%region_5.6 | sort | flops 4608 | bytes 8192 | tf_op jit(solution)/shard_map/jit(argsort)/sort | solution.py:96
  110.6 3.5 %gather_fusion.1 = s32[512]{0:T(512)S(1)} fusion(s32[512]{0:T(512)S(1)} %copy-done.1, s32[1024]{0:T(1024)S(1)} %pad_clamp_fusion), kind=kCustom, calls=%fused_computation.1 | custom fusion | bytes 6144 | tf_op jit(solution)/shard_map/gather | solution.py:98
  114.1 0.7 all_to_all.16
  114.8 10.2 %all-to-all-start.1 = ((s32[32,1,16]{2,1,0:T(1,128)}), s32[32,1,16]{2,1,0:T(1,128)S(1)}, u32[]{:S(2)}, u32[]{:S(2)}) async-start(s32[32,1,16]{2,1,0:T(1,128)} %bitcast.32), calls=%async_computation.1 | async-start | bytes 32768 | tf_op jit(solution)/shard_map/all_to_all | solution.py:101
  125.2 0.1 copy.45
  125.3 1.9 gather_fusion.2
  127.3 6.4 %all-to-all-done.1 = s32[32,1,16]{2,1,0:T(1,128)S(1)} async-done(((s32[32,1,16]{2,1,0:T(1,128)}), s32[32,1,16]{2,1,0:T(1,128)S(1)}, u32[]{:S(2)}, u32[]{:S(2)}) %all-to-all-start.1) | async-done | bytes 2080 | tf_op jit(solution)/shard_map/all_to_all | solution.py:101
  133.7 4.9 %all-to-all-start.2 = ((bf16[32,16,1,128]{3,1,2,0:T(8,128)(2,1)}), bf16[32,16,1,128]{3,1,2,0:T(8,128)(2,1)S(1)}, u32[]{:S(2)}, u32[]{:S(2)}) async-start(bf16[32,16,1,128]{3,1,2,0:T(8,128)(2,1)} %bitcast.36), calls=%async_computation.2 | async-start | bytes 262144 | tf_op jit(solution)/shard_map/all_to_all | solution.py:100
  138.8 10.4 %all-to-all-done.2 = bf16[32,16,1,128]{3,1,2,0:T(8,128)(2,1)S(1)} async-done(((bf16[32,16,1,128]{3,1,2,0:T(8,128)(2,1)}), bf16[32,16,1,128]{3,1,2,0:T(8,128)(2,1)S(1)}, u32[]{:S(2)}, u32[]{:S(2)}) %all-to-all-start.2) | async-done | bytes 131104 | tf_op jit(solution)/shard_map/all_to_all | solution.py:100
  149.2 2.4 %scatter_custom_fusion = bf16[512,128]{1,0:T(8,128)(2,1)} fusion(s32[512]{0:T(512)S(1)} %bitcast.107, bf16[512,128]{1,0:T(8,128)(2,1)S(1)} %bitcast.103, bf16[]{:T(256)} %constant.137.clone.1), kind=kCustom, calls=%fused_computation.73 | custom fusion | bytes 131074 | tf_op jit(solution)/shard_map/scatter | solution.py:104
  151.5 1.8 fusion.5
  153.4 8.7 %convolution_bitcast_fusion = f32[5,512,512]{2,1,0:T(8,128)S(1)} fusion(bf16[5,1536,512]{2,1,0:T(8,128)(2,1)} %param.27, bf16[512,1536]{0,1:T(8,128)(2,1)} %all-gather.5.cloned.1.call-done, f32[1536]{0:T(1024)S(1)} %get-tuple-element.39, f32[512]{0:T(512)S(1)} %add_rsqrt_fusion), kind=kOutput, calls=%fused_computation.27 | convolution fusion | flops 4029677568 | bytes 14688256 | tf_op jit(solution)/shard_map/td,edf->etf/dot_general | solution.py:64
  162.1 3.5 %multiply_reduce_fusion = bf16[512,1536]{1,0:T(8,128)(2,1)S(1)} fusion(bf16[5,256,1536]{2,1,0:T(8,128)(2,1)S(1)} %copy-done.9, f32[5,512]{1,0:T(8,128)S(1)} %bitcast.106, f32[5,512,512]{2,1,0:T(8,128)S(1)} %convolution_bitcast_fusion), kind=kOutput, calls=%fused_computation.4 | convolution fusion | flops 2024275968 | bytes 10758144 | tf_op jit(solution)/shard_map/etf,efd->etd/dot_general | solution.py:68
  165.6 1.6 copy.48
  167.2 3.7 %all-to-all-start.3 = ((bf16[8,512,192]{1,2,0:T(8,128)(2,1)}), bf16[8,512,192]{1,2,0:T(8,128)(2,1)S(1)}, u32[]{:S(2)}, u32[]{:S(2)}) async-start(bf16[8,512,192]{1,2,0:T(8,128)(2,1)} %bitcast.42), calls=%async_computation.3 | async-start | bytes 3145728 | tf_op jit(solution)/shard_map/all_to_all | solution.py:180
  170.9 0.6 log_add_fusion
  171.5 20.6 %all-to-all-done.3 = bf16[8,512,192]{1,2,0:T(8,128)(2,1)S(1)} async-done(((bf16[8,512,192]{1,2,0:T(8,128)(2,1)}), bf16[8,512,192]{1,2,0:T(8,128)(2,1)S(1)}, u32[]{:S(2)}, u32[]{:S(2)}) %all-to-all-start.3) | async-done | bytes 1572896 | tf_op jit(solution)/shard_map/all_to_all | solution.py:180
  192.1 0.2 convert_reduce_fusion
  192.3 0.7 add_convert_fusion
  (65 shorter events, 1.2 us)
Async XLA Ops:
  7.2 70.7 %copy-start = (bf16[192,1536]{1,0:T(8,128)(2,1)S(1)}, bf16[192,1536]{1,0:T(8,128)(2,1)}, u32[]{:S(2)}) copy-start(bf16[192,1536]{1,0:T(8,128)(2,1)} %param.24) | copy-start | bytes 1769476
  7.2 52.2 %copy-start.8 = (s32[512]{0:T(512)S(1)}, s32[512]{0:T(512)}, u32[]{:S(2)}) copy-start(s32[512]{0:T(512)} %param.18) | copy-start | bytes 6148
  7.2 52.2 %copy-start.5 = (s32[512]{0:T(512)S(1)}, s32[512]{0:T(512)}, u32[]{:S(2)}) copy-start(s32[512]{0:T(512)} %param.19) | copy-start | bytes 6148
  7.2 58.1 %all-gather.3.cloned.1.call-start = ((), (), s32[]{:S(2)}) async-start(), calls=%async_computation.4 | async-start | bytes 2211840 | tf_op jit(solution)/shard_map/all_gather | solution.py:131
  8.1 18.9 %collective-permute-start = (bf16[48,320]{1,0:T(8,128)(2,1)S(1)}, bf16[48,320]{1,0:T(8,128)(2,1)S(1)}, u32[]{:S(2)}, u32[]{:S(2)}) collective-permute-start(bf16[48,320]{1,0:T(8,128)(2,1)S(1)} %pad_maximum_fusion.3), channel_id=1, source_target_pairs={{0,32},{32,64},{64,96},{96,128},{128,160},{160,192},{192,224},{224... | collective-permute-start | bytes 92168 | tf_op jit(solution)/shard_map/ppermute | solution.py:78
  10.1 19.5 %collective-permute-start.1 = (bf16[48,320]{1,0:T(8,128)(2,1)S(1)}, bf16[48,320]{1,0:T(8,128)(2,1)S(1)}, u32[]{:S(2)}, u32[]{:S(2)}) collective-permute-start(bf16[48,320]{1,0:T(8,128)(2,1)S(1)} %pad_maximum_fusion.3), channel_id=1, source_target_pairs={{0,64},{32,96},{64,128},{96,160},{128,192},{160,224},{192,0},{224,... | collective-permute-start | bytes 92168 | tf_op jit(solution)/shard_map/ppermute | solution.py:78
  14.6 17.3 %collective-permute-start.2 = (bf16[48,320]{1,0:T(8,128)(2,1)S(1)}, bf16[48,320]{1,0:T(8,128)(2,1)S(1)}, u32[]{:S(2)}, u32[]{:S(2)}) collective-permute-start(bf16[48,320]{1,0:T(8,128)(2,1)S(1)} %pad_maximum_fusion.3), channel_id=1, source_target_pairs={{0,96},{32,128},{64,160},{96,192},{128,224},{160,0},{192,32},{224,... | collective-permute-start | bytes 92168 | tf_op jit(solution)/shard_map/ppermute | solution.py:78
  16.5 15.5 %collective-permute-start.3 = (bf16[48,320]{1,0:T(8,128)(2,1)S(1)}, bf16[48,320]{1,0:T(8,128)(2,1)S(1)}, u32[]{:S(2)}, u32[]{:S(2)}) collective-permute-start(bf16[48,320]{1,0:T(8,128)(2,1)S(1)} %pad_maximum_fusion.3), channel_id=1, source_target_pairs={{0,128},{32,160},{64,192},{96,224},{128,0},{160,32},{192,64},{224,... | collective-permute-start | bytes 92168 | tf_op jit(solution)/shard_map/ppermute | solution.py:78
  21.1 130.4 %all-gather.5.cloned.1.call-start = ((), (), s32[]{:S(2)}) async-start(), calls=%async_computation.5 | async-start | bytes 1769472 | tf_op jit(solution)/shard_map/all_gather | solution.py:171
  21.2 2.0 %collective-permute-start.10 = (s32[512]{0:T(512)}, s32[512]{0:T(512)S(1)}, u32[]{:S(2)}, u32[]{:S(2)}) collective-permute-start(s32[512]{0:T(512)} %param.18), channel_id=1, source_target_pairs={{0,8},{8,0},{1,9},{9,1},{2,10},{10,2},{3,11},{11,3},{4,12},{12,4},... | collective-permute-start | bytes 6152 | tf_op jit(solution)/shard_map/ppermute | solution.py:153
  23.2 8.8 %collective-permute-start.4 = (bf16[48,320]{1,0:T(8,128)(2,1)S(1)}, bf16[48,320]{1,0:T(8,128)(2,1)S(1)}, u32[]{:S(2)}, u32[]{:S(2)}) collective-permute-start(bf16[48,320]{1,0:T(8,128)(2,1)S(1)} %pad_maximum_fusion.3), channel_id=1, source_target_pairs={{0,160},{32,192},{64,224},{96,0},{128,32},{160,64},{192,96},{224,1... | collective-permute-start | bytes 92168 | tf_op jit(solution)/shard_map/ppermute | solution.py:78
  27.1 5.0 %collective-permute-start.5 = (bf16[48,320]{1,0:T(8,128)(2,1)S(1)}, bf16[48,320]{1,0:T(8,128)(2,1)S(1)}, u32[]{:S(2)}, u32[]{:S(2)}) collective-permute-start(bf16[48,320]{1,0:T(8,128)(2,1)S(1)} %pad_maximum_fusion.3), channel_id=1, source_target_pairs={{0,192},{32,224},{64,0},{96,32},{128,64},{160,96},{192,128},{224,1... | collective-permute-start | bytes 92168 | tf_op jit(solution)/shard_map/ppermute | solution.py:78
  29.5 4.0 %collective-permute-start.6 = (bf16[48,320]{1,0:T(8,128)(2,1)S(1)}, bf16[48,320]{1,0:T(8,128)(2,1)S(1)}, u32[]{:S(2)}, u32[]{:S(2)}) collective-permute-start(bf16[48,320]{1,0:T(8,128)(2,1)S(1)} %pad_maximum_fusion.3), channel_id=1, source_target_pairs={{0,224},{32,0},{64,32},{96,64},{128,96},{160,128},{192,160},{224,1... | collective-permute-start | bytes 92168 | tf_op jit(solution)/shard_map/ppermute | solution.py:78
  31.8 5.7 %collective-permute-start.11 = (s32[512]{0:T(512)}, s32[512]{0:T(512)S(1)}, u32[]{:S(2)}, u32[]{:S(2)}) collective-permute-start(s32[512]{0:T(512)} %param.19), channel_id=1, source_target_pairs={{0,8},{8,0},{1,9},{9,1},{2,10},{10,2},{3,11},{11,3},{4,12},{12,4},... | collective-permute-start | bytes 6152 | tf_op jit(solution)/shard_map/ppermute | solution.py:153
  34.3 24.8 %collective-permute-start.7 = (bf16[8,48,320]{2,1,0:T(8,128)(2,1)S(1)}, bf16[8,48,320]{2,1,0:T(8,128)(2,1)S(1)}, u32[]{:S(2)}, u32[]{:S(2)}) collective-permute-start(bf16[8,48,320]{2,1,0:T(8,128)(2,1)S(1)} %broadcast_select_fusion), channel_id=1, source_target_pairs={{0,16},{16,0},{1,17},{17,1},{2,18},{18,2},{3,19},{19,3},{4,20},{20... | collective-permute-start | bytes 737288 | tf_op jit(solution)/shard_map/ppermute | solution.py:82
  59.3 2.1 %collective-permute-start.8 = (bf16[2,8,48,320]{3,2,1,0:T(8,128)(2,1)S(1)}, bf16[2,8,48,320]{3,2,1,0:T(8,128)(2,1)S(1)}, u32[]{:S(2)}, u32[]{:S(2)}) collective-permute-start(bf16[2,8,48,320]{3,2,1,0:T(8,128)(2,1)S(1)} %maximum_select_fusion.2), channel_id=1, source_target_pairs={{0,8},{8,0},{1,9},{9,1},{2,10},{10,2},{3,11},{11,3},{4,12},{12,4},... | collective-permute-start | bytes 1474568 | tf_op jit(solution)/shard_map/ppermute | solution.py:85
  67.1 4.6 %copy-start.2 = (bf16[520,1536]{0,1:T(8,128)(2,1)S(1)}, bf16[520,1536]{0,1:T(8,128)(2,1)}, u32[]{:S(2)}) copy-start(bf16[520,1536]{0,1:T(8,128)(2,1)} %all-gather.3.cloned.1.call-done) | copy-start | bytes 4792324
  71.5 1.6 collective-permute-start.9
  80.0 26.0 %copy-start.4 = (bf16[512,192]{0,1:T(8,128)(2,1)S(1)}, bf16[512,192]{0,1:T(8,128)(2,1)}, u32[]{:S(2)}) copy-start(bf16[512,192]{0,1:T(8,128)(2,1)} %param.17) | copy-start | bytes 589828
  80.0 26.8 %copy-start.1 = (s32[512]{0:T(512)S(1)}, s32[512]{0:T(512)}, u32[]{:S(2)}) copy-start(s32[512]{0:T(512)} %param.29) | copy-start | bytes 6148
  105.8 19.3 %copy-start.6 = (f32[512,8]{0,1:T(8,128)S(1)}, f32[512,8]{0,1:T(8,128)}, u32[]{:S(2)}) copy-start(f32[512,8]{0,1:T(8,128)} %param.26) | copy-start | bytes 49156
  105.8 19.3 %copy-start.7 = (s32[512,8]{0,1:T(8,128)S(1)}, s32[512,8]{0,1:T(8,128)}, u32[]{:S(2)}) copy-start(s32[512,8]{0,1:T(8,128)} %param.25) | copy-start | bytes 49156
  114.8 18.9 %all-to-all-start.1 = ((s32[32,1,16]{2,1,0:T(1,128)}), s32[32,1,16]{2,1,0:T(1,128)S(1)}, u32[]{:S(2)}, u32[]{:S(2)}) async-start(s32[32,1,16]{2,1,0:T(1,128)} %bitcast.32), calls=%async_computation.1 | async-start | bytes 32768 | tf_op jit(solution)/shard_map/all_to_all | solution.py:101
  133.7 15.5 %all-to-all-start.2 = ((bf16[32,16,1,128]{3,1,2,0:T(8,128)(2,1)}), bf16[32,16,1,128]{3,1,2,0:T(8,128)(2,1)S(1)}, u32[]{:S(2)}, u32[]{:S(2)}) async-start(bf16[32,16,1,128]{3,1,2,0:T(8,128)(2,1)} %bitcast.36), calls=%async_computation.2 | async-start | bytes 262144 | tf_op jit(solution)/shard_map/all_to_all | solution.py:100
  153.3 8.7 %copy-start.9 = (bf16[5,256,1536]{2,1,0:T(8,128)(2,1)S(1)}, bf16[5,256,1536]{2,1,0:T(8,128)(2,1)}, u32[]{:S(2)}) copy-start(bf16[5,256,1536]{2,1,0:T(8,128)(2,1)} %param.28) | copy-start | bytes 11796484
  167.2 25.1 %copy-start.3 = (bf16[512,192]{0,1:T(8,128)(2,1)S(1)}, bf16[512,192]{0,1:T(8,128)(2,1)}, u32[]{:S(2)}) copy-start(bf16[512,192]{0,1:T(8,128)(2,1)} %add_convert_fusion.1) | copy-start | bytes 589828
  167.2 24.9 %all-to-all-start.3 = ((bf16[8,512,192]{1,2,0:T(8,128)(2,1)}), bf16[8,512,192]{1,2,0:T(8,128)(2,1)S(1)}, u32[]{:S(2)}, u32[]{:S(2)}) async-start(bf16[8,512,192]{1,2,0:T(8,128)(2,1)} %bitcast.42), calls=%async_computation.3 | async-start | bytes 3145728 | tf_op jit(solution)/shard_map/all_to_all | solution.py:180
Sparse Core Ops, SparseCore 0:
  21.2 44.0 all-gather.2
  106.9 42.7 all-gather.4

commit v5 on v4

--- a/solution.py
+++ b/solution.py
@@ -89,21 +89,37 @@
 
 def place_cache_rows(own_rows, cache_slots, group_rank):
     tokens, keyvalue_heads, row_width = own_rows.shape
+    width = keyvalue_heads * row_width
     group_count = lax.axis_size(G)
     per_owner = tokens // group_count
+    sequence = jnp.arange(tokens, dtype=jnp.int32)
     owners = cache_slots // tokens
-    sequence = jnp.arange(tokens, dtype=jnp.int32)
-    ordering = jnp.argsort(owners * tokens + sequence)
-    send_rows = own_rows[ordering].reshape(group_count, per_owner, keyvalue_heads, row_width)
-    send_slots = cache_slots[ordering].reshape(group_count, per_owner)
-    got_rows, got_slots = (
-        lax.all_to_all(send_rows, G, split_axis=0, concat_axis=0, tiled=True),
-        lax.all_to_all(send_slots, G, split_axis=0, concat_axis=0, tiled=True),
-    )
-    targets = got_slots.reshape(tokens) - group_rank * tokens
-    return jnp.zeros_like(own_rows).at[targets].set(
-        got_rows.reshape(tokens, keyvalue_heads, row_width)
-    )
+    owner_hot = (owners[:, None] == jnp.arange(group_count, dtype=jnp.int32)[None, :]).astype(
+        jnp.bfloat16
+    )
+    earlier = (sequence[:, None] > sequence[None, :]).astype(jnp.bfloat16)
+    before = jnp.dot(earlier, owner_hot, preferred_element_type=jnp.float32)
+    rank = jnp.sum(before * owner_hot.astype(jnp.float32), axis=1).astype(jnp.int32)
+    place = owners * per_owner + rank
+    moving = (place[None, :] == sequence[:, None]).astype(jnp.bfloat16)
+    digits = jnp.stack([cache_slots // 128, cache_slots % 128], axis=1).astype(jnp.bfloat16)
+    payload = jnp.concatenate([own_rows.reshape(tokens, width), digits], axis=1)
+    sent = jnp.dot(moving, payload, preferred_element_type=jnp.float32).astype(jnp.bfloat16)
+    sent_rows = sent[:, :width].reshape(group_count, per_owner, width)
+    sent_digits = sent[:, width:].reshape(group_count, per_owner, 2).transpose(0, 2, 1)
+    digit_row = jnp.zeros((group_count, 1, width), jnp.bfloat16)
+    digit_row = lax.dynamic_update_slice(
+        digit_row, sent_digits.reshape(group_count, 1, 2 * per_owner), (0, 0, 0)
+    )
+    packet = jnp.concatenate([sent_rows, digit_row], axis=1)
+    got = lax.all_to_all(packet, G, 0, 0, tiled=True)
+    got_rows = got[:, :per_owner, :].reshape(tokens, width)
+    got_digits = got[:, per_owner, : 2 * per_owner].astype(jnp.int32).reshape(group_count, 2, per_owner)
+    got_slots = (got_digits[:, 0, :] * 128 + got_digits[:, 1, :]).reshape(tokens)
+    targets = got_slots - group_rank * tokens
+    landing = (targets[None, :] == sequence[:, None]).astype(jnp.bfloat16)
+    placed = jnp.dot(landing, got_rows, preferred_element_type=jnp.float32).astype(jnp.bfloat16)
+    return placed.reshape(tokens, keyvalue_heads, row_width)
 
 
 def shards(

time: 203 us -> 195 us (0.961); the launches traced: 200 us -> 194 us
  waiting for transfers between devices: 64.4 us -> 72.8 us
  local copies, waits for them, and re-layouts: 14.2 us -> 6.23 us
  starting transfers between devices: 40.5 us -> 35.6 us
  other arithmetic: 21.2 us -> 18.1 us
    all_gather x1, waiting for transfers between devices: 0.01 us -> 17.9 us  [shards(): residual = lax.all_gather(residual_share, T, axis=1, tiled=True)]
    gather x2 -> x0, local copies, waits for them, and re-layouts: 5.41 us -> none  [the longest x1 3.49 us: place_cache_rows(): send_slots = cache_slots[ordering].reshape(group_count, per_owner)]
    all_to_all x2 -> x1, waiting for transfers between devices: 16.8 us -> 11.6 us  [place_cache_rows(): got = lax.all_to_all(packet, G, 0, 0, tiled=True)]
    all_to_all x2 -> x1, starting transfers between devices: 15.2 us -> 10.3 us  [place_cache_rows(): got = lax.all_to_all(packet, G, 0, 0, tiled=True)]
    all_to_all x1, waiting for transfers between devices: 20.6 us -> 16.3 us  [shards(): term_got = lax.all_to_all(term_parts, T, 0, 0, tiled=True)]
    sort x1 -> x0, other arithmetic: 3.77 us -> none  [place_cache_rows(): ordering = jnp.argsort(owners * tokens + sequence)]
    scatter x1 -> x0, local copies, waits for them, and re-layouts: 2.36 us -> none  [place_cache_rows(): jnp.zeros_like(own_rows).at[targets]]
  transfers between devices with their start and end apart: 17 -> 16, of which waited for: 9 -> 9; matrix products, arithmetic and copies ran while one was open for 11% -> 7% of each run, Pallas kernels for 0% -> 0%
where the time goes in v5:
time: 195 us; the launch traced here: 194 us
  waiting for transfers between devices  72.8 us (37%)
  starting transfers between devices  35.6 us (18%)
  blocking collectives  25.7 us (13%)
  matrix products  20.9 us (11%)
  other arithmetic  18.1 us (9%)
  between operations  14.6 us (7%)
  local copies, waits for them, and re-layouts  6.23 us (3%)
    all_to_all x1, blocking collectives, shards(): value_got = lax.all_to_all(value_parts, T, 0, 0, tiled=True)  25.7 us
    ppermute x1, waiting for transfers between devices, gather_rows_over_groups(): other_y = lax.ppermute(zfull, 'yh', [(0, 1), (1, 0)])  20.7 us
    all_gather x1, waiting for transfers between devices, shards(): residual = lax.all_gather(residual_share, T, axis=1, tiled=True)  17.9 us
    ppermute x7, starting transfers between devices, gather_rows_over_groups(): got.append(lax.ppermute(block, 'z', [(i, (i + k) % nz) for i in range(nz)]))  17.7 us
    all_to_all x1, waiting for transfers between devices, shards(): term_got = lax.all_to_all(term_parts, T, 0, 0, tiled=True)  16.3 us
    all_to_all x1, waiting for transfers between devices, place_cache_rows(): got = lax.all_to_all(packet, G, 0, 0, tiled=True)  11.6 us
    all_to_all x1, starting transfers between devices, place_cache_rows(): got = lax.all_to_all(packet, G, 0, 0, tiled=True)  10.3 us
    dot_general x1, matrix products, expert_terms(): jnp.einsum('td,edf->etf', normed, gateup, preferred_element_type=jnp.floa...  8.72 us
  transfers between devices with their start and end apart: 16, of which 9 were waited for; matrix products, arithmetic and copies ran while one was open for 7% of the time, Pallas kernels for 0%

profile of v5, /device:TPU:32, one launch (start us, length us, event | category | flops | bytes accessed | tf_op | source)
XLA Modules:
  0.0 193.9 jit_solution(18098482847668023071)
XLA Ops:
  7.2 0.9 pad_maximum_fusion.3
  8.1 1.9 %collective-permute-start = (bf16[48,320]{1,0:T(8,128)(2,1)S(1)}, bf16[48,320]{1,0:T(8,128)(2,1)S(1)}, u32[]{:S(2)}, u32[]{:S(2)}) collective-permute-start(bf16[48,320]{1,0:T(8,128)(2,1)S(1)} %pad_maximum_fusion.3), channel_id=1, source_target_pairs={{0,32},{32,64},{64,96},{96,128},{128,160},{160,192},{192,224},{224... | collective-permute-start | bytes 92168 | tf_op jit(solution)/shard_map/ppermute | solution.py:78
  10.1 4.5 %collective-permute-start.1 = (bf16[48,320]{1,0:T(8,128)(2,1)S(1)}, bf16[48,320]{1,0:T(8,128)(2,1)S(1)}, u32[]{:S(2)}, u32[]{:S(2)}) collective-permute-start(bf16[48,320]{1,0:T(8,128)(2,1)S(1)} %pad_maximum_fusion.3), channel_id=1, source_target_pairs={{0,64},{32,96},{64,128},{96,160},{128,192},{160,224},{192,0},{224,... | collective-permute-start | bytes 92168 | tf_op jit(solution)/shard_map/ppermute | solution.py:78
  14.6 1.9 collective-permute-start.2
  16.5 1.4 collective-permute-start.3
  17.9 0.7 reshape.431
  18.6 0.7 reshape.432
  19.3 0.1 copy.69
  19.4 1.7 pad_maximum_fusion.1
  21.3 0.8 bitcast_dynamic-update-slice_fusion.7
  22.2 0.7 convert_element_type.105
  22.9 0.3 multiply_cosine_fusion
  23.2 3.2 %collective-permute-start.4 = (bf16[48,320]{1,0:T(8,128)(2,1)S(1)}, bf16[48,320]{1,0:T(8,128)(2,1)S(1)}, u32[]{:S(2)}, u32[]{:S(2)}) collective-permute-start(bf16[48,320]{1,0:T(8,128)(2,1)S(1)} %pad_maximum_fusion.3), channel_id=1, source_target_pairs={{0,160},{32,192},{64,224},{96,0},{128,32},{160,64},{192,96},{224,1... | collective-permute-start | bytes 92168 | tf_op jit(solution)/shard_map/ppermute | solution.py:78
  26.4 0.7 pad_add_fusion
  27.1 2.5 %collective-permute-start.5 = (bf16[48,320]{1,0:T(8,128)(2,1)S(1)}, bf16[48,320]{1,0:T(8,128)(2,1)S(1)}, u32[]{:S(2)}, u32[]{:S(2)}) collective-permute-start(bf16[48,320]{1,0:T(8,128)(2,1)S(1)} %pad_maximum_fusion.3), channel_id=1, source_target_pairs={{0,192},{32,224},{64,0},{96,32},{128,64},{160,96},{192,128},{224,1... | collective-permute-start | bytes 92168 | tf_op jit(solution)/shard_map/ppermute | solution.py:78
  29.6 2.3 %collective-permute-start.6 = (bf16[48,320]{1,0:T(8,128)(2,1)S(1)}, bf16[48,320]{1,0:T(8,128)(2,1)S(1)}, u32[]{:S(2)}, u32[]{:S(2)}) collective-permute-start(bf16[48,320]{1,0:T(8,128)(2,1)S(1)} %pad_maximum_fusion.3), channel_id=1, source_target_pairs={{0,224},{32,0},{64,32},{96,64},{128,96},{160,128},{192,160},{224,1... | collective-permute-start | bytes 92168 | tf_op jit(solution)/shard_map/ppermute | solution.py:78
  32.1 1.5 collective-permute-done.6
  33.6 0.6 gather_fusion
  34.2 0.1 broadcast_select_fusion
  34.3 3.3 %collective-permute-start.7 = (bf16[8,48,320]{2,1,0:T(8,128)(2,1)S(1)}, bf16[8,48,320]{2,1,0:T(8,128)(2,1)S(1)}, u32[]{:S(2)}, u32[]{:S(2)}) collective-permute-start(bf16[8,48,320]{2,1,0:T(8,128)(2,1)S(1)} %broadcast_select_fusion), channel_id=1, source_target_pairs={{0,16},{16,0},{1,17},{17,1},{2,18},{18,2},{3,19},{19,3},{4,20},{20... | collective-permute-start | bytes 737288 | tf_op jit(solution)/shard_map/ppermute | solution.py:82
  37.6 0.7 pad_add_fusion.1
  38.3 0.1 bitcast_select_fusion.1
  38.4 20.7 %collective-permute-done.7 = bf16[8,48,320]{2,1,0:T(8,128)(2,1)S(1)} collective-permute-done((bf16[8,48,320]{2,1,0:T(8,128)(2,1)S(1)}, bf16[8,48,320]{2,1,0:T(8,128)(2,1)S(1)}, u32[]{:S(2)}, u32[]{:S(2)}) %collective-permute-start.7) | collective-permute-done | bytes 245792 | tf_op jit(solution)/shard_map/ppermute | solution.py:82
  59.1 0.2 maximum_select_fusion.2
  59.4 0.8 compare_and_fusion
  60.3 0.1 fusion.68
  60.4 0.2 maximum_select_fusion.1
  60.6 0.8 collective-permute-done.8
  61.4 0.4 fusion.17
  61.8 0.1 copy.70
  61.9 3.4 %all-gather.3.cloned.1.call-done = bf16[520,1536]{0,1:T(8,128)(2,1)} async-done(((bf16[520,192]{0,1:T(8,128)(2,1)}), bf16[520,1536]{0,1:T(8,128)(2,1)}) %all-gather.3.cloned.1.call-update) | async-done | bytes 1597456 | tf_op jit(solution)/shard_map/all_gather | solution.py:147
  65.3 1.8 fusion.2
  67.2 1.7 convert_reduce_fusion.2
  68.8 2.3 %convolution_bitcast_fusion.1 = f32[512,1,128]{0,2,1:T(8,128)S(1)} fusion(bf16[1536,320]{1,0:T(8,128)(2,1)S(1)} %bitcast.99, f32[1536]{0:T(1024)S(1)} %get-tuple-element.38, f32[512]{0:T(512)S(1)} %add_rsqrt_fusion.1, bf16[520,1536]{0,1:T(8,128)(2,1)} %all-gather.3.cloned.1.call-done), kind=kOutput, calls=%fused_computation.33 | convolution fusion | flops 204472320 | bytes 2238464 | tf_op jit(solution)/shard_map/dot_general | solution.py:163
  71.1 0.3 fusion.46
  71.5 0.3 collective-permute-start.9
  71.8 0.8 fusion.23
  72.7 0.4 collective-permute-done.9
  73.1 1.4 fusion.1
  74.5 1.4 fusion
  75.9 2.0 %fusion.18 = bf16[64,3,512]{2,0,1:T(8,128)(2,1)S(1)} fusion(f32[3,512]{1,0:T(4,128)S(1)} %fusion, f32[3,512]{1,0:T(4,128)S(1)} %get-tuple-element.48, f32[1024,512,3]{1,0,2:T(8,128)S(1)} %get-tuple-element.49, pred[512,1024]{0,1:T(8,128)(4,1)S(1)} %compare_and_fusion, bf16[1024,1,128]{0,2,1:T(8,128)(2,1)S(1)} %pad_maximum_fusion), kind=kOutput, calls=%fused_computation.32 | convolution fusion | flops 209289216 | bytes 7159808 | tf_op jit(solution)/shard_map/grqk,kgd->qgrd/dot_general | solution.py:52
  77.9 0.6 convolution_convert_fusion
  78.6 1.6 copy.72
  80.2 25.7 %all_to_all.15 = bf16[8,512,192]{1,2,0:T(8,128)(2,1)S(1)} all-to-all(bf16[8,512,192]{1,2,0:T(8,128)(2,1)} %bitcast.98), channel_id=1, replica_groups=mesh['z'=8,'yh'=2,'c'=2,'yl'=2,'x'=4] {'yl','x'}, dimensions={0} | all-to-all | bytes 3145728 | tf_op jit(solution)/shard_map/all_to_all | solution.py:183
  105.8 0.2 convert_reduce_fusion.1
  106.1 0.7 add_convert_fusion.1
  106.9 0.3 fusion.22
  107.2 0.4 convolution_convert_fusion.1
  107.5 0.1 copy.73
  107.8 0.1 copy.75
  107.9 0.7 fusion.31
  108.7 10.3 %all-to-all-start.1 = ((bf16[32,17,128]{2,1,0:T(8,128)(2,1)}), bf16[32,17,128]{2,1,0:T(8,128)(2,1)S(1)}, u32[]{:S(2)}, u32[]{:S(2)}) async-start(bf16[32,17,128]{2,1,0:T(8,128)(2,1)} %fusion.31), calls=%async_computation.1 | async-start | bytes 393216 | tf_op jit(solution)/shard_map/all_to_all | solution.py:115
  119.1 11.6 %all-to-all-done.1 = bf16[32,17,128]{2,1,0:T(8,128)(2,1)S(1)} async-done(((bf16[32,17,128]{2,1,0:T(8,128)(2,1)}), bf16[32,17,128]{2,1,0:T(8,128)(2,1)S(1)}, u32[]{:S(2)}, u32[]{:S(2)}) %all-to-all-start.1) | async-done | bytes 139296 | tf_op jit(solution)/shard_map/all_to_all | solution.py:115
  131.0 1.0 fusion.21
  132.0 17.9 %all-gather.5.cloned.1.call-done = bf16[512,1536]{0,1:T(8,128)(2,1)} async-done(((bf16[512,192]{0,1:T(8,128)(2,1)}), bf16[512,1536]{0,1:T(8,128)(2,1)}) %all-gather.5.cloned.1.call-update) | async-done | bytes 1572880 | tf_op jit(solution)/shard_map/all_gather | solution.py:187
  149.8 1.8 fusion.5
  151.6 8.7 %convolution_bitcast_fusion = f32[5,512,512]{2,1,0:T(8,128)S(1)} fusion(bf16[5,1536,512]{2,1,0:T(8,128)(2,1)} %param.27, bf16[512,1536]{0,1:T(8,128)(2,1)} %all-gather.5.cloned.1.call-done, f32[1536]{0:T(1024)S(1)} %get-tuple-element.37, f32[512]{0:T(512)S(1)} %add_rsqrt_fusion), kind=kOutput, calls=%fused_computation.24 | convolution fusion | flops 4029677568 | bytes 14688256 | tf_op jit(solution)/shard_map/td,edf->etf/dot_general | solution.py:64
  160.4 3.5 %multiply_reduce_fusion = bf16[512,1536]{1,0:T(8,128)(2,1)S(1)} fusion(bf16[5,256,1536]{2,1,0:T(8,128)(2,1)S(1)} %copy-done.9, f32[5,512]{1,0:T(8,128)S(1)} %bitcast.114, f32[5,512,512]{2,1,0:T(8,128)S(1)} %convolution_bitcast_fusion), kind=kOutput, calls=%fused_computation.1 | convolution fusion | flops 2024275968 | bytes 10758144 | tf_op jit(solution)/shard_map/etf,efd->etd/dot_general | solution.py:68
  163.9 1.6 copy.80
  165.5 3.7 %all-to-all-start.2 = ((bf16[8,512,192]{1,2,0:T(8,128)(2,1)}), bf16[8,512,192]{1,2,0:T(8,128)(2,1)S(1)}, u32[]{:S(2)}, u32[]{:S(2)}) async-start(bf16[8,512,192]{1,2,0:T(8,128)(2,1)} %bitcast.42), calls=%async_computation.2 | async-start | bytes 3145728 | tf_op jit(solution)/shard_map/all_to_all | solution.py:196
  169.2 0.6 log_add_fusion
  169.8 16.3 %all-to-all-done.2 = bf16[8,512,192]{1,2,0:T(8,128)(2,1)S(1)} async-done(((bf16[8,512,192]{1,2,0:T(8,128)(2,1)}), bf16[8,512,192]{1,2,0:T(8,128)(2,1)S(1)}, u32[]{:S(2)}, u32[]{:S(2)}) %all-to-all-start.2) | async-done | bytes 1572896 | tf_op jit(solution)/shard_map/all_to_all | solution.py:196
  186.1 0.2 convert_reduce_fusion
  186.3 0.7 add_convert_fusion
  (71 shorter events, 1.4 us)
Async XLA Ops:
  7.2 70.8 %copy-start = (bf16[192,1536]{1,0:T(8,128)(2,1)S(1)}, bf16[192,1536]{1,0:T(8,128)(2,1)}, u32[]{:S(2)}) copy-start(bf16[192,1536]{1,0:T(8,128)(2,1)} %param.24) | copy-start | bytes 1769476
  7.2 52.2 %copy-start.7 = (s32[512]{0:T(512)S(1)}, s32[512]{0:T(512)}, u32[]{:S(2)}) copy-start(s32[512]{0:T(512)} %param.18) | copy-start | bytes 6148
  7.2 52.2 %copy-start.4 = (s32[512]{0:T(512)S(1)}, s32[512]{0:T(512)}, u32[]{:S(2)}) copy-start(s32[512]{0:T(512)} %param.19) | copy-start | bytes 6148
  7.2 58.1 %all-gather.3.cloned.1.call-start = ((), (), s32[]{:S(2)}) async-start(), calls=%async_computation.3 | async-start | bytes 2211840 | tf_op jit(solution)/shard_map/all_gather | solution.py:147
  8.1 19.0 %collective-permute-start = (bf16[48,320]{1,0:T(8,128)(2,1)S(1)}, bf16[48,320]{1,0:T(8,128)(2,1)S(1)}, u32[]{:S(2)}, u32[]{:S(2)}) collective-permute-start(bf16[48,320]{1,0:T(8,128)(2,1)S(1)} %pad_maximum_fusion.3), channel_id=1, source_target_pairs={{0,32},{32,64},{64,96},{96,128},{128,160},{160,192},{192,224},{224... | collective-permute-start | bytes 92168 | tf_op jit(solution)/shard_map/ppermute | solution.py:78
  10.1 19.5 %collective-permute-start.1 = (bf16[48,320]{1,0:T(8,128)(2,1)S(1)}, bf16[48,320]{1,0:T(8,128)(2,1)S(1)}, u32[]{:S(2)}, u32[]{:S(2)}) collective-permute-start(bf16[48,320]{1,0:T(8,128)(2,1)S(1)} %pad_maximum_fusion.3), channel_id=1, source_target_pairs={{0,64},{32,96},{64,128},{96,160},{128,192},{160,224},{192,0},{224,... | collective-permute-start | bytes 92168 | tf_op jit(solution)/shard_map/ppermute | solution.py:78
  14.6 17.3 %collective-permute-start.2 = (bf16[48,320]{1,0:T(8,128)(2,1)S(1)}, bf16[48,320]{1,0:T(8,128)(2,1)S(1)}, u32[]{:S(2)}, u32[]{:S(2)}) collective-permute-start(bf16[48,320]{1,0:T(8,128)(2,1)S(1)} %pad_maximum_fusion.3), channel_id=1, source_target_pairs={{0,96},{32,128},{64,160},{96,192},{128,224},{160,0},{192,32},{224,... | collective-permute-start | bytes 92168 | tf_op jit(solution)/shard_map/ppermute | solution.py:78
  16.5 15.5 %collective-permute-start.3 = (bf16[48,320]{1,0:T(8,128)(2,1)S(1)}, bf16[48,320]{1,0:T(8,128)(2,1)S(1)}, u32[]{:S(2)}, u32[]{:S(2)}) collective-permute-start(bf16[48,320]{1,0:T(8,128)(2,1)S(1)} %pad_maximum_fusion.3), channel_id=1, source_target_pairs={{0,128},{32,160},{64,192},{96,224},{128,0},{160,32},{192,64},{224,... | collective-permute-start | bytes 92168 | tf_op jit(solution)/shard_map/ppermute | solution.py:78
  21.1 128.7 %all-gather.5.cloned.1.call-start = ((), (), s32[]{:S(2)}) async-start(), calls=%async_computation.4 | async-start | bytes 1769472 | tf_op jit(solution)/shard_map/all_gather | solution.py:187
  21.2 2.0 %collective-permute-start.10 = (s32[512]{0:T(512)}, s32[512]{0:T(512)S(1)}, u32[]{:S(2)}, u32[]{:S(2)}) collective-permute-start(s32[512]{0:T(512)} %param.18), channel_id=1, source_target_pairs={{0,8},{8,0},{1,9},{9,1},{2,10},{10,2},{3,11},{11,3},{4,12},{12,4},... | collective-permute-start | bytes 6152 | tf_op jit(solution)/shard_map/ppermute | solution.py:169
  23.2 8.8 %collective-permute-start.4 = (bf16[48,320]{1,0:T(8,128)(2,1)S(1)}, bf16[48,320]{1,0:T(8,128)(2,1)S(1)}, u32[]{:S(2)}, u32[]{:S(2)}) collective-permute-start(bf16[48,320]{1,0:T(8,128)(2,1)S(1)} %pad_maximum_fusion.3), channel_id=1, source_target_pairs={{0,160},{32,192},{64,224},{96,0},{128,32},{160,64},{192,96},{224,1... | collective-permute-start | bytes 92168 | tf_op jit(solution)/shard_map/ppermute | solution.py:78
  27.1 5.0 %collective-permute-start.5 = (bf16[48,320]{1,0:T(8,128)(2,1)S(1)}, bf16[48,320]{1,0:T(8,128)(2,1)S(1)}, u32[]{:S(2)}, u32[]{:S(2)}) collective-permute-start(bf16[48,320]{1,0:T(8,128)(2,1)S(1)} %pad_maximum_fusion.3), channel_id=1, source_target_pairs={{0,192},{32,224},{64,0},{96,32},{128,64},{160,96},{192,128},{224,1... | collective-permute-start | bytes 92168 | tf_op jit(solution)/shard_map/ppermute | solution.py:78
  29.6 4.0 %collective-permute-start.6 = (bf16[48,320]{1,0:T(8,128)(2,1)S(1)}, bf16[48,320]{1,0:T(8,128)(2,1)S(1)}, u32[]{:S(2)}, u32[]{:S(2)}) collective-permute-start(bf16[48,320]{1,0:T(8,128)(2,1)S(1)} %pad_maximum_fusion.3), channel_id=1, source_target_pairs={{0,224},{32,0},{64,32},{96,64},{128,96},{160,128},{192,160},{224,1... | collective-permute-start | bytes 92168 | tf_op jit(solution)/shard_map/ppermute | solution.py:78
  31.9 5.7 %collective-permute-start.11 = (s32[512]{0:T(512)}, s32[512]{0:T(512)S(1)}, u32[]{:S(2)}, u32[]{:S(2)}) collective-permute-start(s32[512]{0:T(512)} %param.19), channel_id=1, source_target_pairs={{0,8},{8,0},{1,9},{9,1},{2,10},{10,2},{3,11},{11,3},{4,12},{12,4},... | collective-permute-start | bytes 6152 | tf_op jit(solution)/shard_map/ppermute | solution.py:169
  34.3 24.8 %collective-permute-start.7 = (bf16[8,48,320]{2,1,0:T(8,128)(2,1)S(1)}, bf16[8,48,320]{2,1,0:T(8,128)(2,1)S(1)}, u32[]{:S(2)}, u32[]{:S(2)}) collective-permute-start(bf16[8,48,320]{2,1,0:T(8,128)(2,1)S(1)} %broadcast_select_fusion), channel_id=1, source_target_pairs={{0,16},{16,0},{1,17},{17,1},{2,18},{18,2},{3,19},{19,3},{4,20},{20... | collective-permute-start | bytes 737288 | tf_op jit(solution)/shard_map/ppermute | solution.py:82
  59.3 2.1 %collective-permute-start.8 = (bf16[2,8,48,320]{3,2,1,0:T(8,128)(2,1)S(1)}, bf16[2,8,48,320]{3,2,1,0:T(8,128)(2,1)S(1)}, u32[]{:S(2)}, u32[]{:S(2)}) collective-permute-start(bf16[2,8,48,320]{3,2,1,0:T(8,128)(2,1)S(1)} %maximum_select_fusion.2), channel_id=1, source_target_pairs={{0,8},{8,0},{1,9},{9,1},{2,10},{10,2},{3,11},{11,3},{4,12},{12,4},... | collective-permute-start | bytes 1474568 | tf_op jit(solution)/shard_map/ppermute | solution.py:85
  67.1 4.6 %copy-start.1 = (bf16[520,1536]{0,1:T(8,128)(2,1)S(1)}, bf16[520,1536]{0,1:T(8,128)(2,1)}, u32[]{:S(2)}) copy-start(bf16[520,1536]{0,1:T(8,128)(2,1)} %all-gather.3.cloned.1.call-done) | copy-start | bytes 4792324
  71.5 1.6 collective-permute-start.9
  80.1 25.9 %copy-start.3 = (bf16[512,192]{0,1:T(8,128)(2,1)S(1)}, bf16[512,192]{0,1:T(8,128)(2,1)}, u32[]{:S(2)}) copy-start(bf16[512,192]{0,1:T(8,128)(2,1)} %param.17) | copy-start | bytes 589828
  80.1 26.7 %copy-start.8 = (s32[512]{0:T(512)S(1)}, s32[512]{0:T(512)}, u32[]{:S(2)}) copy-start(s32[512]{0:T(512)} %param.29) | copy-start | bytes 6148
  105.8 13.1 %copy-start.5 = (f32[512,8]{0,1:T(8,128)S(1)}, f32[512,8]{0,1:T(8,128)}, u32[]{:S(2)}) copy-start(f32[512,8]{0,1:T(8,128)} %param.26) | copy-start | bytes 49156
  105.8 13.2 %copy-start.6 = (s32[512,8]{0,1:T(8,128)S(1)}, s32[512,8]{0,1:T(8,128)}, u32[]{:S(2)}) copy-start(s32[512,8]{0,1:T(8,128)} %param.25) | copy-start | bytes 49156
  108.7 22.0 %all-to-all-start.1 = ((bf16[32,17,128]{2,1,0:T(8,128)(2,1)}), bf16[32,17,128]{2,1,0:T(8,128)(2,1)S(1)}, u32[]{:S(2)}, u32[]{:S(2)}) async-start(bf16[32,17,128]{2,1,0:T(8,128)(2,1)} %fusion.31), calls=%async_computation.1 | async-start | bytes 393216 | tf_op jit(solution)/shard_map/all_to_all | solution.py:115
  151.6 8.7 %copy-start.9 = (bf16[5,256,1536]{2,1,0:T(8,128)(2,1)S(1)}, bf16[5,256,1536]{2,1,0:T(8,128)(2,1)}, u32[]{:S(2)}) copy-start(bf16[5,256,1536]{2,1,0:T(8,128)(2,1)} %param.28) | copy-start | bytes 11796484
  165.5 20.9 %copy-start.2 = (bf16[512,192]{0,1:T(8,128)(2,1)S(1)}, bf16[512,192]{0,1:T(8,128)(2,1)}, u32[]{:S(2)}) copy-start(bf16[512,192]{0,1:T(8,128)(2,1)} %add_convert_fusion.1) | copy-start | bytes 589828
  165.5 20.6 %all-to-all-start.2 = ((bf16[8,512,192]{1,2,0:T(8,128)(2,1)}), bf16[8,512,192]{1,2,0:T(8,128)(2,1)S(1)}, u32[]{:S(2)}, u32[]{:S(2)}) async-start(bf16[8,512,192]{1,2,0:T(8,128)(2,1)} %bitcast.42), calls=%async_computation.2 | async-start | bytes 3145728 | tf_op jit(solution)/shard_map/all_to_all | solution.py:196
Sparse Core Ops, SparseCore 0:
  21.3 44.0 all-gather.2
  106.9 42.8 all-gather.4

commit v6 on v5

--- a/solution.py
+++ b/solution.py
@@ -71,21 +71,20 @@
 
 def gather_rows_over_groups(block):
     width = block.shape[1]
+    ci = lax.axis_index("c")
+    other_c = lax.ppermute(block, "c", [(0, 1), (1, 0)])
+    cfull = jnp.where(ci == 0, jnp.stack([block, other_c]), jnp.stack([other_c, block]))
+    yi = lax.axis_index("yh")
+    other_y = lax.ppermute(cfull, "yh", [(0, 1), (1, 0)])
+    yfull = jnp.where(yi == 0, jnp.stack([cfull, other_y]), jnp.stack([other_y, cfull]))
     nz = lax.axis_size("z")
     zi = lax.axis_index("z")
-    got = [block]
+    got = [yfull]
     for k in range(1, nz):
-        got.append(lax.ppermute(block, "z", [(i, (i + k) % nz) for i in range(nz)]))
+        got.append(lax.ppermute(yfull, "z", [(i, (i + k) % nz) for i in range(nz)]))
     stacked = jnp.stack(got)
     zfull = jnp.take(stacked, (zi - jnp.arange(nz)) % nz, axis=0)
-    yi = lax.axis_index("yh")
-    other_y = lax.ppermute(zfull, "yh", [(0, 1), (1, 0)])
-    yfull = jnp.where(yi == 0, jnp.stack([zfull, other_y]), jnp.stack([other_y, zfull]))
-    ci = lax.axis_index("c")
-    other_c = lax.ppermute(yfull, "c", [(0, 1), (1, 0)])
-    cfull = jnp.where(ci == 0, jnp.stack([yfull, other_c]), jnp.stack([other_c, yfull]))
-    return cfull.transpose(2, 1, 0, 3, 4).reshape(-1, width)
-
+    return zfull.reshape(-1, width)
 
 def place_cache_rows(own_rows, cache_slots, group_rank):
     tokens, keyvalue_heads, row_width = own_rows.shape

time: 195 us -> 188 us (0.964)
  waiting for transfers between devices: 72.8 us -> 67.8 us
    all_to_all x1, starting transfers between devices: 10.3 us -> 6.58 us  [place_cache_rows(): got = lax.all_to_all(packet, G, 0, 0, tiled=True)]
    all_gather x1, waiting for transfers between devices: 3.45 us -> 0.02 us  [shards(): packed_full = lax.all_gather(packed, T, axis=1, tiled=True)]
where the time goes in v6:
time: 188 us
  waiting for transfers between devices  67.8 us (36%)
  starting transfers between devices  34.1 us (18%)
  blocking collectives  27 us (14%)
  matrix products  19.5 us (10%)
  other arithmetic  18.1 us (10%)
  between operations  14.6 us (8%)
  local copies, waits for them, and re-layouts  6.55 us (3%)
    all_to_all x1, blocking collectives, shards(): value_got = lax.all_to_all(value_parts, T, 0, 0, tiled=True)  27 us
    ppermute x7, starting transfers between devices, gather_rows_over_groups(): got.append(lax.ppermute(yfull, 'z', [(i, (i + k) % nz) for i in range(nz)]))  19.3 us
    ppermute x7, waiting for transfers between devices, gather_rows_over_groups(): got.append(lax.ppermute(yfull, 'z', [(i, (i + k) % nz) for i in range(nz)]))  18.6 us
    all_gather x1, waiting for transfers between devices, shards(): residual = lax.all_gather(residual_share, T, axis=1, tiled=True)  17.9 us
    all_to_all x1, waiting for transfers between devices, shards(): term_got = lax.all_to_all(term_parts, T, 0, 0, tiled=True)  16.3 us
    all_to_all x1, waiting for transfers between devices, place_cache_rows(): got = lax.all_to_all(packet, G, 0, 0, tiled=True)  11.6 us
    dot_general x1, matrix products, expert_terms(): jnp.einsum('td,edf->etf', normed, gateup, preferred_element_type=jnp.floa...  8.71 us
    all_to_all x1, starting transfers between devices, place_cache_rows(): got = lax.all_to_all(packet, G, 0, 0, tiled=True)  6.58 us
  transfers between devices with their start and end apart: 16, of which 9 were waited for; matrix products, arithmetic and copies ran while one was open for 7% of the time, Pallas kernels for 0%

profile of v6, /device:TPU:32, one launch (start us, length us, event | category | flops | bytes accessed | tf_op | source)
XLA Modules:
  0.0 187.5 jit_solution(6620179228807870160)
XLA Ops:
  7.2 0.9 fusion.64
  8.1 0.1 collective-permute-start
  8.2 0.7 reshape.546
  8.9 0.7 reshape.547
  9.6 0.1 copy.65
  9.7 1.7 pad_maximum_fusion.1
  11.5 0.6 collective-permute-start.10
  12.1 0.1 collective-permute-start.11
  12.2 0.7 convert_element_type.105
  12.9 0.9 multiply_cosine_fusion
  13.9 0.1 broadcast_in_dim.31
  14.0 0.7 pad_add_fusion
  14.7 0.7 pad_add_fusion.1
  15.4 1.5 compare_and_fusion
  17.0 3.3 %collective-permute-start.1 = (bf16[2,48,320]{2,1,0:T(8,128)(2,1)S(1)}, bf16[2,48,320]{2,1,0:T(8,128)(2,1)S(1)}, u32[]{:S(2)}, u32[]{:S(2)}) collective-permute-start(bf16[2,48,320]{2,1,0:T(8,128)(2,1)S(1)} %maximum_select_fusion.3), channel_id=1, source_target_pairs={{0,16},{16,0},{1,17},{17,1},{2,18},{18,2},{3,19},{19,3},{4,20},{20... | collective-permute-start | bytes 184328 | tf_op jit(solution)/shard_map/ppermute | solution.py:78
  20.3 2.9 %collective-permute-done.1 = bf16[2,48,320]{2,1,0:T(8,128)(2,1)S(1)} collective-permute-done((bf16[2,48,320]{2,1,0:T(8,128)(2,1)S(1)}, bf16[2,48,320]{2,1,0:T(8,128)(2,1)S(1)}, u32[]{:S(2)}, u32[]{:S(2)}) %collective-permute-start.1) | collective-permute-done | bytes 61472 | tf_op jit(solution)/shard_map/ppermute | solution.py:78
  23.2 2.0 %collective-permute-start.2 = (bf16[2,2,48,320]{3,2,1,0:T(8,128)(2,1)S(1)}, bf16[2,2,48,320]{3,2,1,0:T(8,128)(2,1)S(1)}, u32[]{:S(2)}, u32[]{:S(2)}) collective-permute-start(bf16[2,2,48,320]{3,2,1,0:T(8,128)(2,1)S(1)} %maximum_select_fusion.1), channel_id=1, source_target_pairs={{0,32},{32,64},{64,96},{96,128},{128,160},{160,192},{192,224},{224... | collective-permute-start | bytes 368648 | tf_op jit(solution)/shard_map/ppermute | solution.py:84
  25.2 4.6 %collective-permute-start.3 = (bf16[2,2,48,320]{3,2,1,0:T(8,128)(2,1)S(1)}, bf16[2,2,48,320]{3,2,1,0:T(8,128)(2,1)S(1)}, u32[]{:S(2)}, u32[]{:S(2)}) collective-permute-start(bf16[2,2,48,320]{3,2,1,0:T(8,128)(2,1)S(1)} %maximum_select_fusion.1), channel_id=1, source_target_pairs={{0,64},{32,96},{64,128},{96,160},{128,192},{160,224},{192,0},{224,... | collective-permute-start | bytes 368648 | tf_op jit(solution)/shard_map/ppermute | solution.py:84
  29.8 1.9 %collective-permute-start.4 = (bf16[2,2,48,320]{3,2,1,0:T(8,128)(2,1)S(1)}, bf16[2,2,48,320]{3,2,1,0:T(8,128)(2,1)S(1)}, u32[]{:S(2)}, u32[]{:S(2)}) collective-permute-start(bf16[2,2,48,320]{3,2,1,0:T(8,128)(2,1)S(1)} %maximum_select_fusion.1), channel_id=1, source_target_pairs={{0,96},{32,128},{64,160},{96,192},{128,224},{160,0},{192,32},{224,... | collective-permute-start | bytes 368648 | tf_op jit(solution)/shard_map/ppermute | solution.py:84
  31.7 1.4 collective-permute-start.5
  33.2 3.0 %collective-permute-start.6 = (bf16[2,2,48,320]{3,2,1,0:T(8,128)(2,1)S(1)}, bf16[2,2,48,320]{3,2,1,0:T(8,128)(2,1)S(1)}, u32[]{:S(2)}, u32[]{:S(2)}) collective-permute-start(bf16[2,2,48,320]{3,2,1,0:T(8,128)(2,1)S(1)} %maximum_select_fusion.1), channel_id=1, source_target_pairs={{0,160},{32,192},{64,224},{96,0},{128,32},{160,64},{192,96},{224,1... | collective-permute-start | bytes 368648 | tf_op jit(solution)/shard_map/ppermute | solution.py:84
  36.3 2.5 %collective-permute-start.7 = (bf16[2,2,48,320]{3,2,1,0:T(8,128)(2,1)S(1)}, bf16[2,2,48,320]{3,2,1,0:T(8,128)(2,1)S(1)}, u32[]{:S(2)}, u32[]{:S(2)}) collective-permute-start(bf16[2,2,48,320]{3,2,1,0:T(8,128)(2,1)S(1)} %maximum_select_fusion.1), channel_id=1, source_target_pairs={{0,192},{32,224},{64,0},{96,32},{128,64},{160,96},{192,128},{224,1... | collective-permute-start | bytes 368648 | tf_op jit(solution)/shard_map/ppermute | solution.py:84
  38.8 1.2 collective-permute-done.3
  40.1 3.8 %collective-permute-start.8 = (bf16[2,2,48,320]{3,2,1,0:T(8,128)(2,1)S(1)}, bf16[2,2,48,320]{3,2,1,0:T(8,128)(2,1)S(1)}, u32[]{:S(2)}, u32[]{:S(2)}) collective-permute-start(bf16[2,2,48,320]{3,2,1,0:T(8,128)(2,1)S(1)} %maximum_select_fusion.1), channel_id=1, source_target_pairs={{0,224},{32,0},{64,32},{96,64},{128,96},{160,128},{192,160},{224,1... | collective-permute-start | bytes 368648 | tf_op jit(solution)/shard_map/ppermute | solution.py:84
  43.9 9.9 %collective-permute-done.4 = bf16[2,2,48,320]{3,2,1,0:T(8,128)(2,1)S(1)} collective-permute-done((bf16[2,2,48,320]{3,2,1,0:T(8,128)(2,1)S(1)}, bf16[2,2,48,320]{3,2,1,0:T(8,128)(2,1)S(1)}, u32[]{:S(2)}, u32[]{:S(2)}) %collective-permute-start.4) | collective-permute-done | bytes 122912 | tf_op jit(solution)/shard_map/ppermute | solution.py:84
  54.0 6.0 %collective-permute-done.7 = bf16[2,2,48,320]{3,2,1,0:T(8,128)(2,1)S(1)} collective-permute-done((bf16[2,2,48,320]{3,2,1,0:T(8,128)(2,1)S(1)}, bf16[2,2,48,320]{3,2,1,0:T(8,128)(2,1)S(1)}, u32[]{:S(2)}, u32[]{:S(2)}) %collective-permute-start.7) | collective-permute-done | bytes 122912 | tf_op jit(solution)/shard_map/ppermute | solution.py:84
  60.0 1.5 collective-permute-done.8
  61.5 0.8 gather_fusion
  62.3 0.3 bitcast_select_fusion.1
  62.7 1.9 %fusion.2 = f32[512]{0:T(512)S(1)} fusion(bf16[520,1536]{0,1:T(8,128)(2,1)} %all-gather.3.cloned.1.call-done), kind=kLoop, calls=%fused_computation.11 | loop fusion | flops 2358784 | bytes 1574912 | tf_op jit(solution)/shard_map/reduce_sum | solution.py:19
  64.6 1.5 convert_reduce_fusion.2
  66.2 0.9 convolution_bitcast_fusion.1
  67.1 0.3 fusion.46
  67.5 0.3 collective-permute-start.9
  67.7 0.8 fusion.22
  68.7 0.4 collective-permute-done.9
  69.1 1.4 fusion.1
  70.5 1.4 fusion
  71.9 2.0 %fusion.17 = bf16[64,3,512]{2,0,1:T(8,128)(2,1)S(1)} fusion(f32[3,512]{1,0:T(4,128)S(1)} %fusion, f32[3,512]{1,0:T(4,128)S(1)} %get-tuple-element.51, f32[1024,512,3]{1,0,2:T(8,128)S(1)} %get-tuple-element.52, pred[512,1024]{0,1:T(8,128)(4,1)S(1)} %compare_and_fusion, bf16[1024,1,128]{0,2,1:T(8,128)(2,1)S(1)} %pad_maximum_fusion), kind=kOutput, calls=%fused_computation.31 | convolution fusion | flops 209289216 | bytes 7159808 | tf_op jit(solution)/shard_map/grqk,kgd->qgrd/dot_general | solution.py:52
  73.9 0.6 convolution_convert_fusion
  74.5 1.6 copy.67
  76.1 27.0 %all_to_all.15 = bf16[8,512,192]{1,2,0:T(8,128)(2,1)S(1)} all-to-all(bf16[8,512,192]{1,2,0:T(8,128)(2,1)} %bitcast.96), channel_id=1, replica_groups=mesh['z'=8,'yh'=2,'c'=2,'yl'=2,'x'=4] {'yl','x'}, dimensions={0} | all-to-all | bytes 3145728 | tf_op jit(solution)/shard_map/all_to_all | solution.py:182
  103.1 0.2 convert_reduce_fusion.1
  103.4 0.7 add_convert_fusion.1
  104.2 0.3 fusion.21
  104.5 0.4 convolution_convert_fusion.1
  104.9 0.1 copy.68
  105.0 0.1 reshape.558
  105.2 0.1 copy.70
  105.3 0.7 fusion.30
  106.0 6.6 %all-to-all-start.1 = ((bf16[32,17,128]{2,1,0:T(8,128)(2,1)}), bf16[32,17,128]{2,1,0:T(8,128)(2,1)S(1)}, u32[]{:S(2)}, u32[]{:S(2)}) async-start(bf16[32,17,128]{2,1,0:T(8,128)(2,1)} %fusion.30), calls=%async_computation.1 | async-start | bytes 393216 | tf_op jit(solution)/shard_map/all_to_all | solution.py:114
  112.6 0.1 select_reduce_fusion
  112.7 11.6 %all-to-all-done.1 = bf16[32,17,128]{2,1,0:T(8,128)(2,1)S(1)} async-done(((bf16[32,17,128]{2,1,0:T(8,128)(2,1)}), bf16[32,17,128]{2,1,0:T(8,128)(2,1)S(1)}, u32[]{:S(2)}, u32[]{:S(2)}) %all-to-all-start.1) | async-done | bytes 139296 | tf_op jit(solution)/shard_map/all_to_all | solution.py:114
  124.6 1.0 fusion.20
  125.6 17.9 %all-gather.5.cloned.1.call-done = bf16[512,1536]{0,1:T(8,128)(2,1)} async-done(((bf16[512,192]{0,1:T(8,128)(2,1)}), bf16[512,1536]{0,1:T(8,128)(2,1)}) %all-gather.5.cloned.1.call-update) | async-done | bytes 1572880 | tf_op jit(solution)/shard_map/all_gather | solution.py:186
  143.5 1.8 fusion.5
  145.3 8.7 %convolution_bitcast_fusion = f32[5,512,512]{2,1,0:T(8,128)S(1)} fusion(bf16[5,1536,512]{2,1,0:T(8,128)(2,1)} %param.27, bf16[512,1536]{0,1:T(8,128)(2,1)} %all-gather.5.cloned.1.call-done, f32[1536]{0:T(1024)S(1)} %get-tuple-element.37, f32[512]{0:T(512)S(1)} %add_rsqrt_fusion), kind=kOutput, calls=%fused_computation.24 | convolution fusion | flops 4029677568 | bytes 14688256 | tf_op jit(solution)/shard_map/td,edf->etf/dot_general | solution.py:64
  154.0 3.5 %multiply_reduce_fusion = bf16[512,1536]{1,0:T(8,128)(2,1)S(1)} fusion(bf16[5,256,1536]{2,1,0:T(8,128)(2,1)S(1)} %copy-done.8, f32[5,512]{1,0:T(8,128)S(1)} %bitcast.110, f32[5,512,512]{2,1,0:T(8,128)S(1)} %convolution_bitcast_fusion), kind=kOutput, calls=%fused_computation.1 | convolution fusion | flops 2024275968 | bytes 10758144 | tf_op jit(solution)/shard_map/etf,efd->etd/dot_general | solution.py:68
  157.5 1.6 copy.75
  159.1 3.7 %all-to-all-start.2 = ((bf16[8,512,192]{1,2,0:T(8,128)(2,1)}), bf16[8,512,192]{1,2,0:T(8,128)(2,1)S(1)}, u32[]{:S(2)}, u32[]{:S(2)}) async-start(bf16[8,512,192]{1,2,0:T(8,128)(2,1)} %bitcast.42), calls=%async_computation.2 | async-start | bytes 3145728 | tf_op jit(solution)/shard_map/all_to_all | solution.py:195
  162.8 0.6 log_add_fusion
  163.4 16.3 %all-to-all-done.2 = bf16[8,512,192]{1,2,0:T(8,128)(2,1)S(1)} async-done(((bf16[8,512,192]{1,2,0:T(8,128)(2,1)}), bf16[8,512,192]{1,2,0:T(8,128)(2,1)S(1)}, u32[]{:S(2)}, u32[]{:S(2)}) %all-to-all-start.2) | async-done | bytes 1572896 | tf_op jit(solution)/shard_map/all_to_all | solution.py:195
  179.7 0.2 convert_reduce_fusion
  180.0 0.7 add_convert_fusion
  (69 shorter events, 1.2 us)
Async XLA Ops:
  7.2 66.7 %copy-start = (bf16[192,1536]{1,0:T(8,128)(2,1)S(1)}, bf16[192,1536]{1,0:T(8,128)(2,1)}, u32[]{:S(2)}) copy-start(bf16[192,1536]{1,0:T(8,128)(2,1)} %param.24) | copy-start | bytes 1769476
  7.2 55.5 %all-gather.3.cloned.1.call-start = ((), (), s32[]{:S(2)}) async-start(), calls=%async_computation.3 | async-start | bytes 2211840 | tf_op jit(solution)/shard_map/all_gather | solution.py:146
  8.1 8.8 %collective-permute-start = (bf16[48,320]{1,0:T(8,128)(2,1)S(1)}, bf16[48,320]{1,0:T(8,128)(2,1)S(1)}, u32[]{:S(2)}, u32[]{:S(2)}) collective-permute-start(bf16[48,320]{1,0:T(8,128)(2,1)S(1)} %get-tuple-element.45), channel_id=1, source_target_pairs={{0,8},{8,0},{1,9},{9,1},{2,10},{10,2},{3,11},{11,3},{4,12},{12,4},... | collective-permute-start | bytes 92168 | tf_op jit(solution)/shard_map/ppermute | solution.py:75
  11.4 132.0 %all-gather.5.cloned.1.call-start = ((), (), s32[]{:S(2)}) async-start(), calls=%async_computation.4 | async-start | bytes 1769472 | tf_op jit(solution)/shard_map/all_gather | solution.py:186
  11.5 2.5 %collective-permute-start.10 = (s32[512]{0:T(512)}, s32[512]{0:T(512)S(1)}, u32[]{:S(2)}, u32[]{:S(2)}) collective-permute-start(s32[512]{0:T(512)} %param.18), channel_id=1, source_target_pairs={{0,8},{8,0},{1,9},{9,1},{2,10},{10,2},{3,11},{11,3},{4,12},{12,4},... | collective-permute-start | bytes 6152 | tf_op jit(solution)/shard_map/ppermute | solution.py:168
  12.1 2.7 %collective-permute-start.11 = (s32[512]{0:T(512)}, s32[512]{0:T(512)S(1)}, u32[]{:S(2)}, u32[]{:S(2)}) collective-permute-start(s32[512]{0:T(512)} %param.19), channel_id=1, source_target_pairs={{0,8},{8,0},{1,9},{9,1},{2,10},{10,2},{3,11},{11,3},{4,12},{12,4},... | collective-permute-start | bytes 6152 | tf_op jit(solution)/shard_map/ppermute | solution.py:168
  17.0 6.2 %collective-permute-start.1 = (bf16[2,48,320]{2,1,0:T(8,128)(2,1)S(1)}, bf16[2,48,320]{2,1,0:T(8,128)(2,1)S(1)}, u32[]{:S(2)}, u32[]{:S(2)}) collective-permute-start(bf16[2,48,320]{2,1,0:T(8,128)(2,1)S(1)} %maximum_select_fusion.3), channel_id=1, source_target_pairs={{0,16},{16,0},{1,17},{17,1},{2,18},{18,2},{3,19},{19,3},{4,20},{20... | collective-permute-start | bytes 184328 | tf_op jit(solution)/shard_map/ppermute | solution.py:78
  23.2 13.0 %collective-permute-start.2 = (bf16[2,2,48,320]{3,2,1,0:T(8,128)(2,1)S(1)}, bf16[2,2,48,320]{3,2,1,0:T(8,128)(2,1)S(1)}, u32[]{:S(2)}, u32[]{:S(2)}) collective-permute-start(bf16[2,2,48,320]{3,2,1,0:T(8,128)(2,1)S(1)} %maximum_select_fusion.1), channel_id=1, source_target_pairs={{0,32},{32,64},{64,96},{96,128},{128,160},{160,192},{192,224},{224... | collective-permute-start | bytes 368648 | tf_op jit(solution)/shard_map/ppermute | solution.py:84
  25.2 14.8 %collective-permute-start.3 = (bf16[2,2,48,320]{3,2,1,0:T(8,128)(2,1)S(1)}, bf16[2,2,48,320]{3,2,1,0:T(8,128)(2,1)S(1)}, u32[]{:S(2)}, u32[]{:S(2)}) collective-permute-start(bf16[2,2,48,320]{3,2,1,0:T(8,128)(2,1)S(1)} %maximum_select_fusion.1), channel_id=1, source_target_pairs={{0,64},{32,96},{64,128},{96,160},{128,192},{160,224},{192,0},{224,... | collective-permute-start | bytes 368648 | tf_op jit(solution)/shard_map/ppermute | solution.py:84
  29.8 24.0 %collective-permute-start.4 = (bf16[2,2,48,320]{3,2,1,0:T(8,128)(2,1)S(1)}, bf16[2,2,48,320]{3,2,1,0:T(8,128)(2,1)S(1)}, u32[]{:S(2)}, u32[]{:S(2)}) collective-permute-start(bf16[2,2,48,320]{3,2,1,0:T(8,128)(2,1)S(1)} %maximum_select_fusion.1), channel_id=1, source_target_pairs={{0,96},{32,128},{64,160},{96,192},{128,224},{160,0},{192,32},{224,... | collective-permute-start | bytes 368648 | tf_op jit(solution)/shard_map/ppermute | solution.py:84
  31.7 22.2 %collective-permute-start.5 = (bf16[2,2,48,320]{3,2,1,0:T(8,128)(2,1)S(1)}, bf16[2,2,48,320]{3,2,1,0:T(8,128)(2,1)S(1)}, u32[]{:S(2)}, u32[]{:S(2)}) collective-permute-start(bf16[2,2,48,320]{3,2,1,0:T(8,128)(2,1)S(1)} %maximum_select_fusion.1), channel_id=1, source_target_pairs={{0,128},{32,160},{64,192},{96,224},{128,0},{160,32},{192,64},{224,... | collective-permute-start | bytes 368648 | tf_op jit(solution)/shard_map/ppermute | solution.py:84
  33.2 20.8 %collective-permute-start.6 = (bf16[2,2,48,320]{3,2,1,0:T(8,128)(2,1)S(1)}, bf16[2,2,48,320]{3,2,1,0:T(8,128)(2,1)S(1)}, u32[]{:S(2)}, u32[]{:S(2)}) collective-permute-start(bf16[2,2,48,320]{3,2,1,0:T(8,128)(2,1)S(1)} %maximum_select_fusion.1), channel_id=1, source_target_pairs={{0,160},{32,192},{64,224},{96,0},{128,32},{160,64},{192,96},{224,1... | collective-permute-start | bytes 368648 | tf_op jit(solution)/shard_map/ppermute | solution.py:84
  36.3 23.7 %collective-permute-start.7 = (bf16[2,2,48,320]{3,2,1,0:T(8,128)(2,1)S(1)}, bf16[2,2,48,320]{3,2,1,0:T(8,128)(2,1)S(1)}, u32[]{:S(2)}, u32[]{:S(2)}) collective-permute-start(bf16[2,2,48,320]{3,2,1,0:T(8,128)(2,1)S(1)} %maximum_select_fusion.1), channel_id=1, source_target_pairs={{0,192},{32,224},{64,0},{96,32},{128,64},{160,96},{192,128},{224,1... | collective-permute-start | bytes 368648 | tf_op jit(solution)/shard_map/ppermute | solution.py:84
  40.1 21.4 %collective-permute-start.8 = (bf16[2,2,48,320]{3,2,1,0:T(8,128)(2,1)S(1)}, bf16[2,2,48,320]{3,2,1,0:T(8,128)(2,1)S(1)}, u32[]{:S(2)}, u32[]{:S(2)}) collective-permute-start(bf16[2,2,48,320]{3,2,1,0:T(8,128)(2,1)S(1)} %maximum_select_fusion.1), channel_id=1, source_target_pairs={{0,224},{32,0},{64,32},{96,64},{128,96},{160,128},{192,160},{224,1... | collective-permute-start | bytes 368648 | tf_op jit(solution)/shard_map/ppermute | solution.py:84
  62.7 3.5 %copy-start.1 = (bf16[520,1536]{0,1:T(8,128)(2,1)S(1)}, bf16[520,1536]{0,1:T(8,128)(2,1)}, u32[]{:S(2)}) copy-start(bf16[520,1536]{0,1:T(8,128)(2,1)} %all-gather.3.cloned.1.call-done) | copy-start | bytes 4792324
  67.4 1.1 copy-start.4
  67.5 1.6 collective-permute-start.9
  76.1 27.2 %copy-start.3 = (bf16[512,192]{0,1:T(8,128)(2,1)S(1)}, bf16[512,192]{0,1:T(8,128)(2,1)}, u32[]{:S(2)}) copy-start(bf16[512,192]{0,1:T(8,128)(2,1)} %param.17) | copy-start | bytes 589828
  103.1 1.0 copy-start.7
  103.4 9.2 %copy-start.5 = (f32[512,8]{0,1:T(8,128)S(1)}, f32[512,8]{0,1:T(8,128)}, u32[]{:S(2)}) copy-start(f32[512,8]{0,1:T(8,128)} %param.26) | copy-start | bytes 49156
  103.4 9.2 %copy-start.6 = (s32[512,8]{0,1:T(8,128)S(1)}, s32[512,8]{0,1:T(8,128)}, u32[]{:S(2)}) copy-start(s32[512,8]{0,1:T(8,128)} %param.25) | copy-start | bytes 49156
  106.0 18.4 %all-to-all-start.1 = ((bf16[32,17,128]{2,1,0:T(8,128)(2,1)}), bf16[32,17,128]{2,1,0:T(8,128)(2,1)S(1)}, u32[]{:S(2)}, u32[]{:S(2)}) async-start(bf16[32,17,128]{2,1,0:T(8,128)(2,1)} %fusion.30), calls=%async_computation.1 | async-start | bytes 393216 | tf_op jit(solution)/shard_map/all_to_all | solution.py:114
  145.3 8.7 %copy-start.8 = (bf16[5,256,1536]{2,1,0:T(8,128)(2,1)S(1)}, bf16[5,256,1536]{2,1,0:T(8,128)(2,1)}, u32[]{:S(2)}) copy-start(bf16[5,256,1536]{2,1,0:T(8,128)(2,1)} %param.28) | copy-start | bytes 11796484
  159.1 20.9 %copy-start.2 = (bf16[512,192]{0,1:T(8,128)(2,1)S(1)}, bf16[512,192]{0,1:T(8,128)(2,1)}, u32[]{:S(2)}) copy-start(bf16[512,192]{0,1:T(8,128)(2,1)} %add_convert_fusion.1) | copy-start | bytes 589828
  159.1 20.6 %all-to-all-start.2 = ((bf16[8,512,192]{1,2,0:T(8,128)(2,1)}), bf16[8,512,192]{1,2,0:T(8,128)(2,1)S(1)}, u32[]{:S(2)}, u32[]{:S(2)}) async-start(bf16[8,512,192]{1,2,0:T(8,128)(2,1)} %bitcast.42), calls=%async_computation.2 | async-start | bytes 3145728 | tf_op jit(solution)/shard_map/all_to_all | solution.py:195
Sparse Core Ops, SparseCore 0:
  11.5 46.6 all-gather.2
  104.2 39.1 all-gather.4
